TPU v7x, 512 devices: a whole 4x4x16 slice. The times are simulated.
512 devices in a mesh: row: 16 (over z), col: 4 (over x_hi, core), depth: 8 (over y, x_lo).
Axes of the slice: x: 4 (x_hi: 2, x_lo: 2; x = x_hi * 2 + x_lo), y: 4, z: 16, core: 2. Of those that a mesh axis runs over, the one named last changes fastest.
Arguments:
- ks_matrix: bfloat16 [4096, 16384], P('col', ('row', 'depth')), may hold values from -6 to 6
- sign_matrix: bfloat16 [16, 8, 128, 12288], P('col', 'depth', None, 'row'), may hold values from -0.046875 to 0.046875
- ks_mask: int32 [32, 128], P('col', ('row', 'depth')), may hold values 0 or 1
- sign_mask: int32 [16, 8, 1, 96], P('col', 'depth', None, 'row'), may hold values 0 or 1
- product_mask: int32 [32, 96], P('col', 'row'), may hold values 0 or 1
- row_order: int32 [4, 8], P('col'), may hold values from 0 to 7, each once within a row
Outputs:
- next_matrix: bfloat16 [4096, 12288], P(('col', 'depth'), 'row')
Inputs may be any that keep to these rules, and one draw needn't show every extreme that they name: Each row of row_order names every number of 0 to 7 once.
All inputs are finite; a program needn't handle non-finite values. No bound on the sum of `ks_mask` or of `sign_mask` or of `product_mask` on one device may be relied on, other than what follows from the above.
Results may differ from a plain program's by a relative error of at most 0.001.
Values may be sent and summed in bfloat16 or wider, within the bound.
No kernel may reach another device: no remote copies, remote signals or barrier semaphores. Data moves between devices by JAX's collectives and lax.ppermute only.
A program may use at most 64 MiB of HBM per device.

v0:
```python
import jax
import jax.numpy as jnp
from jax import lax
from jax.sharding import PartitionSpec as P

BS = 128


def from_behind(block, axis, distance):
    devices = range(lax.axis_size(axis))
    route = [((i - distance) % len(devices), i) for i in devices]
    return lax.ppermute(block, axis, route)


def per_device(ks_matrix, sign_matrix, ks_mask, sign_mask, product_mask, row_order):
    row_blocks, inner_blocks = ks_mask.shape
    local_groups = sign_mask.shape[0]
    sign_inner = sign_mask.shape[2]
    col_blocks = sign_mask.shape[3]
    ks_panel = (
        ks_matrix.reshape(row_blocks, BS, inner_blocks, BS)
        * ks_mask.astype(jnp.bfloat16)[:, None, :, None]
    )
    ks_panel = ks_panel.reshape(row_blocks * BS, inner_blocks * BS)
    sign_kept = sign_matrix.reshape(local_groups, sign_inner, BS, col_blocks, BS)
    sign_kept = sign_kept * sign_mask.astype(jnp.bfloat16).reshape(
        local_groups, sign_inner, 1, col_blocks, 1
    )
    sign_kept = sign_kept.reshape(local_groups, 1, sign_inner * BS, col_blocks * BS)
    sign_whole = lax.all_gather(sign_kept, "col", axis=0, tiled=True)
    row_count = lax.axis_size("row")
    start_sum = jnp.zeros((row_blocks * BS, col_blocks * BS), jnp.float32)
    row_index = lax.axis_index("row")

    def advance(step, carry):
        running, moving = carry
        source = (row_index - step) % row_count
        sign_piece = lax.dynamic_index_in_dim(sign_whole, source, 0, keepdims=False)[0]
        running = running + jnp.dot(moving, sign_piece, preferred_element_type=jnp.float32)
        moving = from_behind(moving, "row", 1)
        return (running, moving)

    running, moving = lax.fori_loop(0, row_count - 1, advance, (start_sum, ks_panel))
    final_source = (row_index - row_count + 1) % row_count
    final_piece = lax.dynamic_index_in_dim(sign_whole, final_source, 0, keepdims=False)[0]
    running = running + jnp.dot(moving, final_piece, preferred_element_type=jnp.float32)
    depth_count = lax.axis_size("depth")
    part_rows = row_blocks // depth_count
    filtered = (
        running.reshape(row_blocks, BS, col_blocks, BS)
        * product_mask.astype(jnp.float32)[:, None, :, None]
    )
    local_order = row_order[0]
    summed = lax.psum(filtered, "depth")
    own_rows = lax.dynamic_slice_in_dim(
        local_order, lax.axis_index("depth") * part_rows, part_rows, 0
    )
    picked = jnp.take(summed, own_rows, axis=0)
    return picked.reshape(part_rows * BS, col_blocks * BS).astype(jnp.bfloat16)


def solution(mesh):
    in_specs = (
        P("col", ("row", "depth")),
        P("col", "depth", None, "row"),
        P("col", ("row", "depth")),
        P("col", "depth", None, "row"),
        P("col", "row"),
        P("col", None),
    )
    out_specs = P(("col", "depth"), "row")
    return jax.shard_map(
        per_device, mesh=mesh, in_specs=in_specs, out_specs=out_specs, check_vma=False
    )
```

profile of v0, /device:TPU:4, one launch (start us, length us, event | category | flops | bytes accessed | tf_op | source)
XLA Modules:
  0.0 356.8 jit_solution(18374426383536028386)
XLA Ops:
  7.3 2.1 broadcast_multiply_fusion.1
  15.4 36.3 %all-gather.2.cloned.1.call-done = bf16[16,1,128,768]{3,2,1,0:T(8,128)(2,1)} async-done(((bf16[4,1,128,768]{3,2,1,0:T(8,128)(2,1)}), bf16[16,1,128,768]{3,2,1,0:T(8,128)(2,1)}) %all-gather.2.cloned.1.call-update) | async-done | bytes 3145744 | tf_op jit(solution)/shard_map/all_gather | solution.py:30
  51.6 171.1 %while.19 = (s32[]{:T(128)}, f32[1024,768]{0,1:T(8,128)S(1)}, bf16[1024,128]{1,0:T(8,128)(2,1)}, s32[]{:T(128)}, bf16[16,1,128,768]{3,2,1,0:T(8,128)(2,1)}, /*index=5*/s32[]{:T(128)}, s32[]{:T(128)}, s32[]{:T(128)}, s32[]{:T(128)}) while((s32[]{:T(128)}, f32[1024,768]{0,1:T(8,128)S(1)}, bf16[1024,128]{1,0:T(8,128)(2,1)}, ...), condition=%wide.region_1.2_spmd.clone, body=%wide.region_0.1_spmd.clone.sunk | while | flops 202899472 | bytes 8323374 | solution.py:43
  52.6 3.7 %collective-permute-start = (bf16[1024,128]{1,0:T(8,128)(2,1)S(1)}, bf16[1024,128]{1,0:T(8,128)(2,1)}, u32[]{:S(2)}, u32[]{:S(2)}) collective-permute-start(bf16[1024,128]{1,0:T(8,128)(2,1)S(1)} %copy.29), channel_id=1, source_target_pairs={{480,0},{0,32},{32,64},{64,96},{96,128},{128,160},{160,192},{192,2... | collective-permute-start | bytes 786440 | tf_op jit(solution)/shard_map/while/body/eval_jaxpr/ppermute | solution.py:12
  58.2 7.4 %collective-permute-done = bf16[1024,128]{1,0:T(8,128)(2,1)} collective-permute-done((bf16[1024,128]{1,0:T(8,128)(2,1)S(1)}, bf16[1024,128]{1,0:T(8,128)(2,1)}, u32[]{:S(2)}, u32[]{:S(2)}) %collective-permute-start) | collective-permute-done | bytes 262176 | tf_op jit(solution)/shard_map/while/body/eval_jaxpr/ppermute | solution.py:12
  70.3 7.3 %collective-permute-done = bf16[1024,128]{1,0:T(8,128)(2,1)} collective-permute-done((bf16[1024,128]{1,0:T(8,128)(2,1)S(1)}, bf16[1024,128]{1,0:T(8,128)(2,1)}, u32[]{:S(2)}, u32[]{:S(2)}) %collective-permute-start) | collective-permute-done | bytes 262176 | tf_op jit(solution)/shard_map/while/body/eval_jaxpr/ppermute | solution.py:12
  82.4 6.5 %collective-permute-done = bf16[1024,128]{1,0:T(8,128)(2,1)} collective-permute-done((bf16[1024,128]{1,0:T(8,128)(2,1)S(1)}, bf16[1024,128]{1,0:T(8,128)(2,1)}, u32[]{:S(2)}, u32[]{:S(2)}) %collective-permute-start) | collective-permute-done | bytes 262176 | tf_op jit(solution)/shard_map/while/body/eval_jaxpr/ppermute | solution.py:12
  93.7 5.7 %collective-permute-done = bf16[1024,128]{1,0:T(8,128)(2,1)} collective-permute-done((bf16[1024,128]{1,0:T(8,128)(2,1)S(1)}, bf16[1024,128]{1,0:T(8,128)(2,1)}, u32[]{:S(2)}, u32[]{:S(2)}) %collective-permute-start) | collective-permute-done | bytes 262176 | tf_op jit(solution)/shard_map/while/body/eval_jaxpr/ppermute | solution.py:12
  104.2 5.7 %collective-permute-done = bf16[1024,128]{1,0:T(8,128)(2,1)} collective-permute-done((bf16[1024,128]{1,0:T(8,128)(2,1)S(1)}, bf16[1024,128]{1,0:T(8,128)(2,1)}, u32[]{:S(2)}, u32[]{:S(2)}) %collective-permute-start) | collective-permute-done | bytes 262176 | tf_op jit(solution)/shard_map/while/body/eval_jaxpr/ppermute | solution.py:12
  114.7 5.7 %collective-permute-done = bf16[1024,128]{1,0:T(8,128)(2,1)} collective-permute-done((bf16[1024,128]{1,0:T(8,128)(2,1)S(1)}, bf16[1024,128]{1,0:T(8,128)(2,1)}, u32[]{:S(2)}, u32[]{:S(2)}) %collective-permute-start) | collective-permute-done | bytes 262176 | tf_op jit(solution)/shard_map/while/body/eval_jaxpr/ppermute | solution.py:12
  125.2 5.7 %collective-permute-done = bf16[1024,128]{1,0:T(8,128)(2,1)} collective-permute-done((bf16[1024,128]{1,0:T(8,128)(2,1)S(1)}, bf16[1024,128]{1,0:T(8,128)(2,1)}, u32[]{:S(2)}, u32[]{:S(2)}) %collective-permute-start) | collective-permute-done | bytes 262176 | tf_op jit(solution)/shard_map/while/body/eval_jaxpr/ppermute | solution.py:12
  135.8 6.7 %collective-permute-done = bf16[1024,128]{1,0:T(8,128)(2,1)} collective-permute-done((bf16[1024,128]{1,0:T(8,128)(2,1)S(1)}, bf16[1024,128]{1,0:T(8,128)(2,1)}, u32[]{:S(2)}, u32[]{:S(2)}) %collective-permute-start) | collective-permute-done | bytes 262176 | tf_op jit(solution)/shard_map/while/body/eval_jaxpr/ppermute | solution.py:12
  147.3 7.9 %collective-permute-done = bf16[1024,128]{1,0:T(8,128)(2,1)} collective-permute-done((bf16[1024,128]{1,0:T(8,128)(2,1)S(1)}, bf16[1024,128]{1,0:T(8,128)(2,1)}, u32[]{:S(2)}, u32[]{:S(2)}) %collective-permute-start) | collective-permute-done | bytes 262176 | tf_op jit(solution)/shard_map/while/body/eval_jaxpr/ppermute | solution.py:12
  160.0 8.0 %collective-permute-done = bf16[1024,128]{1,0:T(8,128)(2,1)} collective-permute-done((bf16[1024,128]{1,0:T(8,128)(2,1)S(1)}, bf16[1024,128]{1,0:T(8,128)(2,1)}, u32[]{:S(2)}, u32[]{:S(2)}) %collective-permute-start) | collective-permute-done | bytes 262176 | tf_op jit(solution)/shard_map/while/body/eval_jaxpr/ppermute | solution.py:12
  172.8 7.2 %collective-permute-done = bf16[1024,128]{1,0:T(8,128)(2,1)} collective-permute-done((bf16[1024,128]{1,0:T(8,128)(2,1)S(1)}, bf16[1024,128]{1,0:T(8,128)(2,1)}, u32[]{:S(2)}, u32[]{:S(2)}) %collective-permute-start) | collective-permute-done | bytes 262176 | tf_op jit(solution)/shard_map/while/body/eval_jaxpr/ppermute | solution.py:12
  184.8 6.3 %collective-permute-done = bf16[1024,128]{1,0:T(8,128)(2,1)} collective-permute-done((bf16[1024,128]{1,0:T(8,128)(2,1)S(1)}, bf16[1024,128]{1,0:T(8,128)(2,1)}, u32[]{:S(2)}, u32[]{:S(2)}) %collective-permute-start) | collective-permute-done | bytes 262176 | tf_op jit(solution)/shard_map/while/body/eval_jaxpr/ppermute | solution.py:12
  195.9 5.7 %collective-permute-done = bf16[1024,128]{1,0:T(8,128)(2,1)} collective-permute-done((bf16[1024,128]{1,0:T(8,128)(2,1)S(1)}, bf16[1024,128]{1,0:T(8,128)(2,1)}, u32[]{:S(2)}, u32[]{:S(2)}) %collective-permute-start) | collective-permute-done | bytes 262176 | tf_op jit(solution)/shard_map/while/body/eval_jaxpr/ppermute | solution.py:12
  206.4 5.7 %collective-permute-done = bf16[1024,128]{1,0:T(8,128)(2,1)} collective-permute-done((bf16[1024,128]{1,0:T(8,128)(2,1)S(1)}, bf16[1024,128]{1,0:T(8,128)(2,1)}, u32[]{:S(2)}, u32[]{:S(2)}) %collective-permute-start) | collective-permute-done | bytes 262176 | tf_op jit(solution)/shard_map/while/body/eval_jaxpr/ppermute | solution.py:12
  217.0 5.7 %collective-permute-done = bf16[1024,128]{1,0:T(8,128)(2,1)} collective-permute-done((bf16[1024,128]{1,0:T(8,128)(2,1)S(1)}, bf16[1024,128]{1,0:T(8,128)(2,1)}, u32[]{:S(2)}, u32[]{:S(2)}) %collective-permute-start) | collective-permute-done | bytes 262176 | tf_op jit(solution)/shard_map/while/body/eval_jaxpr/ppermute | solution.py:12
  222.7 2.4 copy.12
  225.1 2.6 convolution_add_fusion
  227.7 2.3 copy.13
  230.0 2.6 copy.19
  233.0 114.2 %all-reduce.1 = bf16[8,128,6,128]{1,0,3,2:T(8,128)(2,1)} all-reduce(f32[8,128,6,128]{1,0,3,2:T(8,128)S(1)} %broadcast_multiply_fusion), channel_id=1, replica_groups=mesh['row'=16,'col'=4,'depth'=8] {'depth'}, use_global_device_ids=true, to_apply=%region_2.3 | all-reduce | flops 786432 | bytes 4718592 | tf_op jit(solution)/shard_map/psum | solution.py:54
  (63 shorter events, 76.9 us)
Async XLA Ops:
  6.5 3.7 %copy-start = (s32[1,8]{1,0:T(1,128)S(1)}, s32[1,8]{1,0:T(1,128)}, u32[]{:S(2)}) copy-start(s32[1,8]{1,0:T(1,128)} %param.13) | copy-start | bytes 100
  6.5 45.1 %all-gather.2.cloned.1.call-start = ((), (), s32[]{:S(2)}) async-start(), calls=%async_computation | async-start | bytes 3932160 | tf_op jit(solution)/shard_map/all_gather | solution.py:30
  52.6 13.0 %collective-permute-start = (bf16[1024,128]{1,0:T(8,128)(2,1)S(1)}, bf16[1024,128]{1,0:T(8,128)(2,1)}, u32[]{:S(2)}, u32[]{:S(2)}) collective-permute-start(bf16[1024,128]{1,0:T(8,128)(2,1)S(1)} %copy.29), channel_id=1, source_target_pairs={{480,0},{0,32},{32,64},{64,96},{96,128},{128,160},{160,192},{192,2... | collective-permute-start | bytes 786440 | tf_op jit(solution)/shard_map/while/body/eval_jaxpr/ppermute | solution.py:12
  66.5 11.2 %collective-permute-start = (bf16[1024,128]{1,0:T(8,128)(2,1)S(1)}, bf16[1024,128]{1,0:T(8,128)(2,1)}, u32[]{:S(2)}, u32[]{:S(2)}) collective-permute-start(bf16[1024,128]{1,0:T(8,128)(2,1)S(1)} %copy.29), channel_id=1, source_target_pairs={{480,0},{0,32},{32,64},{64,96},{96,128},{128,160},{160,192},{192,2... | collective-permute-start | bytes 786440 | tf_op jit(solution)/shard_map/while/body/eval_jaxpr/ppermute | solution.py:12
  78.6 10.3 %collective-permute-start = (bf16[1024,128]{1,0:T(8,128)(2,1)S(1)}, bf16[1024,128]{1,0:T(8,128)(2,1)}, u32[]{:S(2)}, u32[]{:S(2)}) collective-permute-start(bf16[1024,128]{1,0:T(8,128)(2,1)S(1)} %copy.29), channel_id=1, source_target_pairs={{480,0},{0,32},{32,64},{64,96},{96,128},{128,160},{160,192},{192,2... | collective-permute-start | bytes 786440 | tf_op jit(solution)/shard_map/while/body/eval_jaxpr/ppermute | solution.py:12
  89.9 9.6 %collective-permute-start = (bf16[1024,128]{1,0:T(8,128)(2,1)S(1)}, bf16[1024,128]{1,0:T(8,128)(2,1)}, u32[]{:S(2)}, u32[]{:S(2)}) collective-permute-start(bf16[1024,128]{1,0:T(8,128)(2,1)S(1)} %copy.29), channel_id=1, source_target_pairs={{480,0},{0,32},{32,64},{64,96},{96,128},{128,160},{160,192},{192,2... | collective-permute-start | bytes 786440 | tf_op jit(solution)/shard_map/while/body/eval_jaxpr/ppermute | solution.py:12
  100.4 9.6 %collective-permute-start = (bf16[1024,128]{1,0:T(8,128)(2,1)S(1)}, bf16[1024,128]{1,0:T(8,128)(2,1)}, u32[]{:S(2)}, u32[]{:S(2)}) collective-permute-start(bf16[1024,128]{1,0:T(8,128)(2,1)S(1)} %copy.29), channel_id=1, source_target_pairs={{480,0},{0,32},{32,64},{64,96},{96,128},{128,160},{160,192},{192,2... | collective-permute-start | bytes 786440 | tf_op jit(solution)/shard_map/while/body/eval_jaxpr/ppermute | solution.py:12
  110.9 9.6 %collective-permute-start = (bf16[1024,128]{1,0:T(8,128)(2,1)S(1)}, bf16[1024,128]{1,0:T(8,128)(2,1)}, u32[]{:S(2)}, u32[]{:S(2)}) collective-permute-start(bf16[1024,128]{1,0:T(8,128)(2,1)S(1)} %copy.29), channel_id=1, source_target_pairs={{480,0},{0,32},{32,64},{64,96},{96,128},{128,160},{160,192},{192,2... | collective-permute-start | bytes 786440 | tf_op jit(solution)/shard_map/while/body/eval_jaxpr/ppermute | solution.py:12
  121.4 9.6 %collective-permute-start = (bf16[1024,128]{1,0:T(8,128)(2,1)S(1)}, bf16[1024,128]{1,0:T(8,128)(2,1)}, u32[]{:S(2)}, u32[]{:S(2)}) collective-permute-start(bf16[1024,128]{1,0:T(8,128)(2,1)S(1)} %copy.29), channel_id=1, source_target_pairs={{480,0},{0,32},{32,64},{64,96},{96,128},{128,160},{160,192},{192,2... | collective-permute-start | bytes 786440 | tf_op jit(solution)/shard_map/while/body/eval_jaxpr/ppermute | solution.py:12
  131.9 10.6 %collective-permute-start = (bf16[1024,128]{1,0:T(8,128)(2,1)S(1)}, bf16[1024,128]{1,0:T(8,128)(2,1)}, u32[]{:S(2)}, u32[]{:S(2)}) collective-permute-start(bf16[1024,128]{1,0:T(8,128)(2,1)S(1)} %copy.29), channel_id=1, source_target_pairs={{480,0},{0,32},{32,64},{64,96},{96,128},{128,160},{160,192},{192,2... | collective-permute-start | bytes 786440 | tf_op jit(solution)/shard_map/while/body/eval_jaxpr/ppermute | solution.py:12
  143.5 11.8 %collective-permute-start = (bf16[1024,128]{1,0:T(8,128)(2,1)S(1)}, bf16[1024,128]{1,0:T(8,128)(2,1)}, u32[]{:S(2)}, u32[]{:S(2)}) collective-permute-start(bf16[1024,128]{1,0:T(8,128)(2,1)S(1)} %copy.29), channel_id=1, source_target_pairs={{480,0},{0,32},{32,64},{64,96},{96,128},{128,160},{160,192},{192,2... | collective-permute-start | bytes 786440 | tf_op jit(solution)/shard_map/while/body/eval_jaxpr/ppermute | solution.py:12
  156.2 11.8 %collective-permute-start = (bf16[1024,128]{1,0:T(8,128)(2,1)S(1)}, bf16[1024,128]{1,0:T(8,128)(2,1)}, u32[]{:S(2)}, u32[]{:S(2)}) collective-permute-start(bf16[1024,128]{1,0:T(8,128)(2,1)S(1)} %copy.29), channel_id=1, source_target_pairs={{480,0},{0,32},{32,64},{64,96},{96,128},{128,160},{160,192},{192,2... | collective-permute-start | bytes 786440 | tf_op jit(solution)/shard_map/while/body/eval_jaxpr/ppermute | solution.py:12
  169.0 11.1 %collective-permute-start = (bf16[1024,128]{1,0:T(8,128)(2,1)S(1)}, bf16[1024,128]{1,0:T(8,128)(2,1)}, u32[]{:S(2)}, u32[]{:S(2)}) collective-permute-start(bf16[1024,128]{1,0:T(8,128)(2,1)S(1)} %copy.29), channel_id=1, source_target_pairs={{480,0},{0,32},{32,64},{64,96},{96,128},{128,160},{160,192},{192,2... | collective-permute-start | bytes 786440 | tf_op jit(solution)/shard_map/while/body/eval_jaxpr/ppermute | solution.py:12
  181.0 10.2 %collective-permute-start = (bf16[1024,128]{1,0:T(8,128)(2,1)S(1)}, bf16[1024,128]{1,0:T(8,128)(2,1)}, u32[]{:S(2)}, u32[]{:S(2)}) collective-permute-start(bf16[1024,128]{1,0:T(8,128)(2,1)S(1)} %copy.29), channel_id=1, source_target_pairs={{480,0},{0,32},{32,64},{64,96},{96,128},{128,160},{160,192},{192,2... | collective-permute-start | bytes 786440 | tf_op jit(solution)/shard_map/while/body/eval_jaxpr/ppermute | solution.py:12
  192.1 9.6 %collective-permute-start = (bf16[1024,128]{1,0:T(8,128)(2,1)S(1)}, bf16[1024,128]{1,0:T(8,128)(2,1)}, u32[]{:S(2)}, u32[]{:S(2)}) collective-permute-start(bf16[1024,128]{1,0:T(8,128)(2,1)S(1)} %copy.29), channel_id=1, source_target_pairs={{480,0},{0,32},{32,64},{64,96},{96,128},{128,160},{160,192},{192,2... | collective-permute-start | bytes 786440 | tf_op jit(solution)/shard_map/while/body/eval_jaxpr/ppermute | solution.py:12
  202.6 9.6 %collective-permute-start = (bf16[1024,128]{1,0:T(8,128)(2,1)S(1)}, bf16[1024,128]{1,0:T(8,128)(2,1)}, u32[]{:S(2)}, u32[]{:S(2)}) collective-permute-start(bf16[1024,128]{1,0:T(8,128)(2,1)S(1)} %copy.29), channel_id=1, source_target_pairs={{480,0},{0,32},{32,64},{64,96},{96,128},{128,160},{160,192},{192,2... | collective-permute-start | bytes 786440 | tf_op jit(solution)/shard_map/while/body/eval_jaxpr/ppermute | solution.py:12
  213.1 9.6 %collective-permute-start = (bf16[1024,128]{1,0:T(8,128)(2,1)S(1)}, bf16[1024,128]{1,0:T(8,128)(2,1)}, u32[]{:S(2)}, u32[]{:S(2)}) collective-permute-start(bf16[1024,128]{1,0:T(8,128)(2,1)S(1)} %copy.29), channel_id=1, source_target_pairs={{480,0},{0,32},{32,64},{64,96},{96,128},{128,160},{160,192},{192,2... | collective-permute-start | bytes 786440 | tf_op jit(solution)/shard_map/while/body/eval_jaxpr/ppermute | solution.py:12
Sparse Core Ops, SparseCore 0:
  9.5 42.0 all-gather.1
where the time goes:
time: 358 us; the launch traced here: 357 us
  waiting for transfers between devices  134 us (37%)
  blocking collectives  114 us (32%)
  matrix products  30.7 us (9%)
  starting transfers between devices  30.4 us (8%)
  local copies, waits for them, and re-layouts  23.3 us (7%)
  between operations  15.4 us (4%)
  other arithmetic  8.19 us (2%)
    psum x1, blocking collectives, per_device(): summed = lax.psum(filtered, 'depth')  114 us
    ppermute x15, waiting for transfers between devices, from_behind(): return lax.ppermute(block, axis, route)  97.7 us
    all_gather x1, waiting for transfers between devices, per_device(): sign_whole = lax.all_gather(sign_kept, 'col', axis=0, tiled=True)  36.3 us
    ppermute x15, starting transfers between devices, from_behind(): return lax.ppermute(block, axis, route)  30.4 us
    dot_general x15, matrix products, advance(): jnp.dot(moving, sign_piece, preferred_element_type=jnp.float32)  28.1 us
    while x15, local copies, waits for them, and re-layouts  14.3 us
  transfers between devices with their start and end apart: 16, of which 16 were waited for; matrix products, arithmetic and copies ran while one was open for 9% of the time, Pallas kernels for 0%

commit v1 on v0

v1 whole, which is shorter than its diff:
```python
import jax
import jax.numpy as jnp
from jax import lax
from jax.sharding import PartitionSpec as P

BS = 128


def per_device(ks_matrix, sign_matrix, ks_mask, sign_mask, product_mask, row_order):
    row_blocks, inner_blocks = ks_mask.shape
    local_groups = sign_mask.shape[0]
    sign_inner = sign_mask.shape[2]
    col_blocks = sign_mask.shape[3]
    ks_panel = (
        ks_matrix.reshape(row_blocks, BS, inner_blocks, BS)
        * ks_mask.astype(jnp.bfloat16)[:, None, :, None]
    )
    ks_panel = ks_panel.reshape(row_blocks * BS, inner_blocks * BS)
    sign_kept = sign_matrix.reshape(local_groups, sign_inner, BS, col_blocks, BS)
    sign_kept = sign_kept * sign_mask.astype(jnp.bfloat16).reshape(
        local_groups, sign_inner, 1, col_blocks, 1
    )
    sign_kept = sign_kept.reshape(local_groups, sign_inner * BS, col_blocks * BS)
    sign_whole = lax.all_gather(sign_kept, "col", axis=0, tiled=True)
    ks_whole = lax.all_gather(ks_panel, "row", axis=0, tiled=False)
    product = jnp.einsum(
        "sik,skn->in", ks_whole, sign_whole, preferred_element_type=jnp.float32
    )
    filtered = (
        product.reshape(row_blocks, BS, col_blocks, BS)
        * product_mask.astype(jnp.float32)[:, None, :, None]
    )
    arranged = jnp.take(filtered, row_order[0], axis=0)
    arranged = arranged.reshape(row_blocks * BS, col_blocks * BS)
    summed = lax.psum_scatter(arranged, "depth", scatter_dimension=0, tiled=True)
    return summed.astype(jnp.bfloat16)


def solution(mesh):
    in_specs = (
        P("col", ("row", "depth")),
        P("col", "depth", None, "row"),
        P("col", ("row", "depth")),
        P("col", "depth", None, "row"),
        P("col", "row"),
        P("col", None),
    )
    out_specs = P(("col", "depth"), "row")
    return jax.shard_map(
        per_device, mesh=mesh, in_specs=in_specs, out_specs=out_specs, check_vma=False
    )
```

time: 358 us -> 243 us (0.68)
  the two profiles are of different devices: /device:TPU:4 before, /device:TPU:1 now
where the time goes in v1:
time: 243 us; the launch traced here: 242 us
  waiting for transfers between devices  199 us (82%)
  other arithmetic  14.5 us (6%)
  between operations  13.2 us (5%)
  local copies, waits for them, and re-layouts  9.19 us (4%)
  matrix products  6.23 us (3%)
    reduce_scatter x1, waiting for transfers between devices, per_device(): lax.psum_scatter(arranged, 'depth', scatter_dimension=0, tiled=True)  84.9 us
    all_gather x1, waiting for transfers between devices, per_device(): ks_whole = lax.all_gather(ks_panel, 'row', axis=0, tiled=False)  71.2 us
    all_gather x1, waiting for transfers between devices, per_device(): sign_whole = lax.all_gather(sign_kept, 'col', axis=0, tiled=True)  43.2 us
    dot_general x1, matrix products, per_device(): jnp.einsum('sik,skn->in', ks_whole, sign_whole, preferred_element_type=jn...  6.23 us
    gather x2, local copies, waits for them, and re-layouts, per_device(): arranged = jnp.take(filtered, row_order[0], axis=0)  5.03 us
  transfers between devices with their start and end apart: 3, of which 3 were waited for; matrix products, arithmetic and copies ran while one was open for 1% of the time, Pallas kernels for 0%

profile of v1, /device:TPU:1, one launch (start us, length us, event | category | flops | bytes accessed | tf_op | source)
XLA Modules:
  0.0 242.5 jit_solution(16776493205895536926)
XLA Ops:
  6.5 0.7 convert_element_type.13
  7.3 0.1 broadcast_bitcast_fusion
  7.3 2.1 bitcast_multiply_fusion
  9.4 0.0 all-gather.4.cloned.1.call-update
  9.4 0.0 all-gather.6.cloned.1.call-start
  9.5 0.7 convert_bitcast_fusion
  10.2 0.1 broadcast_bitcast_fusion.2
  10.2 1.9 broadcast_multiply_fusion.1
  12.1 0.0 all-gather.6.cloned.1.call-update
  12.2 0.0 reduce-scatter.2.cloned.1.call-start
  12.3 0.1 broadcast_bitcast_fusion.1
  12.4 43.2 %all-gather.4.cloned.1.call-done = bf16[16,128,768]{2,1,0:T(8,128)(2,1)} async-done(((bf16[4,128,768]{2,1,0:T(8,128)(2,1)}), bf16[16,128,768]{2,1,0:T(8,128)(2,1)}) %all-gather.4.cloned.1.call-update) | async-done | bytes 3145744 | tf_op jit(solution)/shard_map/all_gather | solution.py:24
  55.5 71.2 %all-gather.6.cloned.1.call-done = bf16[16384,128]{1,0:T(8,128)(2,1)} async-done(((bf16[1024,128]{1,0:T(8,128)(2,1)}), bf16[16384,128]{1,0:T(8,128)(2,1)}) %all-gather.6.cloned.1.call-update) | async-done | bytes 4194320 | tf_op jit(solution)/shard_map/all_gather | solution.py:25
  126.7 6.2 %convolution_bitcast_fusion = f32[96,8,8,128]{3,1,2,0:T(8,128)S(1)} fusion(bf16[16,1024,128]{2,1,0:T(8,128)(2,1)} %bitcast.42, bf16[16,128,768]{2,1,0:T(8,128)(2,1)} %all-gather.4.cloned.1.call-done), kind=kOutput, calls=%fused_computation.2 | convolution fusion | flops 3221225472 | bytes 10485760 | tf_op jit(solution)/shard_map/sik,skn->in/dot_general | solution.py:26
  132.9 0.7 copy.22
  133.7 2.3 copy.15
  136.0 3.8 %broadcast_multiply_fusion = f32[8,128,6,128]{3,1,2,0:T(8,128)} fusion(f32[8,128,6,128]{3,1,2,0:T(8,128)} %copy.15, f32[8,6]{1,0:T(8,128)S(1)} %convert_element_type.14), kind=kLoop, calls=%fused_computation.3 | loop fusion | flops 786432 | bytes 6291648 | tf_op jit(solution)/shard_map/mul | solution.py:30
  139.8 2.6 %gather_fusion = f32[8,128,6,128]{3,1,2,0:T(8,128)S(1)} fusion(f32[8,128,6,128]{3,1,2,0:T(8,128)} %broadcast_multiply_fusion, s32[1024]{0:T(1024)S(1)} %pad_clamp_fusion), kind=kCustom, calls=%fused_computation | custom fusion | bytes 6291488 | tf_op jit(solution)/shard_map/jit(_take)/gather | solution.py:33
  142.5 2.4 copy.16
  144.9 4.3 %bitcast_select_fusion = f32[1024,768]{0,1:T(8,128)} fusion(f32[96,8,8,128]{3,2,1,0:T(8,128)} %bitcast.39, pred[1024]{0:T(1024)(128)(4,1)S(1)} %broadcast_bitcast_fusion.1), kind=kLoop, calls=%fused_computation.1 | loop fusion | flops 786432 | bytes 6292480 | tf_op jit(solution)/shard_map/jit(_take)/select_n | solution.py:33
  149.2 0.0 reduce-scatter.2.cloned.1.call-update
  149.2 84.9 %reduce-scatter.2.cloned.1.call-done = f32[128,768]{0,1:T(8,128)} async-done(((f32[1024,768]{0,1:T(8,128)}), f32[128,768]{0,1:T(8,128)}) %reduce-scatter.2.cloned.1.call-update) | async-done | bytes 393232 | tf_op jit(solution)/shard_map/reduce_scatter | solution.py:35
  234.1 1.0 convert_element_type.15
  235.1 0.8 copy.17
  (11 shorter events, 0.0 us)
Async XLA Ops:
  6.5 5.7 %copy-start = (s32[8,6]{1,0:T(8,128)S(1)}, s32[8,6]{1,0:T(8,128)}, u32[]{:S(2)}) copy-start(s32[8,6]{1,0:T(8,128)} %param.10) | copy-start | bytes 580
  6.5 5.7 %copy-start.1 = (s32[1,8]{1,0:T(1,128)S(1)}, s32[1,8]{1,0:T(1,128)}, u32[]{:S(2)}) copy-start(s32[1,8]{1,0:T(1,128)} %param.11) | copy-start | bytes 100
  6.5 49.0 %all-gather.4.cloned.1.call-start = ((), (), s32[]{:S(2)}) async-start(), calls=%async_computation.1 | async-start | bytes 3932160 | tf_op jit(solution)/shard_map/all_gather | solution.py:24
  9.4 117.3 %all-gather.6.cloned.1.call-start = ((), (), s32[]{:S(2)}) async-start(), calls=%async_computation.3 | async-start | bytes 4456448 | tf_op jit(solution)/shard_map/all_gather | solution.py:25
  12.2 221.9 %reduce-scatter.2.cloned.1.call-start = ((), (), s32[]{:S(2)}) async-start(), calls=%async_computation.2 | async-start | bytes 3538944 | tf_op jit(solution)/shard_map/reduce_scatter | solution.py:35
Sparse Core Ops, SparseCore 0:
  9.6 45.9 all-gather.3
  57.6 69.0 all-gather.5
  149.3 84.7 reduce-scatter.1

commit v2 on v1

v2 whole, which is shorter than its diff:
```python
import jax
import jax.numpy as jnp
from jax import lax
from jax.sharding import PartitionSpec as P

BS = 128


def swap_with(block, axis, flip):
    devices = range(lax.axis_size(axis))
    return lax.ppermute(block, axis, [(i, i ^ flip) for i in devices])


def per_device(ks_matrix, sign_matrix, ks_mask, sign_mask, product_mask, row_order):
    row_blocks, inner_blocks = ks_mask.shape
    local_groups = sign_mask.shape[0]
    sign_inner = sign_mask.shape[2]
    col_blocks = sign_mask.shape[3]
    col_count = lax.axis_size("col")
    local_order = row_order[0]
    ks_panel = (
        ks_matrix.reshape(row_blocks, BS, inner_blocks, BS)
        * ks_mask.astype(jnp.bfloat16)[:, None, :, None]
    )
    ks_panel = jnp.take(ks_panel, local_order, axis=0, mode="clip")
    ks_panel = ks_panel.reshape(row_blocks * BS, inner_blocks * BS)
    sign_kept = sign_matrix.reshape(local_groups, sign_inner, BS, col_blocks, BS)
    sign_kept = sign_kept * sign_mask.astype(jnp.bfloat16).reshape(
        local_groups, sign_inner, 1, col_blocks, 1
    )
    sign_kept = sign_kept.reshape(local_groups, sign_inner * BS, col_blocks * BS)
    far = swap_with(sign_kept, "col", 2)
    pair = jnp.concatenate([sign_kept, far], axis=0)
    near = swap_with(pair, "col", 1)
    sign_four = jnp.concatenate([pair, near], axis=0)
    me = lax.axis_index("col")
    held_cols = jnp.stack([me, me ^ 2, me ^ 1, me ^ 3])
    ks_whole = lax.all_gather(ks_panel, "row", axis=0, tiled=False)
    ks_whole = ks_whole.reshape(
        col_count, local_groups, row_blocks * BS, inner_blocks * BS
    )
    ks_matched = jnp.take(ks_whole, held_cols, axis=0, mode="clip")
    ks_matched = ks_matched.reshape(
        col_count * local_groups, row_blocks * BS, inner_blocks * BS
    )
    product = jnp.einsum(
        "sik,skn->in", ks_matched, sign_four, preferred_element_type=jnp.float32
    )
    summed = lax.psum_scatter(product, "depth", scatter_dimension=0, tiled=True)
    own_row = lax.dynamic_index_in_dim(
        local_order, lax.axis_index("depth"), 0, keepdims=False
    )
    own_mask = lax.dynamic_index_in_dim(product_mask, own_row, 0, keepdims=False)
    kept = summed.reshape(BS, col_blocks, BS) * own_mask.astype(jnp.float32)[None, :, None]
    return kept.reshape(BS, col_blocks * BS).astype(jnp.bfloat16)


def solution(mesh):
    in_specs = (
        P("col", ("row", "depth")),
        P("col", "depth", None, "row"),
        P("col", ("row", "depth")),
        P("col", "depth", None, "row"),
        P("col", "row"),
        P("col", None),
    )
    out_specs = P(("col", "depth"), "row")
    return jax.shard_map(
        per_device, mesh=mesh, in_specs=in_specs, out_specs=out_specs, check_vma=False
    )
```

time: 243 us -> 191 us (0.79)
  waiting for transfers between devices: 199 us -> 142 us
  starting transfers between devices: 0.09 us -> 12.1 us
  other arithmetic: 14.5 us -> 6.85 us
    all_gather x1 -> x0, waiting for transfers between devices: 43.2 us -> none  [per_device(): sign_whole = lax.all_gather(sign_kept, 'col', axis=0, tiled=True)]
    all_gather x1, waiting for transfers between devices: 71.2 us -> 47.5 us  [per_device(): ks_whole = lax.all_gather(ks_panel, 'row', axis=0, tiled=False)]
    ppermute x0 -> x2, waiting for transfers between devices: none -> 13.8 us  [swap_with(): return lax.ppermute(block, axis, [(i, i ^ flip) for i in devices])]
    ppermute x0 -> x2, starting transfers between devices: none -> 12.1 us  [swap_with(): return lax.ppermute(block, axis, [(i, i ^ flip) for i in devices])]
    select_n x2 -> x0, other arithmetic: 4.34 us -> none  [per_device(): arranged = jnp.take(filtered, row_order[0], axis=0)]
    reduce_scatter x1, waiting for transfers between devices: 84.9 us -> 80.7 us  [per_device(): summed = lax.psum_scatter(product, 'depth', scatter_dimension=0, tiled=True)]
    mul x1 -> x0, other arithmetic: 3.8 us -> none  [per_device(): product.reshape(row_blocks, BS, col_blocks, BS)]
  transfers between devices with their start and end apart: 3 -> 4, of which waited for: 3 -> 3; matrix products, arithmetic and copies ran while one was open for 1% -> 5% of each run, Pallas kernels for 0% -> 0%
where the time goes in v2:
time: 191 us
  waiting for transfers between devices  142 us (74%)
  between operations  15.4 us (8%)
  starting transfers between devices  12.1 us (6%)
  local copies, waits for them, and re-layouts  7.9 us (4%)
  other arithmetic  6.85 us (4%)
  matrix products  6.81 us (4%)
    reduce_scatter x1, waiting for transfers between devices, per_device(): summed = lax.psum_scatter(product, 'depth', scatter_dimension=0, tiled=True)  80.7 us
    all_gather x1, waiting for transfers between devices, per_device(): ks_whole = lax.all_gather(ks_panel, 'row', axis=0, tiled=False)  47.5 us
    ppermute x2, waiting for transfers between devices, swap_with(): return lax.ppermute(block, axis, [(i, i ^ flip) for i in devices])  13.8 us
    ppermute x2, starting transfers between devices, swap_with(): return lax.ppermute(block, axis, [(i, i ^ flip) for i in devices])  12.1 us
    dot_general x1, matrix products, per_device(): jnp.einsum('sik,skn->in', ks_matched, sign_four, preferred_element_type=j...  6.81 us
    gather x1, local copies, waits for them, and re-layouts, per_device(): ks_matched = jnp.take(ks_whole, held_cols, axis=0, mode='clip')  5.24 us
  transfers between devices with their start and end apart: 4, of which 3 were waited for; matrix products, arithmetic and copies ran while one was open for 5% of the time, Pallas kernels for 0%

profile of v2, /device:TPU:1, one launch (start us, length us, event | category | flops | bytes accessed | tf_op | source)
XLA Modules:
  0.0 191.1 jit_solution(15614657143289792770)
XLA Ops:
  6.5 0.7 convert_bitcast_fusion.1
  7.2 0.7 pad_clamp_fusion.1
  7.9 1.0 multiply_bitcast_fusion
  8.9 1.3 gather_fusion
  10.2 0.0 all-gather.2.cloned.1.call-update
  10.2 0.0 reduce-scatter.2.cloned.1.call-start
  10.3 0.7 convert_element_type.20
  11.0 0.1 broadcast_bitcast_fusion
  11.0 1.2 bitcast_multiply_fusion
  12.2 5.5 %collective-permute-start = (bf16[4,128,768]{2,1,0:T(8,128)(2,1)S(1)}, bf16[4,128,768]{2,1,0:T(8,128)(2,1)S(1)}, u32[]{:S(2)}, u32[]{:S(2)}) collective-permute-start(bf16[4,128,768]{2,1,0:T(8,128)(2,1)S(1)} %bitcast_multiply_fusion), channel_id=1, source_target_pairs={{0,16},{8,24},{16,0},{24,8},{1,17},{9,25},{17,1},{25,9},{2,18},{10... | collective-permute-start | bytes 2359304 | tf_op jit(solution)/shard_map/ppermute | solution.py:11
  17.7 13.8 %collective-permute-done = bf16[4,128,768]{2,1,0:T(8,128)(2,1)S(1)} collective-permute-done((bf16[4,128,768]{2,1,0:T(8,128)(2,1)S(1)}, bf16[4,128,768]{2,1,0:T(8,128)(2,1)S(1)}, u32[]{:S(2)}, u32[]{:S(2)}) %collective-permute-start) | collective-permute-done | bytes 786464 | tf_op jit(solution)/shard_map/ppermute | solution.py:11
  31.5 0.1 pad_maximum_fusion
  31.6 6.6 %collective-permute-start.1 = (bf16[8,128,768]{2,1,0:T(8,128)(2,1)S(1)}, bf16[8,128,768]{2,1,0:T(8,128)(2,1)}, u32[]{:S(2)}, u32[]{:S(2)}) collective-permute-start(bf16[8,128,768]{2,1,0:T(8,128)(2,1)S(1)} %pad_maximum_fusion), channel_id=1, source_target_pairs={{0,8},{8,0},{16,24},{24,16},{1,9},{9,1},{17,25},{25,17},{2,10},{10... | collective-permute-start | bytes 4718600 | tf_op jit(solution)/shard_map/ppermute | solution.py:11
  38.3 0.1 pad_add_fusion
  38.4 47.5 %all-gather.2.cloned.1.call-done = bf16[16,1024,128]{2,1,0:T(8,128)(2,1)} async-done(((bf16[1,1024,128]{2,1,0:T(8,128)(2,1)}), bf16[16,1024,128]{2,1,0:T(8,128)(2,1)}) %all-gather.2.cloned.1.call-update) | async-done | bytes 4194320 | tf_op jit(solution)/shard_map/all_gather | solution.py:38
  85.8 5.2 %gather_fusion.1 = bf16[4,4,1024,128]{3,2,1,0:T(8,128)(2,1)} fusion(bf16[4,4,1024,128]{3,2,1,0:T(8,128)(2,1)} %bitcast.31, s32[1024]{0:T(1024)S(1)} %pad_clamp_fusion), kind=kCustom, calls=%fused_computation.1 | custom fusion | bytes 8388624 | tf_op jit(solution)/shard_map/jit(_take)/gather | solution.py:42
  91.1 6.8 %fusion.6 = f32[1024,768]{1,0:T(8,128)} fusion(bf16[16,1024,128]{2,1,0:T(8,128)(2,1)} %bitcast.32, bf16[8,128,768]{2,1,0:T(8,128)(2,1)} %collective-permute-done.1, bf16[4,128,768]{2,1,0:T(8,128)(2,1)S(1)} %collective-permute-done, bf16[4,128,768]{2,1,0:T(8,128)(2,1)S(1)} %bitcast_multiply_fusion), kind=kOutput, calls=%fused_computation.8 | convolution fusion | flops 3224371200 | bytes 10485760 | tf_op jit(solution)/shard_map/sik,skn->in/dot_general | solution.py:46
  97.9 0.0 reduce-scatter.2.cloned.1.call-update
  97.9 0.6 copy-done
  98.6 0.6 constant_dynamic-slice_fusion
  101.1 0.7 convert_bitcast_fusion
  101.8 0.1 broadcast_bitcast_fusion.1
  101.8 80.7 %reduce-scatter.2.cloned.1.call-done = f32[128,768]{1,0:T(8,128)} async-done(((f32[1024,768]{1,0:T(8,128)}), f32[128,768]{1,0:T(8,128)}) %reduce-scatter.2.cloned.1.call-update) | async-done | bytes 393232 | tf_op jit(solution)/shard_map/reduce_scatter | solution.py:49
  182.5 1.7 multiply_convert_fusion
  (6 shorter events, 0.0 us)
Async XLA Ops:
  6.5 79.3 %all-gather.2.cloned.1.call-start = ((), (), s32[]{:S(2)}) async-start(), calls=%async_computation.1 | async-start | bytes 4456448 | tf_op jit(solution)/shard_map/all_gather | solution.py:38
  10.2 172.3 %reduce-scatter.2.cloned.1.call-start = ((), (), s32[]{:S(2)}) async-start(), calls=%async_computation.2 | async-start | bytes 3538944 | tf_op jit(solution)/shard_map/reduce_scatter | solution.py:49
  12.2 19.3 %collective-permute-start = (bf16[4,128,768]{2,1,0:T(8,128)(2,1)S(1)}, bf16[4,128,768]{2,1,0:T(8,128)(2,1)S(1)}, u32[]{:S(2)}, u32[]{:S(2)}) collective-permute-start(bf16[4,128,768]{2,1,0:T(8,128)(2,1)S(1)} %bitcast_multiply_fusion), channel_id=1, source_target_pairs={{0,16},{8,24},{16,0},{24,8},{1,17},{9,25},{17,1},{25,9},{2,18},{10... | collective-permute-start | bytes 2359304 | tf_op jit(solution)/shard_map/ppermute | solution.py:11
  31.6 59.5 %collective-permute-start.1 = (bf16[8,128,768]{2,1,0:T(8,128)(2,1)S(1)}, bf16[8,128,768]{2,1,0:T(8,128)(2,1)}, u32[]{:S(2)}, u32[]{:S(2)}) collective-permute-start(bf16[8,128,768]{2,1,0:T(8,128)(2,1)S(1)} %pad_maximum_fusion), channel_id=1, source_target_pairs={{0,8},{8,0},{16,24},{24,16},{1,9},{9,1},{17,25},{25,17},{2,10},{10... | collective-permute-start | bytes 4718600 | tf_op jit(solution)/shard_map/ppermute | solution.py:11
  97.9 0.7 copy-start
Sparse Core Ops, SparseCore 0:
  10.3 75.4 all-gather.1
  98.0 84.4 reduce-scatter.1

commit v3 on v2

--- a/solution.py
+++ b/solution.py
@@ -43,10 +43,34 @@
     ks_matched = ks_matched.reshape(
         col_count * local_groups, row_blocks * BS, inner_blocks * BS
     )
-    product = jnp.einsum(
-        "sik,skn->in", ks_matched, sign_four, preferred_element_type=jnp.float32
+    depth_count = lax.axis_size("depth")
+    pair_count = 2
+    ring_count = depth_count // pair_count
+    depth_me = lax.axis_index("depth")
+    ring_me = depth_me // pair_count
+    piece_rows = row_blocks * BS // ring_count
+
+    def piece_for(ring_spot):
+        rows = lax.dynamic_slice_in_dim(ks_matched, ring_spot * piece_rows, piece_rows, 1)
+        return jnp.einsum(
+            "sik,skn->in", rows, sign_four, preferred_element_type=jnp.float32
+        )
+
+    total = piece_for(ring_me)
+    for shift in range(1, ring_count):
+        piece = piece_for((ring_me + shift) % ring_count)
+        route = [
+            (d, ((d // pair_count + shift) % ring_count) * pair_count + d % pair_count)
+            for d in range(depth_count)
+        ]
+        total = total + lax.ppermute(piece, "depth", route)
+    halves = total.reshape(pair_count, BS, col_blocks * BS)
+    pair_me = depth_me % pair_count
+    keep = lax.dynamic_index_in_dim(halves, pair_me, 0, keepdims=False)
+    give = lax.dynamic_index_in_dim(halves, 1 - pair_me, 0, keepdims=False)
+    summed = keep + lax.ppermute(
+        give, "depth", [(d, d ^ 1) for d in range(depth_count)]
     )
-    summed = lax.psum_scatter(product, "depth", scatter_dimension=0, tiled=True)
     own_row = lax.dynamic_index_in_dim(
         local_order, lax.axis_index("depth"), 0, keepdims=False
     )

time: 191 us -> 162 us (0.85)
  the two profiles are of different devices: /device:TPU:1 before, /device:TPU:12 now
where the time goes in v3:
time: 162 us; the launch traced here: 161 us
  waiting for transfers between devices  100 us (62%)
  starting transfers between devices  17.6 us (11%)
  between operations  15.6 us (10%)
  matrix products  13.6 us (8%)
  local copies, waits for them, and re-layouts  8.19 us (5%)
  other arithmetic  5.87 us (4%)
    all_gather x1, waiting for transfers between devices, per_device(): ks_whole = lax.all_gather(ks_panel, 'row', axis=0, tiled=False)  56.3 us
    ppermute x2, waiting for transfers between devices, swap_with(): return lax.ppermute(block, axis, [(i, i ^ flip) for i in devices])  20.3 us
    ppermute x3, waiting for transfers between devices, per_device(): total = total + lax.ppermute(piece, 'depth', route)  20.1 us
    dot_general x4, matrix products, piece_for(): jnp.einsum('sik,skn->in', rows, sign_four, preferred_element_type=jnp.flo...  13.6 us
    ppermute x3, starting transfers between devices, per_device(): total = total + lax.ppermute(piece, 'depth', route)  10.4 us
    gather x1, local copies, waits for them, and re-layouts, per_device(): ks_matched = jnp.take(ks_whole, held_cols, axis=0, mode='clip')  5.23 us
    ppermute x2, starting transfers between devices, swap_with(): return lax.ppermute(block, axis, [(i, i ^ flip) for i in devices])  4.34 us
    ppermute x1, waiting for transfers between devices, per_device(): lax.ppermute(give, 'depth', [(d, d ^ 1) for d in range(depth_count)])  3.55 us
  transfers between devices with their start and end apart: 7, of which 6 were waited for; matrix products, arithmetic and copies ran while one was open for 10% of the time, Pallas kernels for 0%

profile of v3, /device:TPU:12, one launch (start us, length us, event | category | flops | bytes accessed | tf_op | source)
XLA Modules:
  0.0 161.1 jit_solution(7936102901542853275)
XLA Ops:
  7.2 0.7 pad_clamp_fusion.1
  7.9 1.0 multiply_bitcast_fusion
  8.9 1.3 gather_fusion
  10.2 0.7 convert_element_type.20
  11.0 1.2 bitcast_multiply_fusion
  12.2 2.4 %collective-permute-start = (bf16[4,128,768]{2,1,0:T(8,128)(2,1)S(1)}, bf16[4,128,768]{2,1,0:T(8,128)(2,1)S(1)}, u32[]{:S(2)}, u32[]{:S(2)}) collective-permute-start(bf16[4,128,768]{2,1,0:T(8,128)(2,1)S(1)} %bitcast_multiply_fusion), channel_id=1, source_target_pairs={{0,16},{8,24},{16,0},{24,8},{1,17},{9,25},{17,1},{25,9},{2,18},{10... | collective-permute-start | bytes 2359304 | tf_op jit(solution)/shard_map/ppermute | solution.py:11
  14.6 20.3 %collective-permute-done = bf16[4,128,768]{2,1,0:T(8,128)(2,1)S(1)} collective-permute-done((bf16[4,128,768]{2,1,0:T(8,128)(2,1)S(1)}, bf16[4,128,768]{2,1,0:T(8,128)(2,1)S(1)}, u32[]{:S(2)}, u32[]{:S(2)}) %collective-permute-start) | collective-permute-done | bytes 786464 | tf_op jit(solution)/shard_map/ppermute | solution.py:11
  35.0 1.9 %collective-permute-start.1 = (bf16[8,128,768]{2,1,0:T(8,128)(2,1)S(1)}, bf16[8,128,768]{2,1,0:T(8,128)(2,1)}, u32[]{:S(2)}, u32[]{:S(2)}) collective-permute-start(bf16[8,128,768]{2,1,0:T(8,128)(2,1)S(1)} %pad_maximum_fusion.1), channel_id=1, source_target_pairs={{0,8},{8,0},{16,24},{24,16},{1,9},{9,1},{17,25},{25,17},{2,10},{10... | collective-permute-start | bytes 4718600 | tf_op jit(solution)/shard_map/ppermute | solution.py:11
  37.1 56.3 %all-gather.2.cloned.1.call-done = bf16[16,1024,128]{2,1,0:T(8,128)(2,1)} async-done(((bf16[1,1024,128]{2,1,0:T(8,128)(2,1)}), bf16[16,1024,128]{2,1,0:T(8,128)(2,1)}) %all-gather.2.cloned.1.call-update) | async-done | bytes 4194320 | tf_op jit(solution)/shard_map/all_gather | solution.py:38
  93.4 5.2 %gather_fusion.1 = bf16[4,4,1024,128]{3,2,1,0:T(8,128)(2,1)} fusion(bf16[4,4,1024,128]{3,2,1,0:T(8,128)(2,1)} %bitcast.51, s32[1024]{0:T(1024)S(1)} %pad_clamp_fusion), kind=kCustom, calls=%fused_computation.1 | custom fusion | bytes 8388624 | tf_op jit(solution)/shard_map/jit(_take)/gather | solution.py:42
  98.7 3.8 %convolution_bitcast_fusion.2 = f32[256,768]{1,0:T(8,128)} fusion(bf16[16,1024,128]{2,1,0:T(8,128)(2,1)} %bitcast.52, s32[]{:T(128)S(6)} %select_n.53, bf16[8,128,768]{2,1,0:T(8,128)(2,1)} %collective-permute-done.1, bf16[4,128,768]{2,1,0:T(8,128)(2,1)S(1)} %collective-permute-done, bf16[4,128,768]{2,1,0:T(8,128)(2,1)S(1)} %bitcast_multiply_fusion), kind=kOutput, calls=%fused_computation.6 | convolution fusion | flops 808452096 | bytes 4980740 | tf_op jit(solution)/shard_map/sik,skn->in/dot_general | solution.py:55
  102.4 3.4 %collective-permute-start.2 = (f32[256,768]{1,0:T(8,128)}, f32[256,768]{1,0:T(8,128)S(1)}, u32[]{:S(2)}, u32[]{:S(2)}) collective-permute-start(f32[256,768]{1,0:T(8,128)} %convolution_bitcast_fusion.2), channel_id=1, source_target_pairs={{0,2},{1,3},{2,4},{3,5},{4,6},{5,7},{6,0},{7,1},{8,10},{9,11},{10,... | collective-permute-start | bytes 2359304 | tf_op jit(solution)/shard_map/ppermute | solution.py:66
  105.9 3.3 %convolution_bitcast_fusion.1 = f32[256,768]{1,0:T(8,128)} fusion(bf16[16,1024,128]{2,1,0:T(8,128)(2,1)S(1)} %bitcast.54, s32[]{:T(128)S(6)} %select_n.55, bf16[8,128,768]{2,1,0:T(8,128)(2,1)} %collective-permute-done.1, bf16[4,128,768]{2,1,0:T(8,128)(2,1)S(1)} %collective-permute-done, bf16[4,128,768]{2,1,0:T(8,128)(2,1)S(1)} %bitcast_multiply_fusion), kind=kOutput, calls=%fused_computation.5 | convolution fusion | flops 808452096 | bytes 4980740 | tf_op jit(solution)/shard_map/sik,skn->in/dot_general | solution.py:55
  109.2 3.0 %collective-permute-start.3 = (f32[256,768]{1,0:T(8,128)}, f32[256,768]{1,0:T(8,128)S(1)}, u32[]{:S(2)}, u32[]{:S(2)}) collective-permute-start(f32[256,768]{1,0:T(8,128)} %convolution_bitcast_fusion.1), channel_id=1, source_target_pairs={{0,4},{1,5},{2,6},{3,7},{4,0},{5,1},{6,2},{7,3},{8,12},{9,13},{10,... | collective-permute-start | bytes 2359304 | tf_op jit(solution)/shard_map/ppermute | solution.py:66
  112.2 3.4 %convolution_bitcast_fusion = f32[256,768]{1,0:T(8,128)} fusion(bf16[16,1024,128]{2,1,0:T(8,128)(2,1)S(1)} %bitcast.55, s32[]{:T(128)S(6)} %select_n.57, bf16[8,128,768]{2,1,0:T(8,128)(2,1)} %collective-permute-done.1, bf16[4,128,768]{2,1,0:T(8,128)(2,1)S(1)} %collective-permute-done, bf16[4,128,768]{2,1,0:T(8,128)(2,1)S(1)} %bitcast_multiply_fusion), kind=kOutput, calls=%fused_computation.4 | convolution fusion | flops 808452096 | bytes 4980740 | tf_op jit(solution)/shard_map/sik,skn->in/dot_general | solution.py:55
  115.6 4.0 %collective-permute-start.4 = (f32[256,768]{1,0:T(8,128)}, f32[256,768]{1,0:T(8,128)}, u32[]{:S(2)}, u32[]{:S(2)}) collective-permute-start(f32[256,768]{1,0:T(8,128)} %convolution_bitcast_fusion), channel_id=1, source_target_pairs={{0,6},{1,7},{2,0},{3,1},{4,2},{5,3},{6,4},{7,5},{8,14},{9,15},{10,... | collective-permute-start | bytes 2359304 | tf_op jit(solution)/shard_map/ppermute | solution.py:66
  119.6 12.1 %collective-permute-done.2 = f32[256,768]{1,0:T(8,128)S(1)} collective-permute-done((f32[256,768]{1,0:T(8,128)}, f32[256,768]{1,0:T(8,128)S(1)}, u32[]{:S(2)}, u32[]{:S(2)}) %collective-permute-start.2) | collective-permute-done | bytes 786464 | tf_op jit(solution)/shard_map/ppermute | solution.py:66
  132.3 0.9 copy-done.2
  133.1 7.5 %collective-permute-done.4 = f32[256,768]{1,0:T(8,128)} collective-permute-done((f32[256,768]{1,0:T(8,128)}, f32[256,768]{1,0:T(8,128)}, u32[]{:S(2)}, u32[]{:S(2)}) %collective-permute-start.4) | collective-permute-done | bytes 786464 | tf_op jit(solution)/shard_map/ppermute | solution.py:66
  140.6 3.2 %fusion.2 = f32[256,768]{1,0:T(8,128)S(1)} fusion(f32[256,768]{1,0:T(8,128)} %collective-permute-done.4, f32[256,768]{1,0:T(8,128)} %copy-done.2, f32[256,768]{1,0:T(8,128)S(1)} %collective-permute-done.2, bf16[16,1024,128]{2,1,0:T(8,128)(2,1)} %bitcast.53, s32[]{:T(128)S(6)} %select_n.51, bf16[8,128,768]{2,1,0:T(8,128)(2,1)} %collective-permute-done.1, ...), kind=kOutput, calls=%fused_computation.10 | convolution fusion | flops 809041920 | bytes 7340036 | tf_op jit(solution)/shard_map/sik,skn->in/dot_general | solution.py:55
  143.9 2.8 %collective-permute-start.5 = (f32[128,768]{1,0:T(8,128)S(1)}, f32[128,768]{1,0:T(8,128)S(1)}, u32[]{:S(2)}, u32[]{:S(2)}) collective-permute-start(f32[128,768]{1,0:T(8,128)S(1)} %dynamic-slice_bitcast_fusion), channel_id=1, source_target_pairs={{0,1},{1,0},{2,3},{3,2},{4,5},{5,4},{6,7},{7,6},{8,9},{9,8},{10,11... | collective-permute-start | bytes 1179656 | tf_op jit(solution)/shard_map/ppermute | solution.py:71
  149.2 0.7 fusion.14
  150.0 3.5 %collective-permute-done.5 = f32[128,768]{1,0:T(8,128)S(1)} collective-permute-done((f32[128,768]{1,0:T(8,128)S(1)}, f32[128,768]{1,0:T(8,128)S(1)}, u32[]{:S(2)}, u32[]{:S(2)}) %collective-permute-start.5) | collective-permute-done | bytes 393248 | tf_op jit(solution)/shard_map/ppermute | solution.py:71
  153.5 0.7 fusion.8
  (19 shorter events, 2.2 us)
Async XLA Ops:
  6.5 86.9 %all-gather.2.cloned.1.call-start = ((), (), s32[]{:S(2)}) async-start(), calls=%async_computation | async-start | bytes 4456448 | tf_op jit(solution)/shard_map/all_gather | solution.py:38
  12.2 22.7 %collective-permute-start = (bf16[4,128,768]{2,1,0:T(8,128)(2,1)S(1)}, bf16[4,128,768]{2,1,0:T(8,128)(2,1)S(1)}, u32[]{:S(2)}, u32[]{:S(2)}) collective-permute-start(bf16[4,128,768]{2,1,0:T(8,128)(2,1)S(1)} %bitcast_multiply_fusion), channel_id=1, source_target_pairs={{0,16},{8,24},{16,0},{24,8},{1,17},{9,25},{17,1},{25,9},{2,18},{10... | collective-permute-start | bytes 2359304 | tf_op jit(solution)/shard_map/ppermute | solution.py:11
  35.0 63.7 %collective-permute-start.1 = (bf16[8,128,768]{2,1,0:T(8,128)(2,1)S(1)}, bf16[8,128,768]{2,1,0:T(8,128)(2,1)}, u32[]{:S(2)}, u32[]{:S(2)}) collective-permute-start(bf16[8,128,768]{2,1,0:T(8,128)(2,1)S(1)} %pad_maximum_fusion.1), channel_id=1, source_target_pairs={{0,8},{8,0},{16,24},{24,16},{1,9},{9,1},{17,25},{25,17},{2,10},{10... | collective-permute-start | bytes 4718600 | tf_op jit(solution)/shard_map/ppermute | solution.py:11
  98.7 7.2 %copy-start = (bf16[4,4,1024,128]{3,2,1,0:T(8,128)(2,1)S(1)}, bf16[4,4,1024,128]{3,2,1,0:T(8,128)(2,1)}, u32[]{:S(2)}) copy-start(bf16[4,4,1024,128]{3,2,1,0:T(8,128)(2,1)} %gather_fusion.1) | copy-start | bytes 12582916
  102.4 29.3 %collective-permute-start.2 = (f32[256,768]{1,0:T(8,128)}, f32[256,768]{1,0:T(8,128)S(1)}, u32[]{:S(2)}, u32[]{:S(2)}) collective-permute-start(f32[256,768]{1,0:T(8,128)} %convolution_bitcast_fusion.2), channel_id=1, source_target_pairs={{0,2},{1,3},{2,4},{3,5},{4,6},{5,7},{6,0},{7,1},{8,10},{9,11},{10,... | collective-permute-start | bytes 2359304 | tf_op jit(solution)/shard_map/ppermute | solution.py:66
  109.2 23.0 %collective-permute-start.3 = (f32[256,768]{1,0:T(8,128)}, f32[256,768]{1,0:T(8,128)S(1)}, u32[]{:S(2)}, u32[]{:S(2)}) collective-permute-start(f32[256,768]{1,0:T(8,128)} %convolution_bitcast_fusion.1), channel_id=1, source_target_pairs={{0,4},{1,5},{2,6},{3,7},{4,0},{5,1},{6,2},{7,3},{8,12},{9,13},{10,... | collective-permute-start | bytes 2359304 | tf_op jit(solution)/shard_map/ppermute | solution.py:66
  115.6 25.0 %collective-permute-start.4 = (f32[256,768]{1,0:T(8,128)}, f32[256,768]{1,0:T(8,128)}, u32[]{:S(2)}, u32[]{:S(2)}) collective-permute-start(f32[256,768]{1,0:T(8,128)} %convolution_bitcast_fusion), channel_id=1, source_target_pairs={{0,6},{1,7},{2,0},{3,1},{4,2},{5,3},{6,4},{7,5},{8,14},{9,15},{10,... | collective-permute-start | bytes 2359304 | tf_op jit(solution)/shard_map/ppermute | solution.py:66
  119.6 27.1 %copy-start.1 = (s32[1,8]{1,0:T(1,128)S(1)}, s32[1,8]{1,0:T(1,128)}, u32[]{:S(2)}) copy-start(s32[1,8]{1,0:T(1,128)} %param.11) | copy-start | bytes 100
  132.3 0.9 copy-start.2
  143.9 9.7 %collective-permute-start.5 = (f32[128,768]{1,0:T(8,128)S(1)}, f32[128,768]{1,0:T(8,128)S(1)}, u32[]{:S(2)}, u32[]{:S(2)}) collective-permute-start(f32[128,768]{1,0:T(8,128)S(1)} %dynamic-slice_bitcast_fusion), channel_id=1, source_target_pairs={{0,1},{1,0},{2,3},{3,2},{4,5},{5,4},{6,7},{7,6},{8,9},{9,8},{10,11... | collective-permute-start | bytes 1179656 | tf_op jit(solution)/shard_map/ppermute | solution.py:71
Sparse Core Ops, SparseCore 0:
  10.3 83.0 all-gather.1

commit v4 on v2

--- a/solution.py
+++ b/solution.py
@@ -17,13 +17,16 @@
     sign_inner = sign_mask.shape[2]
     col_blocks = sign_mask.shape[3]
     col_count = lax.axis_size("col")
+    depth_count = lax.axis_size("depth")
+    pair_count = 2
+    ring_count = depth_count // pair_count
     local_order = row_order[0]
     ks_panel = (
         ks_matrix.reshape(row_blocks, BS, inner_blocks, BS)
         * ks_mask.astype(jnp.bfloat16)[:, None, :, None]
     )
     ks_panel = jnp.take(ks_panel, local_order, axis=0, mode="clip")
-    ks_panel = ks_panel.reshape(row_blocks * BS, inner_blocks * BS)
+    ks_halves = ks_panel.reshape(ring_count, pair_count, BS, inner_blocks * BS)
     sign_kept = sign_matrix.reshape(local_groups, sign_inner, BS, col_blocks, BS)
     sign_kept = sign_kept * sign_mask.astype(jnp.bfloat16).reshape(
         local_groups, sign_inner, 1, col_blocks, 1
@@ -35,21 +38,38 @@
     sign_four = jnp.concatenate([pair, near], axis=0)
     me = lax.axis_index("col")
     held_cols = jnp.stack([me, me ^ 2, me ^ 1, me ^ 3])
-    ks_whole = lax.all_gather(ks_panel, "row", axis=0, tiled=False)
-    ks_whole = ks_whole.reshape(
-        col_count, local_groups, row_blocks * BS, inner_blocks * BS
-    )
-    ks_matched = jnp.take(ks_whole, held_cols, axis=0, mode="clip")
-    ks_matched = ks_matched.reshape(
-        col_count * local_groups, row_blocks * BS, inner_blocks * BS
-    )
-    product = jnp.einsum(
-        "sik,skn->in", ks_matched, sign_four, preferred_element_type=jnp.float32
-    )
-    summed = lax.psum_scatter(product, "depth", scatter_dimension=0, tiled=True)
-    own_row = lax.dynamic_index_in_dim(
-        local_order, lax.axis_index("depth"), 0, keepdims=False
-    )
+    depth_me = lax.axis_index("depth")
+    ring_me = depth_me // pair_count
+    pair_me = depth_me % pair_count
+
+    results = []
+    for owner_pair in range(pair_count):
+        half = ks_halves[:, owner_pair].reshape(ring_count * BS, inner_blocks * BS)
+        ks_whole = lax.all_gather(half, "row", axis=0, tiled=False)
+        ks_whole = ks_whole.reshape(col_count, local_groups, ring_count * BS, inner_blocks * BS)
+        ks_matched = jnp.take(ks_whole, held_cols, axis=0, mode="clip")
+        ks_matched = ks_matched.reshape(
+            col_count * local_groups, ring_count, BS, inner_blocks * BS
+        )
+
+        def piece_for(ring_spot):
+            rows = lax.dynamic_index_in_dim(ks_matched, ring_spot, 1, keepdims=False)
+            return jnp.einsum(
+                "sik,skn->in", rows, sign_four, preferred_element_type=jnp.float32
+            )
+
+        total = piece_for(ring_me)
+        for shift in range(1, ring_count):
+            piece = piece_for((ring_me + shift) % ring_count)
+            route = [
+                (d, ((d // pair_count + shift) % ring_count) * pair_count + d % pair_count)
+                for d in range(depth_count)
+            ]
+            total = total + lax.ppermute(piece, "depth", route)
+        route = [(d, d ^ 1) for d in range(depth_count) if d % pair_count != owner_pair]
+        results.append(total + lax.ppermute(total, "depth", route))
+    summed = jnp.where(pair_me == 0, results[0], results[1])
+    own_row = lax.dynamic_index_in_dim(local_order, depth_me, 0, keepdims=False)
     own_mask = lax.dynamic_index_in_dim(product_mask, own_row, 0, keepdims=False)
     kept = summed.reshape(BS, col_blocks, BS) * own_mask.astype(jnp.float32)[None, :, None]
     return kept.reshape(BS, col_blocks * BS).astype(jnp.bfloat16)

time: 191 us -> 212 us (1.11)
  the two profiles are of different devices: /device:TPU:1 before, /device:TPU:2 now
where the time goes in v4:
time: 212 us; the launch traced here: 211 us
  waiting for transfers between devices  125 us (59%)
  starting transfers between devices  32.4 us (15%)
  matrix products  22.7 us (11%)
  between operations  15.7 us (7%)
  local copies, waits for them, and re-layouts  9.3 us (4%)
  other arithmetic  6.05 us (3%)
    all_gather x2, waiting for transfers between devices, per_device(): ks_whole = lax.all_gather(half, 'row', axis=0, tiled=False)  98.9 us
    dot_general x8, matrix products, piece_for(): jnp.einsum('sik,skn->in', rows, sign_four, preferred_element_type=jnp.flo...  22.7 us
    ppermute x6, starting transfers between devices, per_device(): total = total + lax.ppermute(piece, 'depth', route)  22.6 us
    ppermute x2, waiting for transfers between devices, swap_with(): return lax.ppermute(block, axis, [(i, i ^ flip) for i in devices])  18.6 us
    gather x2, local copies, waits for them, and re-layouts, per_device(): ks_matched = jnp.take(ks_whole, held_cols, axis=0, mode='clip')  6.33 us
    ppermute x2, starting transfers between devices, swap_with(): return lax.ppermute(block, axis, [(i, i ^ flip) for i in devices])  5.94 us
    ppermute x2, waiting for transfers between devices, per_device(): results.append(total + lax.ppermute(total, 'depth', route))  5.04 us
  transfers between devices with their start and end apart: 12, of which 5 were waited for; matrix products, arithmetic and copies ran while one was open for 15% of the time, Pallas kernels for 0%

profile of v4, /device:TPU:2, one launch (start us, length us, event | category | flops | bytes accessed | tf_op | source)
XLA Modules:
  0.0 210.9 jit_solution(7897830152322649062)
XLA Ops:
  11.9 4.0 %collective-permute-start = (bf16[4,128,768]{2,1,0:T(8,128)(2,1)S(1)}, bf16[4,128,768]{2,1,0:T(8,128)(2,1)S(1)}, u32[]{:S(2)}, u32[]{:S(2)}) collective-permute-start(bf16[4,128,768]{2,1,0:T(8,128)(2,1)S(1)} %bitcast_multiply_fusion), channel_id=1, source_target_pairs={{0,16},{8,24},{16,0},{24,8},{1,17},{9,25},{17,1},{25,9},{2,18},{10... | collective-permute-start | bytes 2359304 | tf_op jit(solution)/shard_map/ppermute | solution.py:11
  16.0 18.6 %collective-permute-done = bf16[4,128,768]{2,1,0:T(8,128)(2,1)S(1)} collective-permute-done((bf16[4,128,768]{2,1,0:T(8,128)(2,1)S(1)}, bf16[4,128,768]{2,1,0:T(8,128)(2,1)S(1)}, u32[]{:S(2)}, u32[]{:S(2)}) %collective-permute-start) | collective-permute-done | bytes 786464 | tf_op jit(solution)/shard_map/ppermute | solution.py:11
  36.8 1.9 collective-permute-start.1
  38.9 49.5 %all-gather.3.cloned.1.call-done = bf16[16,512,128]{2,1,0:T(8,128)(2,1)} async-done(((bf16[1,512,128]{2,1,0:T(8,128)(2,1)}), bf16[16,512,128]{2,1,0:T(8,128)(2,1)}) %all-gather.3.cloned.1.call-update) | async-done | bytes 2097168 | tf_op jit(solution)/shard_map/all_gather | solution.py:48
  88.4 2.5 %gather_fusion.1 = bf16[4,4,512,128]{3,2,1,0:T(8,128)(2,1)S(1)} fusion(bf16[4,4,512,128]{3,2,1,0:T(8,128)(2,1)} %bitcast.85, s32[1024]{0:T(1024)S(1)} %pad_clamp_fusion), kind=kCustom, calls=%fused_computation.1 | custom fusion | bytes 4194320 | tf_op jit(solution)/shard_map/jit(_take)/gather | solution.py:50
  91.0 3.1 %convolution_bitcast_fusion.6 = f32[128,768]{1,0:T(8,128)} fusion(bf16[16,4,128,128]{3,2,1,0:T(8,128)(2,1)S(1)} %bitcast.86, s32[]{:T(128)S(6)} %select_n.67, bf16[8,128,768]{2,1,0:T(8,128)(2,1)} %collective-permute-done.1, bf16[4,128,768]{2,1,0:T(8,128)(2,1)} %copy-done.2, bf16[4,128,768]{2,1,0:T(8,128)(2,1)S(1)} %bitcast_multiply_fusion), kind=kOutput, calls=%fused_computation.11 | convolution fusion | flops 405798912 | bytes 4063236 | tf_op jit(solution)/shard_map/sik,skn->in/dot_general | solution.py:57
  94.1 3.3 %collective-permute-start.2 = (f32[128,768]{1,0:T(8,128)}, f32[128,768]{1,0:T(8,128)S(1)}, u32[]{:S(2)}, u32[]{:S(2)}) collective-permute-start(f32[128,768]{1,0:T(8,128)} %convolution_bitcast_fusion.6), channel_id=1, source_target_pairs={{0,2},{1,3},{2,4},{3,5},{4,6},{5,7},{6,0},{7,1},{8,10},{9,11},{10,... | collective-permute-start | bytes 1179656 | tf_op jit(solution)/shard_map/ppermute | solution.py:68
  97.4 2.8 %convolution_bitcast_fusion.5 = f32[128,768]{1,0:T(8,128)} fusion(bf16[16,4,128,128]{3,2,1,0:T(8,128)(2,1)S(1)} %bitcast.87, s32[]{:T(128)S(6)} %select_n.69, bf16[8,128,768]{2,1,0:T(8,128)(2,1)} %collective-permute-done.1, bf16[4,128,768]{2,1,0:T(8,128)(2,1)S(1)} %copy-done.3, bf16[4,128,768]{2,1,0:T(8,128)(2,1)S(1)} %bitcast_multiply_fusion), kind=kOutput, calls=%fused_computation.10 | convolution fusion | flops 405798912 | bytes 4063236 | tf_op jit(solution)/shard_map/sik,skn->in/dot_general | solution.py:57
  100.1 4.7 %collective-permute-start.3 = (f32[128,768]{1,0:T(8,128)}, f32[128,768]{1,0:T(8,128)}, u32[]{:S(2)}, u32[]{:S(2)}) collective-permute-start(f32[128,768]{1,0:T(8,128)} %convolution_bitcast_fusion.5), channel_id=1, source_target_pairs={{0,4},{1,5},{2,6},{3,7},{4,0},{5,1},{6,2},{7,3},{8,12},{9,13},{10,... | collective-permute-start | bytes 1179656 | tf_op jit(solution)/shard_map/ppermute | solution.py:68
  104.9 2.8 %convolution_bitcast_fusion.4 = f32[128,768]{1,0:T(8,128)} fusion(bf16[16,4,128,128]{3,2,1,0:T(8,128)(2,1)S(1)} %bitcast.88, s32[]{:T(128)S(6)} %select_n.71, bf16[8,128,768]{2,1,0:T(8,128)(2,1)} %collective-permute-done.1, bf16[4,128,768]{2,1,0:T(8,128)(2,1)S(1)} %copy-done.3, bf16[4,128,768]{2,1,0:T(8,128)(2,1)S(1)} %bitcast_multiply_fusion), kind=kOutput, calls=%fused_computation.9 | convolution fusion | flops 405798912 | bytes 4063236 | tf_op jit(solution)/shard_map/sik,skn->in/dot_general | solution.py:57
  107.7 3.3 %collective-permute-start.4 = (f32[128,768]{1,0:T(8,128)}, f32[128,768]{1,0:T(8,128)}, u32[]{:S(2)}, u32[]{:S(2)}) collective-permute-start(f32[128,768]{1,0:T(8,128)} %convolution_bitcast_fusion.4), channel_id=1, source_target_pairs={{0,6},{1,7},{2,0},{3,1},{4,2},{5,3},{6,4},{7,5},{8,14},{9,15},{10,... | collective-permute-start | bytes 1179656 | tf_op jit(solution)/shard_map/ppermute | solution.py:68
  111.0 49.4 %all-gather.5.cloned.1.call-done = bf16[16,512,128]{2,1,0:T(8,128)(2,1)} async-done(((bf16[1,512,128]{2,1,0:T(8,128)(2,1)}), bf16[16,512,128]{2,1,0:T(8,128)(2,1)}) %all-gather.5.cloned.1.call-update) | async-done | bytes 2097168 | tf_op jit(solution)/shard_map/all_gather | solution.py:48
  160.4 3.8 %gather_fusion.2 = bf16[4,4,512,128]{3,2,1,0:T(8,128)(2,1)} fusion(bf16[4,4,512,128]{3,2,1,0:T(8,128)(2,1)} %bitcast.84, s32[1024]{0:T(1024)S(1)} %pad_clamp_fusion), kind=kCustom, calls=%fused_computation.2 | custom fusion | bytes 4194320 | tf_op jit(solution)/shard_map/jit(_take)/gather | solution.py:50
  164.2 3.3 %convolution_bitcast_fusion.2 = f32[128,768]{1,0:T(8,128)} fusion(bf16[16,4,128,128]{3,2,1,0:T(8,128)(2,1)} %bitcast.90, s32[]{:T(128)S(6)} %select_n.67, bf16[8,128,768]{2,1,0:T(8,128)(2,1)} %collective-permute-done.1, bf16[4,128,768]{2,1,0:T(8,128)(2,1)} %copy-done.2, bf16[4,128,768]{2,1,0:T(8,128)(2,1)S(1)} %bitcast_multiply_fusion), kind=kOutput, calls=%fused_computation.7 | convolution fusion | flops 405798912 | bytes 4063236 | tf_op jit(solution)/shard_map/sik,skn->in/dot_general | solution.py:57
  167.4 3.3 %collective-permute-start.6 = (f32[128,768]{1,0:T(8,128)}, f32[128,768]{1,0:T(8,128)}, u32[]{:S(2)}, u32[]{:S(2)}) collective-permute-start(f32[128,768]{1,0:T(8,128)} %convolution_bitcast_fusion.2), channel_id=1, source_target_pairs={{0,2},{1,3},{2,4},{3,5},{4,6},{5,7},{6,0},{7,1},{8,10},{9,11},{10,... | collective-permute-start | bytes 1179656 | tf_op jit(solution)/shard_map/ppermute | solution.py:68
  170.8 2.8 %convolution_bitcast_fusion.1 = f32[128,768]{1,0:T(8,128)} fusion(bf16[16,4,128,128]{3,2,1,0:T(8,128)(2,1)S(1)} %bitcast.92, s32[]{:T(128)S(6)} %select_n.69, bf16[8,128,768]{2,1,0:T(8,128)(2,1)} %collective-permute-done.1, bf16[4,128,768]{2,1,0:T(8,128)(2,1)S(1)} %copy-done.4, bf16[4,128,768]{2,1,0:T(8,128)(2,1)S(1)} %bitcast_multiply_fusion), kind=kOutput, calls=%fused_computation.6 | convolution fusion | flops 405798912 | bytes 4063236 | tf_op jit(solution)/shard_map/sik,skn->in/dot_general | solution.py:57
  173.6 4.7 %collective-permute-start.7 = (f32[128,768]{1,0:T(8,128)}, f32[128,768]{1,0:T(8,128)}, u32[]{:S(2)}, u32[]{:S(2)}) collective-permute-start(f32[128,768]{1,0:T(8,128)} %convolution_bitcast_fusion.1), channel_id=1, source_target_pairs={{0,4},{1,5},{2,6},{3,7},{4,0},{5,1},{6,2},{7,3},{8,12},{9,13},{10,... | collective-permute-start | bytes 1179656 | tf_op jit(solution)/shard_map/ppermute | solution.py:68
  178.3 2.9 %convolution_bitcast_fusion = f32[128,768]{1,0:T(8,128)} fusion(bf16[16,4,128,128]{3,2,1,0:T(8,128)(2,1)S(1)} %bitcast.93, s32[]{:T(128)S(6)} %select_n.71, bf16[8,128,768]{2,1,0:T(8,128)(2,1)} %collective-permute-done.1, bf16[4,128,768]{2,1,0:T(8,128)(2,1)S(1)} %copy-done.4, bf16[4,128,768]{2,1,0:T(8,128)(2,1)S(1)} %bitcast_multiply_fusion), kind=kOutput, calls=%fused_computation.5 | convolution fusion | flops 405798912 | bytes 4063236 | tf_op jit(solution)/shard_map/sik,skn->in/dot_general | solution.py:57
  181.2 3.3 %collective-permute-start.8 = (f32[128,768]{1,0:T(8,128)}, f32[128,768]{1,0:T(8,128)}, u32[]{:S(2)}, u32[]{:S(2)}) collective-permute-start(f32[128,768]{1,0:T(8,128)} %convolution_bitcast_fusion), channel_id=1, source_target_pairs={{0,6},{1,7},{2,0},{3,1},{4,2},{5,3},{6,4},{7,5},{8,14},{9,15},{10,... | collective-permute-start | bytes 1179656 | tf_op jit(solution)/shard_map/ppermute | solution.py:68
  184.5 2.6 %fusion.2 = f32[128,768]{1,0:T(8,128)S(1)} fusion(f32[128,768]{1,0:T(8,128)} %collective-permute-done.4, f32[128,768]{1,0:T(8,128)} %collective-permute-done.3, f32[128,768]{1,0:T(8,128)} %copy-done.7, bf16[16,4,128,128]{3,2,1,0:T(8,128)(2,1)S(1)} %bitcast.89, s32[]{:T(128)S(6)} %select_n.65, bf16[8,128,768]{2,1,0:T(8,128)(2,1)} %collective-permute-done.1, ...), kind=kOutput, calls=%fused_computation.15 | convolution fusion | flops 406093824 | bytes 5242884 | tf_op jit(solution)/shard_map/sik,skn->in/dot_general | solution.py:57
  187.2 2.5 %collective-permute-start.5 = (f32[128,768]{1,0:T(8,128)S(1)}, f32[128,768]{1,0:T(8,128)S(1)}, u32[]{:S(2)}, u32[]{:S(2)}) collective-permute-start(f32[128,768]{1,0:T(8,128)S(1)} %fusion.2), channel_id=1, source_target_pairs={{1,0},{3,2},{5,4},{7,6},{9,8},{11,10},{13,12},{15,14},{17,16},{19,... | collective-permute-start | bytes 1179656 | tf_op jit(solution)/shard_map/ppermute | solution.py:70
  189.7 1.5 collective-permute-done.8
  191.1 2.5 %fusion.5 = f32[128,768]{1,0:T(8,128)S(1)} fusion(f32[128,768]{1,0:T(8,128)} %collective-permute-done.8, f32[128,768]{1,0:T(8,128)} %collective-permute-done.7, f32[128,768]{1,0:T(8,128)} %collective-permute-done.6, bf16[16,4,128,128]{3,2,1,0:T(8,128)(2,1)} %bitcast.91, s32[]{:T(128)S(6)} %select_n.65, bf16[8,128,768]{2,1,0:T(8,128)(2,1)} %collective-permute-done.1, ...), kind=kOutput, calls=%fused_computation.18 | convolution fusion | flops 406093824 | bytes 5242884 | tf_op jit(solution)/shard_map/sik,skn->in/dot_general | solution.py:57
  198.3 5.0 %collective-permute-done.9 = f32[128,768]{1,0:T(8,128)S(1)} collective-permute-done((f32[128,768]{1,0:T(8,128)S(1)}, f32[128,768]{1,0:T(8,128)S(1)}, u32[]{:S(2)}, u32[]{:S(2)}) %collective-permute-start.9) | collective-permute-done | bytes 393248 | tf_op jit(solution)/shard_map/ppermute | solution.py:70
  (45 shorter events, 11.1 us)
Async XLA Ops:
  6.5 5.3 %copy-start.1 = (bf16[4,1,128,768]{3,2,1,0:T(8,128)(2,1)S(1)}, bf16[4,1,128,768]{3,2,1,0:T(8,128)(2,1)}, u32[]{:S(2)}) copy-start(bf16[4,1,128,768]{3,2,1,0:T(8,128)(2,1)} %param.7) | copy-start | bytes 2359300
  6.5 81.9 %all-gather.3.cloned.1.call-start = ((), (), s32[]{:S(2)}) async-start(), calls=%async_computation | async-start | bytes 2228224 | tf_op jit(solution)/shard_map/all_gather | solution.py:48
  10.3 150.1 %all-gather.5.cloned.1.call-start = ((), (), s32[]{:S(2)}) async-start(), calls=%async_computation.1 | async-start | bytes 2228224 | tf_op jit(solution)/shard_map/all_gather | solution.py:48
  11.9 22.7 %collective-permute-start = (bf16[4,128,768]{2,1,0:T(8,128)(2,1)S(1)}, bf16[4,128,768]{2,1,0:T(8,128)(2,1)S(1)}, u32[]{:S(2)}, u32[]{:S(2)}) collective-permute-start(bf16[4,128,768]{2,1,0:T(8,128)(2,1)S(1)} %bitcast_multiply_fusion), channel_id=1, source_target_pairs={{0,16},{8,24},{16,0},{24,8},{1,17},{9,25},{17,1},{25,9},{2,18},{10... | collective-permute-start | bytes 2359304 | tf_op jit(solution)/shard_map/ppermute | solution.py:11
  34.6 0.9 copy-start.2
  36.8 54.2 %collective-permute-start.1 = (bf16[8,128,768]{2,1,0:T(8,128)(2,1)}, bf16[8,128,768]{2,1,0:T(8,128)(2,1)}, u32[]{:S(2)}, u32[]{:S(2)}) collective-permute-start(bf16[8,128,768]{2,1,0:T(8,128)(2,1)} %pad_maximum_fusion.1), channel_id=1, source_target_pairs={{0,8},{8,0},{16,24},{24,16},{1,9},{9,1},{17,25},{25,17},{2,10},{10... | collective-permute-start | bytes 4718600 | tf_op jit(solution)/shard_map/ppermute | solution.py:11
  91.0 6.4 %copy-start.3 = (bf16[4,128,768]{2,1,0:T(8,128)(2,1)S(1)}, bf16[4,128,768]{2,1,0:T(8,128)(2,1)}, u32[]{:S(2)}) copy-start(bf16[4,128,768]{2,1,0:T(8,128)(2,1)} %copy-done.2) | copy-start | bytes 2359300
  94.1 87.1 %collective-permute-start.2 = (f32[128,768]{1,0:T(8,128)}, f32[128,768]{1,0:T(8,128)S(1)}, u32[]{:S(2)}, u32[]{:S(2)}) collective-permute-start(f32[128,768]{1,0:T(8,128)} %convolution_bitcast_fusion.6), channel_id=1, source_target_pairs={{0,2},{1,3},{2,4},{3,5},{4,6},{5,7},{6,0},{7,1},{8,10},{9,11},{10,... | collective-permute-start | bytes 1179656 | tf_op jit(solution)/shard_map/ppermute | solution.py:68
  100.1 84.3 %collective-permute-start.3 = (f32[128,768]{1,0:T(8,128)}, f32[128,768]{1,0:T(8,128)}, u32[]{:S(2)}, u32[]{:S(2)}) collective-permute-start(f32[128,768]{1,0:T(8,128)} %convolution_bitcast_fusion.5), channel_id=1, source_target_pairs={{0,4},{1,5},{2,6},{3,7},{4,0},{5,1},{6,2},{7,3},{8,12},{9,13},{10,... | collective-permute-start | bytes 1179656 | tf_op jit(solution)/shard_map/ppermute | solution.py:68
  107.7 76.8 %collective-permute-start.4 = (f32[128,768]{1,0:T(8,128)}, f32[128,768]{1,0:T(8,128)}, u32[]{:S(2)}, u32[]{:S(2)}) collective-permute-start(f32[128,768]{1,0:T(8,128)} %convolution_bitcast_fusion.4), channel_id=1, source_target_pairs={{0,6},{1,7},{2,0},{3,1},{4,2},{5,3},{6,4},{7,5},{8,14},{9,15},{10,... | collective-permute-start | bytes 1179656 | tf_op jit(solution)/shard_map/ppermute | solution.py:68
  164.2 6.6 %copy-start = (bf16[4,4,512,128]{3,2,1,0:T(8,128)(2,1)S(1)}, bf16[4,4,512,128]{3,2,1,0:T(8,128)(2,1)}, u32[]{:S(2)}) copy-start(bf16[4,4,512,128]{3,2,1,0:T(8,128)(2,1)} %gather_fusion.2) | copy-start | bytes 6291460
  164.2 6.6 %copy-start.4 = (bf16[4,128,768]{2,1,0:T(8,128)(2,1)S(1)}, bf16[4,128,768]{2,1,0:T(8,128)(2,1)}, u32[]{:S(2)}) copy-start(bf16[4,128,768]{2,1,0:T(8,128)(2,1)} %copy-done.2) | copy-start | bytes 2359300
  167.4 22.2 %collective-permute-start.6 = (f32[128,768]{1,0:T(8,128)}, f32[128,768]{1,0:T(8,128)}, u32[]{:S(2)}, u32[]{:S(2)}) collective-permute-start(f32[128,768]{1,0:T(8,128)} %convolution_bitcast_fusion.2), channel_id=1, source_target_pairs={{0,2},{1,3},{2,4},{3,5},{4,6},{5,7},{6,0},{7,1},{8,10},{9,11},{10,... | collective-permute-start | bytes 1179656 | tf_op jit(solution)/shard_map/ppermute | solution.py:68
  173.6 16.0 %collective-permute-start.7 = (f32[128,768]{1,0:T(8,128)}, f32[128,768]{1,0:T(8,128)}, u32[]{:S(2)}, u32[]{:S(2)}) collective-permute-start(f32[128,768]{1,0:T(8,128)} %convolution_bitcast_fusion.1), channel_id=1, source_target_pairs={{0,4},{1,5},{2,6},{3,7},{4,0},{5,1},{6,2},{7,3},{8,12},{9,13},{10,... | collective-permute-start | bytes 1179656 | tf_op jit(solution)/shard_map/ppermute | solution.py:68
  181.2 3.3 %copy-start.7 = (f32[128,768]{1,0:T(8,128)}, f32[128,768]{1,0:T(8,128)S(1)}, u32[]{:S(2)}) copy-start(f32[128,768]{1,0:T(8,128)S(1)} %collective-permute-done.2) | copy-start | bytes 1179652
  181.2 10.0 %collective-permute-start.8 = (f32[128,768]{1,0:T(8,128)}, f32[128,768]{1,0:T(8,128)}, u32[]{:S(2)}, u32[]{:S(2)}) collective-permute-start(f32[128,768]{1,0:T(8,128)} %convolution_bitcast_fusion), channel_id=1, source_target_pairs={{0,6},{1,7},{2,0},{3,1},{4,2},{5,3},{6,4},{7,5},{8,14},{9,15},{10,... | collective-permute-start | bytes 1179656 | tf_op jit(solution)/shard_map/ppermute | solution.py:68
  184.5 6.7 %copy-start.5 = (bf16[4,128,768]{2,1,0:T(8,128)(2,1)S(1)}, bf16[4,128,768]{2,1,0:T(8,128)(2,1)}, u32[]{:S(2)}) copy-start(bf16[4,128,768]{2,1,0:T(8,128)(2,1)} %copy-done.2) | copy-start | bytes 2359300
  187.1 7.8 %copy-start.6 = (s32[1,8]{1,0:T(1,128)S(1)}, s32[1,8]{1,0:T(1,128)}, u32[]{:S(2)}) copy-start(s32[1,8]{1,0:T(1,128)} %param.11) | copy-start | bytes 100
  187.2 11.1 %collective-permute-start.5 = (f32[128,768]{1,0:T(8,128)S(1)}, f32[128,768]{1,0:T(8,128)S(1)}, u32[]{:S(2)}, u32[]{:S(2)}) collective-permute-start(f32[128,768]{1,0:T(8,128)S(1)} %fusion.2), channel_id=1, source_target_pairs={{1,0},{3,2},{5,4},{7,6},{9,8},{11,10},{13,12},{15,14},{17,16},{19,... | collective-permute-start | bytes 1179656 | tf_op jit(solution)/shard_map/ppermute | solution.py:70
  193.7 9.7 %collective-permute-start.9 = (f32[128,768]{1,0:T(8,128)S(1)}, f32[128,768]{1,0:T(8,128)S(1)}, u32[]{:S(2)}, u32[]{:S(2)}) collective-permute-start(f32[128,768]{1,0:T(8,128)S(1)} %fusion.5), channel_id=1, source_target_pairs={{0,1},{2,3},{4,5},{6,7},{8,9},{10,11},{12,13},{14,15},{16,17},{18,... | collective-permute-start | bytes 1179656 | tf_op jit(solution)/shard_map/ppermute | solution.py:70
Sparse Core Ops, SparseCore 0:
  10.4 77.9 all-gather.2
  90.5 69.8 all-gather.4

commit v5 on v3

--- a/solution.py
+++ b/solution.py
@@ -16,7 +16,6 @@
     local_groups = sign_mask.shape[0]
     sign_inner = sign_mask.shape[2]
     col_blocks = sign_mask.shape[3]
-    col_count = lax.axis_size("col")
     local_order = row_order[0]
     ks_panel = (
         ks_matrix.reshape(row_blocks, BS, inner_blocks, BS)
@@ -33,16 +32,28 @@
     pair = jnp.concatenate([sign_kept, far], axis=0)
     near = swap_with(pair, "col", 1)
     sign_four = jnp.concatenate([pair, near], axis=0)
+    row_count = lax.axis_size("row")
+    row_me = lax.axis_index("row")
+    rightward = [(i, (i + 1) % row_count) for i in range(row_count)]
+    leftward = [(i, (i - 1) % row_count) for i in range(row_count)]
+    going_right = ks_panel
+    going_left = ks_panel
+    panels = [ks_panel]
+    offsets = [0]
+    for step in range(1, row_count // 2 + 1):
+        going_right = lax.ppermute(going_right, "row", rightward)
+        panels.append(going_right)
+        offsets.append(-step)
+        if step < row_count - step:
+            going_left = lax.ppermute(going_left, "row", leftward)
+            panels.append(going_left)
+            offsets.append(step)
+    ks_matched = jnp.stack(panels)
     me = lax.axis_index("col")
-    held_cols = jnp.stack([me, me ^ 2, me ^ 1, me ^ 3])
-    ks_whole = lax.all_gather(ks_panel, "row", axis=0, tiled=False)
-    ks_whole = ks_whole.reshape(
-        col_count, local_groups, row_blocks * BS, inner_blocks * BS
-    )
-    ks_matched = jnp.take(ks_whole, held_cols, axis=0, mode="clip")
-    ks_matched = ks_matched.reshape(
-        col_count * local_groups, row_blocks * BS, inner_blocks * BS
-    )
+    inner_of = (row_me + jnp.array(offsets, jnp.int32)) % row_count
+    flipped = (inner_of // local_groups) ^ me
+    spot = (flipped % 2) * 2 + flipped // 2
+    sign_four = jnp.take(sign_four, spot * local_groups + inner_of % local_groups, axis=0, mode="clip")
     depth_count = lax.axis_size("depth")
     pair_count = 2
     ring_count = depth_count // pair_count

time: 162 us -> 169 us (1.043)
  the two profiles are of different devices: /device:TPU:12 before, /device:TPU:8 now
where the time goes in v5:
time: 169 us; the launch traced here: 168 us
  starting transfers between devices  77.6 us (46%)
  waiting for transfers between devices  57.3 us (34%)
  matrix products  14.3 us (8%)
  other arithmetic  9.15 us (5%)
  local copies, waits for them, and re-layouts  7.3 us (4%)
  between operations  2.53 us (1%)
    ppermute x7, starting transfers between devices, per_device(): going_left = lax.ppermute(going_left, 'row', leftward)  40.3 us
    ppermute x3, waiting for transfers between devices, per_device(): total = total + lax.ppermute(piece, 'depth', route)  25.8 us
    ppermute x8, waiting for transfers between devices, per_device(): going_right = lax.ppermute(going_right, 'row', rightward)  24.4 us
    ppermute x8, starting transfers between devices, per_device(): going_right = lax.ppermute(going_right, 'row', rightward)  17.2 us
    dot_general x4, matrix products, piece_for(): jnp.einsum('sik,skn->in', rows, sign_four, preferred_element_type=jnp.flo...  14.3 us
    ppermute x3, starting transfers between devices, per_device(): total = total + lax.ppermute(piece, 'depth', route)  10.8 us
    ppermute x1, waiting for transfers between devices, per_device(): lax.ppermute(give, 'depth', [(d, d ^ 1) for d in range(depth_count)])  7.1 us
    ppermute x2, starting transfers between devices, swap_with(): return lax.ppermute(block, axis, [(i, i ^ flip) for i in devices])  6.85 us
  transfers between devices with their start and end apart: 21, of which 11 were waited for; matrix products, arithmetic and copies ran while one was open for 6% of the time, Pallas kernels for 0%

profile of v5, /device:TPU:8, one launch (start us, length us, event | category | flops | bytes accessed | tf_op | source)
XLA Modules:
  0.0 168.2 jit_solution(8411120704636343719)
XLA Ops:
  3.0 3.8 %collective-permute-start = (bf16[1024,128]{1,0:T(8,128)(2,1)S(1)}, bf16[1024,128]{1,0:T(8,128)(2,1)S(1)}, u32[]{:S(2)}, u32[]{:S(2)}) collective-permute-start(bf16[1024,128]{1,0:T(8,128)(2,1)S(1)} %bitcast.82), channel_id=1, source_target_pairs={{0,32},{32,64},{64,96},{96,128},{128,160},{160,192},{192,224},{224... | collective-permute-start | bytes 786440 | tf_op jit(solution)/shard_map/ppermute | solution.py:44
  6.8 9.5 %collective-permute-start.1 = (bf16[1024,128]{1,0:T(8,128)(2,1)S(1)}, bf16[1024,128]{1,0:T(8,128)(2,1)S(1)}, u32[]{:S(2)}, u32[]{:S(2)}) collective-permute-start(bf16[1024,128]{1,0:T(8,128)(2,1)S(1)} %bitcast.83), channel_id=1, source_target_pairs={{0,480},{32,0},{64,32},{96,64},{128,96},{160,128},{192,160},{224,1... | collective-permute-start | bytes 786440 | tf_op jit(solution)/shard_map/ppermute | solution.py:48
  18.3 4.9 %collective-permute-start.15 = (bf16[4,128,768]{2,1,0:T(8,128)(2,1)S(1)}, bf16[4,128,768]{2,1,0:T(8,128)(2,1)S(1)}, u32[]{:S(2)}, u32[]{:S(2)}) collective-permute-start(bf16[4,128,768]{2,1,0:T(8,128)(2,1)S(1)} %bitcast_multiply_fusion), channel_id=1, source_target_pairs={{0,16},{8,24},{16,0},{24,8},{1,17},{9,25},{17,1},{25,9},{2,18},{10... | collective-permute-start | bytes 2359304 | tf_op jit(solution)/shard_map/ppermute | solution.py:11
  26.0 5.1 %collective-permute-start.3 = (bf16[1024,128]{1,0:T(8,128)(2,1)S(1)}, bf16[1024,128]{1,0:T(8,128)(2,1)S(1)}, u32[]{:S(2)}, u32[]{:S(2)}) collective-permute-start(bf16[1024,128]{1,0:T(8,128)(2,1)S(1)} %collective-permute-done.1), channel_id=1, source_target_pairs={{0,480},{32,0},{64,32},{96,64},{128,96},{160,128},{192,160},{224,1... | collective-permute-start | bytes 786440 | tf_op jit(solution)/shard_map/ppermute | solution.py:48
  31.2 3.4 %collective-permute-done.2 = bf16[1024,128]{1,0:T(8,128)(2,1)S(1)} collective-permute-done((bf16[1024,128]{1,0:T(8,128)(2,1)S(1)}, bf16[1024,128]{1,0:T(8,128)(2,1)S(1)}, u32[]{:S(2)}, u32[]{:S(2)}) %collective-permute-start.2) | collective-permute-done | bytes 262176 | tf_op jit(solution)/shard_map/ppermute | solution.py:44
  36.6 5.1 %collective-permute-start.5 = (bf16[1024,128]{1,0:T(8,128)(2,1)S(1)}, bf16[1024,128]{1,0:T(8,128)(2,1)S(1)}, u32[]{:S(2)}, u32[]{:S(2)}) collective-permute-start(bf16[1024,128]{1,0:T(8,128)(2,1)S(1)} %collective-permute-done.3), channel_id=1, source_target_pairs={{0,480},{32,0},{64,32},{96,64},{128,96},{160,128},{192,160},{224,1... | collective-permute-start | bytes 786440 | tf_op jit(solution)/shard_map/ppermute | solution.py:48
  46.2 5.1 %collective-permute-start.7 = (bf16[1024,128]{1,0:T(8,128)(2,1)S(1)}, bf16[1024,128]{1,0:T(8,128)(2,1)S(1)}, u32[]{:S(2)}, u32[]{:S(2)}) collective-permute-start(bf16[1024,128]{1,0:T(8,128)(2,1)S(1)} %collective-permute-done.5), channel_id=1, source_target_pairs={{0,480},{32,0},{64,32},{96,64},{128,96},{160,128},{192,160},{224,1... | collective-permute-start | bytes 786440 | tf_op jit(solution)/shard_map/ppermute | solution.py:48
  55.7 5.1 %collective-permute-start.9 = (bf16[1024,128]{1,0:T(8,128)(2,1)S(1)}, bf16[1024,128]{1,0:T(8,128)(2,1)S(1)}, u32[]{:S(2)}, u32[]{:S(2)}) collective-permute-start(bf16[1024,128]{1,0:T(8,128)(2,1)S(1)} %collective-permute-done.7), channel_id=1, source_target_pairs={{0,480},{32,0},{64,32},{96,64},{128,96},{160,128},{192,160},{224,1... | collective-permute-start | bytes 786440 | tf_op jit(solution)/shard_map/ppermute | solution.py:48
  60.9 4.5 %collective-permute-done.8 = bf16[1024,128]{1,0:T(8,128)(2,1)S(1)} collective-permute-done((bf16[1024,128]{1,0:T(8,128)(2,1)S(1)}, bf16[1024,128]{1,0:T(8,128)(2,1)S(1)}, u32[]{:S(2)}, u32[]{:S(2)}) %collective-permute-start.8) | collective-permute-done | bytes 262176 | tf_op jit(solution)/shard_map/ppermute | solution.py:44
  67.4 5.1 %collective-permute-start.11 = (bf16[1024,128]{1,0:T(8,128)(2,1)S(1)}, bf16[1024,128]{1,0:T(8,128)(2,1)S(1)}, u32[]{:S(2)}, u32[]{:S(2)}) collective-permute-start(bf16[1024,128]{1,0:T(8,128)(2,1)S(1)} %collective-permute-done.9), channel_id=1, source_target_pairs={{0,480},{32,0},{64,32},{96,64},{128,96},{160,128},{192,160},{224,1... | collective-permute-start | bytes 786440 | tf_op jit(solution)/shard_map/ppermute | solution.py:48
  72.5 3.6 %collective-permute-done.10 = bf16[1024,128]{1,0:T(8,128)(2,1)S(1)} collective-permute-done((bf16[1024,128]{1,0:T(8,128)(2,1)S(1)}, bf16[1024,128]{1,0:T(8,128)(2,1)S(1)}, u32[]{:S(2)}, u32[]{:S(2)}) %collective-permute-start.10) | collective-permute-done | bytes 262176 | tf_op jit(solution)/shard_map/ppermute | solution.py:44
  78.1 5.1 %collective-permute-start.13 = (bf16[1024,128]{1,0:T(8,128)(2,1)S(1)}, bf16[1024,128]{1,0:T(8,128)(2,1)S(1)}, u32[]{:S(2)}, u32[]{:S(2)}) collective-permute-start(bf16[1024,128]{1,0:T(8,128)(2,1)S(1)} %collective-permute-done.11), channel_id=1, source_target_pairs={{0,480},{32,0},{64,32},{96,64},{128,96},{160,128},{192,160},{224,1... | collective-permute-start | bytes 786440 | tf_op jit(solution)/shard_map/ppermute | solution.py:48
  88.1 7.4 %collective-permute-done.14 = bf16[1024,128]{1,0:T(8,128)(2,1)S(1)} collective-permute-done((bf16[1024,128]{1,0:T(8,128)(2,1)S(1)}, bf16[1024,128]{1,0:T(8,128)(2,1)S(1)}, u32[]{:S(2)}, u32[]{:S(2)}) %collective-permute-start.14) | collective-permute-done | bytes 262176 | tf_op jit(solution)/shard_map/ppermute | solution.py:44
  101.6 4.3 %convolution_bitcast_fusion.2 = f32[256,768]{1,0:T(8,128)} fusion(bf16[16,128,768]{2,1,0:T(8,128)(2,1)} %gather_fusion.1, bf16[16,1024,128]{2,1,0:T(8,128)(2,1)} %copy-done.3, s32[]{:T(128)S(6)} %select_n.80), kind=kOutput, calls=%fused_computation.6 | convolution fusion | flops 805306368 | bytes 4980740 | tf_op jit(solution)/shard_map/sik,skn->in/dot_general | solution.py:66
  105.9 3.5 %collective-permute-start.17 = (f32[256,768]{1,0:T(8,128)}, f32[256,768]{1,0:T(8,128)}, u32[]{:S(2)}, u32[]{:S(2)}) collective-permute-start(f32[256,768]{1,0:T(8,128)} %convolution_bitcast_fusion.2), channel_id=1, source_target_pairs={{0,2},{1,3},{2,4},{3,5},{4,6},{5,7},{6,0},{7,1},{8,10},{9,11},{10,... | collective-permute-start | bytes 2359304 | tf_op jit(solution)/shard_map/ppermute | solution.py:77
  109.4 3.1 %convolution_bitcast_fusion.1 = f32[256,768]{1,0:T(8,128)} fusion(bf16[16,128,768]{2,1,0:T(8,128)(2,1)S(1)} %copy-done, bf16[16,1024,128]{2,1,0:T(8,128)(2,1)} %copy-done.3, s32[]{:T(128)S(6)} %select_n.82), kind=kOutput, calls=%fused_computation.5 | convolution fusion | flops 805306368 | bytes 4980740 | tf_op jit(solution)/shard_map/sik,skn->in/dot_general | solution.py:66
  112.5 2.8 %collective-permute-start.18 = (f32[256,768]{1,0:T(8,128)}, f32[256,768]{1,0:T(8,128)}, u32[]{:S(2)}, u32[]{:S(2)}) collective-permute-start(f32[256,768]{1,0:T(8,128)} %convolution_bitcast_fusion.1), channel_id=1, source_target_pairs={{0,4},{1,5},{2,6},{3,7},{4,0},{5,1},{6,2},{7,3},{8,12},{9,13},{10,... | collective-permute-start | bytes 2359304 | tf_op jit(solution)/shard_map/ppermute | solution.py:77
  115.4 3.1 %convolution_bitcast_fusion = f32[256,768]{1,0:T(8,128)} fusion(bf16[16,128,768]{2,1,0:T(8,128)(2,1)S(1)} %copy-done, bf16[16,1024,128]{2,1,0:T(8,128)(2,1)} %copy-done.3, s32[]{:T(128)S(6)} %select_n.84), kind=kOutput, calls=%fused_computation.4 | convolution fusion | flops 805306368 | bytes 4980740 | tf_op jit(solution)/shard_map/sik,skn->in/dot_general | solution.py:66
  118.5 4.4 %collective-permute-start.19 = (f32[256,768]{1,0:T(8,128)}, f32[256,768]{1,0:T(8,128)}, u32[]{:S(2)}, u32[]{:S(2)}) collective-permute-start(f32[256,768]{1,0:T(8,128)} %convolution_bitcast_fusion), channel_id=1, source_target_pairs={{0,6},{1,7},{2,0},{3,1},{4,2},{5,3},{6,4},{7,5},{8,14},{9,15},{10,... | collective-permute-start | bytes 2359304 | tf_op jit(solution)/shard_map/ppermute | solution.py:77
  122.9 5.7 %collective-permute-done.17 = f32[256,768]{1,0:T(8,128)} collective-permute-done((f32[256,768]{1,0:T(8,128)}, f32[256,768]{1,0:T(8,128)}, u32[]{:S(2)}, u32[]{:S(2)}) %collective-permute-start.17) | collective-permute-done | bytes 786464 | tf_op jit(solution)/shard_map/ppermute | solution.py:77
  128.6 8.2 %collective-permute-done.18 = f32[256,768]{1,0:T(8,128)} collective-permute-done((f32[256,768]{1,0:T(8,128)}, f32[256,768]{1,0:T(8,128)}, u32[]{:S(2)}, u32[]{:S(2)}) %collective-permute-start.18) | collective-permute-done | bytes 786464 | tf_op jit(solution)/shard_map/ppermute | solution.py:77
  136.7 12.0 %collective-permute-done.19 = f32[256,768]{1,0:T(8,128)} collective-permute-done((f32[256,768]{1,0:T(8,128)}, f32[256,768]{1,0:T(8,128)}, u32[]{:S(2)}, u32[]{:S(2)}) %collective-permute-start.19) | collective-permute-done | bytes 786464 | tf_op jit(solution)/shard_map/ppermute | solution.py:77
  148.7 3.8 %fusion.2 = f32[256,768]{1,0:T(8,128)} fusion(f32[256,768]{1,0:T(8,128)} %collective-permute-done.19, f32[256,768]{1,0:T(8,128)} %collective-permute-done.18, f32[256,768]{1,0:T(8,128)} %collective-permute-done.17, bf16[16,128,768]{2,1,0:T(8,128)(2,1)S(1)} %copy-done, bf16[16,1024,128]{2,1,0:T(8,128)(2,1)} %copy-done.3, s32[]{:T(128)S(6)} %select_n.73), kind=kOutput, calls=%fused_computation.10 | convolution fusion | flops 805896192 | bytes 7340036 | tf_op jit(solution)/shard_map/sik,skn->in/dot_general | solution.py:66
  159.4 7.1 %collective-permute-done.20 = f32[128,768]{1,0:T(8,128)S(1)} collective-permute-done((f32[128,768]{1,0:T(8,128)S(1)}, f32[128,768]{1,0:T(8,128)S(1)}, u32[]{:S(2)}, u32[]{:S(2)}) %collective-permute-start.20) | collective-permute-done | bytes 393248 | tf_op jit(solution)/shard_map/ppermute | solution.py:82
  (67 shorter events, 39.7 us)
Async XLA Ops:
  3.0 21.1 %collective-permute-start = (bf16[1024,128]{1,0:T(8,128)(2,1)S(1)}, bf16[1024,128]{1,0:T(8,128)(2,1)S(1)}, u32[]{:S(2)}, u32[]{:S(2)}) collective-permute-start(bf16[1024,128]{1,0:T(8,128)(2,1)S(1)} %bitcast.82), channel_id=1, source_target_pairs={{0,32},{32,64},{64,96},{96,128},{128,160},{160,192},{192,224},{224... | collective-permute-start | bytes 786440 | tf_op jit(solution)/shard_map/ppermute | solution.py:44
  6.8 19.2 %collective-permute-start.1 = (bf16[1024,128]{1,0:T(8,128)(2,1)S(1)}, bf16[1024,128]{1,0:T(8,128)(2,1)S(1)}, u32[]{:S(2)}, u32[]{:S(2)}) collective-permute-start(bf16[1024,128]{1,0:T(8,128)(2,1)S(1)} %bitcast.83), channel_id=1, source_target_pairs={{0,480},{32,0},{64,32},{96,64},{128,96},{160,128},{192,160},{224,1... | collective-permute-start | bytes 786440 | tf_op jit(solution)/shard_map/ppermute | solution.py:48
  18.3 49.1 %copy-start.1 = (bf16[4,128,768]{2,1,0:T(8,128)(2,1)}, bf16[4,128,768]{2,1,0:T(8,128)(2,1)S(1)}, u32[]{:S(2)}) copy-start(bf16[4,128,768]{2,1,0:T(8,128)(2,1)S(1)} %bitcast_multiply_fusion) | copy-start | bytes 2359300
  18.3 33.2 %collective-permute-start.15 = (bf16[4,128,768]{2,1,0:T(8,128)(2,1)S(1)}, bf16[4,128,768]{2,1,0:T(8,128)(2,1)S(1)}, u32[]{:S(2)}, u32[]{:S(2)}) collective-permute-start(bf16[4,128,768]{2,1,0:T(8,128)(2,1)S(1)} %bitcast_multiply_fusion), channel_id=1, source_target_pairs={{0,16},{8,24},{16,0},{24,8},{1,17},{9,25},{17,1},{25,9},{2,18},{10... | collective-permute-start | bytes 2359304 | tf_op jit(solution)/shard_map/ppermute | solution.py:11
  24.0 10.6 %collective-permute-start.2 = (bf16[1024,128]{1,0:T(8,128)(2,1)S(1)}, bf16[1024,128]{1,0:T(8,128)(2,1)S(1)}, u32[]{:S(2)}, u32[]{:S(2)}) collective-permute-start(bf16[1024,128]{1,0:T(8,128)(2,1)S(1)} %collective-permute-done), channel_id=1, source_target_pairs={{0,32},{32,64},{64,96},{96,128},{128,160},{160,192},{192,224},{224... | collective-permute-start | bytes 786440 | tf_op jit(solution)/shard_map/ppermute | solution.py:44
  26.0 10.6 %collective-permute-start.3 = (bf16[1024,128]{1,0:T(8,128)(2,1)S(1)}, bf16[1024,128]{1,0:T(8,128)(2,1)S(1)}, u32[]{:S(2)}, u32[]{:S(2)}) collective-permute-start(bf16[1024,128]{1,0:T(8,128)(2,1)S(1)} %collective-permute-done.1), channel_id=1, source_target_pairs={{0,480},{32,0},{64,32},{96,64},{128,96},{160,128},{192,160},{224,1... | collective-permute-start | bytes 786440 | tf_op jit(solution)/shard_map/ppermute | solution.py:48
  34.6 9.7 %collective-permute-start.4 = (bf16[1024,128]{1,0:T(8,128)(2,1)S(1)}, bf16[1024,128]{1,0:T(8,128)(2,1)S(1)}, u32[]{:S(2)}, u32[]{:S(2)}) collective-permute-start(bf16[1024,128]{1,0:T(8,128)(2,1)S(1)} %collective-permute-done.2), channel_id=1, source_target_pairs={{0,32},{32,64},{64,96},{96,128},{128,160},{160,192},{192,224},{224... | collective-permute-start | bytes 786440 | tf_op jit(solution)/shard_map/ppermute | solution.py:44
  36.6 9.6 %collective-permute-start.5 = (bf16[1024,128]{1,0:T(8,128)(2,1)S(1)}, bf16[1024,128]{1,0:T(8,128)(2,1)S(1)}, u32[]{:S(2)}, u32[]{:S(2)}) collective-permute-start(bf16[1024,128]{1,0:T(8,128)(2,1)S(1)} %collective-permute-done.3), channel_id=1, source_target_pairs={{0,480},{32,0},{64,32},{96,64},{128,96},{160,128},{192,160},{224,1... | collective-permute-start | bytes 786440 | tf_op jit(solution)/shard_map/ppermute | solution.py:48
  44.3 9.5 %collective-permute-start.6 = (bf16[1024,128]{1,0:T(8,128)(2,1)S(1)}, bf16[1024,128]{1,0:T(8,128)(2,1)S(1)}, u32[]{:S(2)}, u32[]{:S(2)}) collective-permute-start(bf16[1024,128]{1,0:T(8,128)(2,1)S(1)} %collective-permute-done.4), channel_id=1, source_target_pairs={{0,32},{32,64},{64,96},{96,128},{128,160},{160,192},{192,224},{224... | collective-permute-start | bytes 786440 | tf_op jit(solution)/shard_map/ppermute | solution.py:44
  46.2 9.5 %collective-permute-start.7 = (bf16[1024,128]{1,0:T(8,128)(2,1)S(1)}, bf16[1024,128]{1,0:T(8,128)(2,1)S(1)}, u32[]{:S(2)}, u32[]{:S(2)}) collective-permute-start(bf16[1024,128]{1,0:T(8,128)(2,1)S(1)} %collective-permute-done.5), channel_id=1, source_target_pairs={{0,480},{32,0},{64,32},{96,64},{128,96},{160,128},{192,160},{224,1... | collective-permute-start | bytes 786440 | tf_op jit(solution)/shard_map/ppermute | solution.py:48
  51.5 44.1 %copy-start.2 = (bf16[4,128,768]{2,1,0:T(8,128)(2,1)}, bf16[4,128,768]{2,1,0:T(8,128)(2,1)S(1)}, u32[]{:S(2)}) copy-start(bf16[4,128,768]{2,1,0:T(8,128)(2,1)S(1)} %collective-permute-done.15) | copy-start | bytes 2359300
  51.6 45.9 %collective-permute-start.16 = (bf16[8,128,768]{2,1,0:T(8,128)(2,1)S(1)}, bf16[8,128,768]{2,1,0:T(8,128)(2,1)S(1)}, u32[]{:S(2)}, u32[]{:S(2)}) collective-permute-start(bf16[8,128,768]{2,1,0:T(8,128)(2,1)S(1)} %pad_maximum_fusion.1), channel_id=1, source_target_pairs={{0,8},{8,0},{16,24},{24,16},{1,9},{9,1},{17,25},{25,17},{2,10},{10... | collective-permute-start | bytes 4718600 | tf_op jit(solution)/shard_map/ppermute | solution.py:11
  53.8 11.6 %collective-permute-start.8 = (bf16[1024,128]{1,0:T(8,128)(2,1)S(1)}, bf16[1024,128]{1,0:T(8,128)(2,1)S(1)}, u32[]{:S(2)}, u32[]{:S(2)}) collective-permute-start(bf16[1024,128]{1,0:T(8,128)(2,1)S(1)} %collective-permute-done.6), channel_id=1, source_target_pairs={{0,32},{32,64},{64,96},{96,128},{128,160},{160,192},{192,224},{224... | collective-permute-start | bytes 786440 | tf_op jit(solution)/shard_map/ppermute | solution.py:44
  55.7 11.6 %collective-permute-start.9 = (bf16[1024,128]{1,0:T(8,128)(2,1)S(1)}, bf16[1024,128]{1,0:T(8,128)(2,1)S(1)}, u32[]{:S(2)}, u32[]{:S(2)}) collective-permute-start(bf16[1024,128]{1,0:T(8,128)(2,1)S(1)} %collective-permute-done.7), channel_id=1, source_target_pairs={{0,480},{32,0},{64,32},{96,64},{128,96},{160,128},{192,160},{224,1... | collective-permute-start | bytes 786440 | tf_op jit(solution)/shard_map/ppermute | solution.py:48
  65.4 10.8 %collective-permute-start.10 = (bf16[1024,128]{1,0:T(8,128)(2,1)S(1)}, bf16[1024,128]{1,0:T(8,128)(2,1)S(1)}, u32[]{:S(2)}, u32[]{:S(2)}) collective-permute-start(bf16[1024,128]{1,0:T(8,128)(2,1)S(1)} %collective-permute-done.8), channel_id=1, source_target_pairs={{0,32},{32,64},{64,96},{96,128},{128,160},{160,192},{192,224},{224... | collective-permute-start | bytes 786440 | tf_op jit(solution)/shard_map/ppermute | solution.py:44
  67.4 10.8 %collective-permute-start.11 = (bf16[1024,128]{1,0:T(8,128)(2,1)S(1)}, bf16[1024,128]{1,0:T(8,128)(2,1)S(1)}, u32[]{:S(2)}, u32[]{:S(2)}) collective-permute-start(bf16[1024,128]{1,0:T(8,128)(2,1)S(1)} %collective-permute-done.9), channel_id=1, source_target_pairs={{0,480},{32,0},{64,32},{96,64},{128,96},{160,128},{192,160},{224,1... | collective-permute-start | bytes 786440 | tf_op jit(solution)/shard_map/ppermute | solution.py:48
  76.2 9.9 %collective-permute-start.12 = (bf16[1024,128]{1,0:T(8,128)(2,1)S(1)}, bf16[1024,128]{1,0:T(8,128)(2,1)S(1)}, u32[]{:S(2)}, u32[]{:S(2)}) collective-permute-start(bf16[1024,128]{1,0:T(8,128)(2,1)S(1)} %collective-permute-done.10), channel_id=1, source_target_pairs={{0,32},{32,64},{64,96},{96,128},{128,160},{160,192},{192,224},{224... | collective-permute-start | bytes 786440 | tf_op jit(solution)/shard_map/ppermute | solution.py:44
  78.1 9.9 %collective-permute-start.13 = (bf16[1024,128]{1,0:T(8,128)(2,1)S(1)}, bf16[1024,128]{1,0:T(8,128)(2,1)S(1)}, u32[]{:S(2)}, u32[]{:S(2)}) collective-permute-start(bf16[1024,128]{1,0:T(8,128)(2,1)S(1)} %collective-permute-done.11), channel_id=1, source_target_pairs={{0,480},{32,0},{64,32},{96,64},{128,96},{160,128},{192,160},{224,1... | collective-permute-start | bytes 786440 | tf_op jit(solution)/shard_map/ppermute | solution.py:48
  86.1 9.5 %collective-permute-start.14 = (bf16[1024,128]{1,0:T(8,128)(2,1)S(1)}, bf16[1024,128]{1,0:T(8,128)(2,1)S(1)}, u32[]{:S(2)}, u32[]{:S(2)}) collective-permute-start(bf16[1024,128]{1,0:T(8,128)(2,1)S(1)} %collective-permute-done.12), channel_id=1, source_target_pairs={{0,32},{32,64},{64,96},{96,128},{128,160},{160,192},{192,224},{224... | collective-permute-start | bytes 786440 | tf_op jit(solution)/shard_map/ppermute | solution.py:44
  105.9 22.7 %collective-permute-start.17 = (f32[256,768]{1,0:T(8,128)}, f32[256,768]{1,0:T(8,128)}, u32[]{:S(2)}, u32[]{:S(2)}) collective-permute-start(f32[256,768]{1,0:T(8,128)} %convolution_bitcast_fusion.2), channel_id=1, source_target_pairs={{0,2},{1,3},{2,4},{3,5},{4,6},{5,7},{6,0},{7,1},{8,10},{9,11},{10,... | collective-permute-start | bytes 2359304 | tf_op jit(solution)/shard_map/ppermute | solution.py:77
  112.5 24.2 %collective-permute-start.18 = (f32[256,768]{1,0:T(8,128)}, f32[256,768]{1,0:T(8,128)}, u32[]{:S(2)}, u32[]{:S(2)}) collective-permute-start(f32[256,768]{1,0:T(8,128)} %convolution_bitcast_fusion.1), channel_id=1, source_target_pairs={{0,4},{1,5},{2,6},{3,7},{4,0},{5,1},{6,2},{7,3},{8,12},{9,13},{10,... | collective-permute-start | bytes 2359304 | tf_op jit(solution)/shard_map/ppermute | solution.py:77
  118.5 37.6 %copy-start.4 = (s32[1,8]{1,0:T(1,128)S(1)}, s32[1,8]{1,0:T(1,128)}, u32[]{:S(2)}) copy-start(s32[1,8]{1,0:T(1,128)} %param.12) | copy-start | bytes 100
  118.5 30.3 %collective-permute-start.19 = (f32[256,768]{1,0:T(8,128)}, f32[256,768]{1,0:T(8,128)}, u32[]{:S(2)}, u32[]{:S(2)}) collective-permute-start(f32[256,768]{1,0:T(8,128)} %convolution_bitcast_fusion), channel_id=1, source_target_pairs={{0,6},{1,7},{2,0},{3,1},{4,2},{5,3},{6,4},{7,5},{8,14},{9,15},{10,... | collective-permute-start | bytes 2359304 | tf_op jit(solution)/shard_map/ppermute | solution.py:77
  153.6 12.9 %collective-permute-start.20 = (f32[128,768]{1,0:T(8,128)S(1)}, f32[128,768]{1,0:T(8,128)S(1)}, u32[]{:S(2)}, u32[]{:S(2)}) collective-permute-start(f32[128,768]{1,0:T(8,128)S(1)} %dynamic-slice_bitcast_fusion), channel_id=1, source_target_pairs={{0,1},{1,0},{2,3},{3,2},{4,5},{5,4},{6,7},{7,6},{8,9},{9,8},{10,11... | collective-permute-start | bytes 1179656 | tf_op jit(solution)/shard_map/ppermute | solution.py:82
  (2 other events, 9.7 us)

commit v6 on v2

--- a/solution.py
+++ b/solution.py
@@ -16,7 +16,6 @@
     local_groups = sign_mask.shape[0]
     sign_inner = sign_mask.shape[2]
     col_blocks = sign_mask.shape[3]
-    col_count = lax.axis_size("col")
     local_order = row_order[0]
     ks_panel = (
         ks_matrix.reshape(row_blocks, BS, inner_blocks, BS)
@@ -34,19 +33,17 @@
     near = swap_with(pair, "col", 1)
     sign_four = jnp.concatenate([pair, near], axis=0)
     me = lax.axis_index("col")
-    held_cols = jnp.stack([me, me ^ 2, me ^ 1, me ^ 3])
     ks_whole = lax.all_gather(ks_panel, "row", axis=0, tiled=False)
-    ks_whole = ks_whole.reshape(
-        col_count, local_groups, row_blocks * BS, inner_blocks * BS
+    inner_of = jnp.arange(lax.axis_size("row"), dtype=jnp.int32)
+    flipped = (inner_of // local_groups) ^ me
+    spot = (flipped % 2) * 2 + flipped // 2
+    sign_four = jnp.take(sign_four, spot * local_groups + inner_of % local_groups, axis=0, mode="clip")
+    product = jnp.einsum(
+        "sik,skn->in", ks_whole, sign_four, preferred_element_type=jnp.float32
     )
-    ks_matched = jnp.take(ks_whole, held_cols, axis=0, mode="clip")
-    ks_matched = ks_matched.reshape(
-        col_count * local_groups, row_blocks * BS, inner_blocks * BS
-    )
-    product = jnp.einsum(
-        "sik,skn->in", ks_matched, sign_four, preferred_element_type=jnp.float32
-    )
-    summed = lax.psum_scatter(product, "depth", scatter_dimension=0, tiled=True)
+    parts = product.reshape(row_blocks, BS, col_blocks * BS)
+    arrived = lax.all_to_all(parts, "depth", 0, 0, tiled=True)
+    summed = jnp.sum(arrived, axis=0)
     own_row = lax.dynamic_index_in_dim(
         local_order, lax.axis_index("depth"), 0, keepdims=False
     )

time: 191 us -> 144 us (0.75)
  the two profiles are of different devices: /device:TPU:1 before, /device:TPU:4 now
where the time goes in v6:
time: 144 us
  waiting for transfers between devices  92.8 us (64%)
  between operations  15.4 us (11%)
  starting transfers between devices  14.7 us (10%)
  other arithmetic  8.16 us (6%)
  matrix products  7.27 us (5%)
  local copies, waits for them, and re-layouts  5.2 us (4%)
    all_gather x1, waiting for transfers between devices, per_device(): ks_whole = lax.all_gather(ks_panel, 'row', axis=0, tiled=False)  47.8 us
    all_to_all x1, waiting for transfers between devices, per_device(): arrived = lax.all_to_all(parts, 'depth', 0, 0, tiled=True)  26.7 us
    ppermute x2, waiting for transfers between devices, swap_with(): return lax.ppermute(block, axis, [(i, i ^ flip) for i in devices])  18.3 us
    ppermute x2, starting transfers between devices, swap_with(): return lax.ppermute(block, axis, [(i, i ^ flip) for i in devices])  9.7 us
    dot_general x1, matrix products, per_device(): jnp.einsum('sik,skn->in', ks_whole, sign_four, preferred_element_type=jnp...  7.27 us
    all_to_all x1, starting transfers between devices, per_device(): arrived = lax.all_to_all(parts, 'depth', 0, 0, tiled=True)  4.97 us
  transfers between devices with their start and end apart: 4, of which 4 were waited for; matrix products, arithmetic and copies ran while one was open for 6% of the time, Pallas kernels for 0%

profile of v6, /device:TPU:4, one launch (start us, length us, event | category | flops | bytes accessed | tf_op | source)
XLA Modules:
  0.0 143.5 jit_solution(17154412518106387187)
XLA Ops:
  6.5 0.7 convert_bitcast_fusion.1
  7.2 0.7 pad_clamp_fusion.1
  7.9 1.0 multiply_bitcast_fusion
  8.9 1.3 gather_fusion
  10.2 0.7 convert_element_type.20
  10.9 0.1 broadcast_bitcast_fusion
  11.0 1.2 bitcast_multiply_fusion
  12.2 7.8 %collective-permute-start = (bf16[4,128,768]{2,1,0:T(8,128)(2,1)S(1)}, bf16[4,128,768]{2,1,0:T(8,128)(2,1)S(1)}, u32[]{:S(2)}, u32[]{:S(2)}) collective-permute-start(bf16[4,128,768]{2,1,0:T(8,128)(2,1)S(1)} %bitcast_multiply_fusion), channel_id=1, source_target_pairs={{0,16},{8,24},{16,0},{24,8},{1,17},{9,25},{17,1},{25,9},{2,18},{10... | collective-permute-start | bytes 2359304 | tf_op jit(solution)/shard_map/ppermute | solution.py:11
  20.0 14.9 %collective-permute-done = bf16[4,128,768]{2,1,0:T(8,128)(2,1)S(1)} collective-permute-done((bf16[4,128,768]{2,1,0:T(8,128)(2,1)S(1)}, bf16[4,128,768]{2,1,0:T(8,128)(2,1)S(1)}, u32[]{:S(2)}, u32[]{:S(2)}) %collective-permute-start) | collective-permute-done | bytes 786464 | tf_op jit(solution)/shard_map/ppermute | solution.py:11
  34.9 0.1 pad_maximum_fusion.1
  35.0 0.8 copy-done.1
  35.8 1.9 %collective-permute-start.1 = (bf16[8,128,768]{2,1,0:T(8,128)(2,1)S(1)}, bf16[8,128,768]{2,1,0:T(8,128)(2,1)}, u32[]{:S(2)}, u32[]{:S(2)}) collective-permute-start(bf16[8,128,768]{2,1,0:T(8,128)(2,1)S(1)} %pad_maximum_fusion.1), channel_id=1, source_target_pairs={{0,8},{8,0},{16,24},{24,16},{1,9},{9,1},{17,25},{25,17},{2,10},{10... | collective-permute-start | bytes 4718600 | tf_op jit(solution)/shard_map/ppermute | solution.py:11
  37.7 3.5 %collective-permute-done.1 = bf16[8,128,768]{2,1,0:T(8,128)(2,1)} collective-permute-done((bf16[8,128,768]{2,1,0:T(8,128)(2,1)S(1)}, bf16[8,128,768]{2,1,0:T(8,128)(2,1)}, u32[]{:S(2)}, u32[]{:S(2)}) %collective-permute-start.1) | collective-permute-done | bytes 1572896 | tf_op jit(solution)/shard_map/ppermute | solution.py:11
  41.2 2.2 %pad_maximum_fusion = bf16[16,128,768]{2,1,0:T(8,128)(2,1)S(1)} fusion(bf16[8,128,768]{2,1,0:T(8,128)(2,1)} %collective-permute-done.1, bf16[4,128,768]{2,1,0:T(8,128)(2,1)} %copy-done.1, bf16[4,128,768]{2,1,0:T(8,128)(2,1)} %copy-done), kind=kLoop, calls=%fused_computation.2 | loop fusion | flops 3145728 | bytes 6291456 | tf_op jit(solution)/shard_map/concatenate | solution.py:34
  43.4 2.4 %gather_fusion.1 = bf16[16,128,768]{2,1,0:T(8,128)(2,1)} fusion(bf16[16,128,768]{2,1,0:T(8,128)(2,1)S(1)} %pad_maximum_fusion, s32[1024]{0:T(1024)S(1)} %pad_clamp_fusion), kind=kCustom, calls=%fused_computation.1 | custom fusion | bytes 6291520 | tf_op jit(solution)/shard_map/jit(_take)/gather | solution.py:40
  45.8 47.8 %all-gather.2.cloned.1.call-done = bf16[16,1024,128]{2,1,0:T(8,128)(2,1)} async-done(((bf16[1,1024,128]{2,1,0:T(8,128)(2,1)}), bf16[16,1024,128]{2,1,0:T(8,128)(2,1)}) %all-gather.2.cloned.1.call-update) | async-done | bytes 4194320 | tf_op jit(solution)/shard_map/all_gather | solution.py:36
  93.6 7.3 %fusion.5 = f32[1024,768,1]{1,0,2:T(8,128)} fusion(bf16[16,1024,128]{2,1,0:T(8,128)(2,1)} %all-gather.2.cloned.1.call-done, bf16[16,128,768]{2,1,0:T(8,128)(2,1)} %gather_fusion.1), kind=kOutput, calls=%fused_computation.31 | convolution fusion | flops 3221225472 | bytes 10485760 | tf_op jit(solution)/shard_map/sik,skn->in/dot_general | solution.py:41
  100.8 5.0 %all-to-all-start = ((f32[8,128,768]{2,1,0:T(8,128)}), f32[8,128,768]{2,1,0:T(8,128)S(1)}, u32[]{:S(2)}, u32[]{:S(2)}) async-start(f32[8,128,768]{2,1,0:T(8,128)} %bitcast.29), calls=%async_computation | async-start | bytes 6291456 | tf_op jit(solution)/shard_map/all_to_all | solution.py:45
  105.8 0.6 constant_dynamic-slice_fusion
  108.3 0.7 convert_bitcast_fusion
  109.0 0.1 broadcast_bitcast_fusion.1
  109.1 26.7 %all-to-all-done = f32[8,128,768]{2,1,0:T(8,128)S(1)} async-done(((f32[8,128,768]{2,1,0:T(8,128)}), f32[8,128,768]{2,1,0:T(8,128)S(1)}, u32[]{:S(2)}, u32[]{:S(2)}) %all-to-all-start) | async-done | bytes 3145760 | tf_op jit(solution)/shard_map/all_to_all | solution.py:45
  135.8 0.2 reduce_sum.9
  136.0 0.7 multiply_convert_fusion
  (11 shorter events, 0.1 us)
Async XLA Ops:
  6.5 87.0 %all-gather.2.cloned.1.call-start = ((), (), s32[]{:S(2)}) async-start(), calls=%async_computation.1 | async-start | bytes 4456448 | tf_op jit(solution)/shard_map/all_gather | solution.py:36
  12.2 22.7 %copy-start = (bf16[4,128,768]{2,1,0:T(8,128)(2,1)}, bf16[4,128,768]{2,1,0:T(8,128)(2,1)S(1)}, u32[]{:S(2)}) copy-start(bf16[4,128,768]{2,1,0:T(8,128)(2,1)S(1)} %bitcast_multiply_fusion) | copy-start | bytes 2359300
  12.2 22.7 %collective-permute-start = (bf16[4,128,768]{2,1,0:T(8,128)(2,1)S(1)}, bf16[4,128,768]{2,1,0:T(8,128)(2,1)S(1)}, u32[]{:S(2)}, u32[]{:S(2)}) collective-permute-start(bf16[4,128,768]{2,1,0:T(8,128)(2,1)S(1)} %bitcast_multiply_fusion), channel_id=1, source_target_pairs={{0,16},{8,24},{16,0},{24,8},{1,17},{9,25},{17,1},{25,9},{2,18},{10... | collective-permute-start | bytes 2359304 | tf_op jit(solution)/shard_map/ppermute | solution.py:11
  34.9 0.9 copy-start.1
  35.8 5.4 %collective-permute-start.1 = (bf16[8,128,768]{2,1,0:T(8,128)(2,1)S(1)}, bf16[8,128,768]{2,1,0:T(8,128)(2,1)}, u32[]{:S(2)}, u32[]{:S(2)}) collective-permute-start(bf16[8,128,768]{2,1,0:T(8,128)(2,1)S(1)} %pad_maximum_fusion.1), channel_id=1, source_target_pairs={{0,8},{8,0},{16,24},{24,16},{1,9},{9,1},{17,25},{25,17},{2,10},{10... | collective-permute-start | bytes 4718600 | tf_op jit(solution)/shard_map/ppermute | solution.py:11
  100.8 5.0 %copy-start.2 = (s32[1,8]{1,0:T(1,128)S(1)}, s32[1,8]{1,0:T(1,128)}, u32[]{:S(2)}) copy-start(s32[1,8]{1,0:T(1,128)} %param.11) | copy-start | bytes 100
  100.8 34.9 %all-to-all-start = ((f32[8,128,768]{2,1,0:T(8,128)}), f32[8,128,768]{2,1,0:T(8,128)S(1)}, u32[]{:S(2)}, u32[]{:S(2)}) async-start(f32[8,128,768]{2,1,0:T(8,128)} %bitcast.29), calls=%async_computation | async-start | bytes 6291456 | tf_op jit(solution)/shard_map/all_to_all | solution.py:45
Sparse Core Ops, SparseCore 0:
  10.3 83.1 all-gather.1

commit v7 on v6

--- a/solution.py
+++ b/solution.py
@@ -33,17 +33,47 @@
     near = swap_with(pair, "col", 1)
     sign_four = jnp.concatenate([pair, near], axis=0)
     me = lax.axis_index("col")
-    ks_whole = lax.all_gather(ks_panel, "row", axis=0, tiled=False)
-    inner_of = jnp.arange(lax.axis_size("row"), dtype=jnp.int32)
-    flipped = (inner_of // local_groups) ^ me
-    spot = (flipped % 2) * 2 + flipped // 2
-    sign_four = jnp.take(sign_four, spot * local_groups + inner_of % local_groups, axis=0, mode="clip")
-    product = jnp.einsum(
-        "sik,skn->in", ks_whole, sign_four, preferred_element_type=jnp.float32
+    row_count = lax.axis_size("row")
+    row_me = lax.axis_index("row")
+    half_rows = BS // 2
+    split = ks_panel.reshape(row_blocks, 2, half_rows, inner_blocks * BS)
+    low = split[:, 0].reshape(row_blocks * half_rows, inner_blocks * BS)
+    high = split[:, 1].reshape(row_blocks * half_rows, inner_blocks * BS)
+
+    def sign_in_order(inner_of):
+        flipped = (inner_of // local_groups) ^ me
+        spot = (flipped % 2) * 2 + flipped // 2
+        return jnp.take(sign_four, spot * local_groups + inner_of % local_groups, axis=0, mode="clip")
+
+    def reduced_over_depth(panels, signs):
+        product = jnp.einsum(
+            "sik,skn->in", panels, signs, preferred_element_type=jnp.float32
+        )
+        parts = product.reshape(row_blocks, half_rows, col_blocks * BS)
+        arrived = lax.all_to_all(parts, "depth", 0, 0, tiled=True)
+        return jnp.sum(arrived, axis=0)
+
+    low_whole = lax.all_gather(low, "row", axis=0, tiled=False)
+    rightward = [(i, (i + 1) % row_count) for i in range(row_count)]
+    leftward = [(i, (i - 1) % row_count) for i in range(row_count)]
+    going_right = high
+    going_left = high
+    panels = [high]
+    offsets = [0]
+    for step in range(1, row_count // 2 + 1):
+        going_right = lax.ppermute(going_right, "row", rightward)
+        panels.append(going_right)
+        offsets.append(-step)
+        if step < row_count - step:
+            going_left = lax.ppermute(going_left, "row", leftward)
+            panels.append(going_left)
+            offsets.append(step)
+    ring_inner = (row_me + jnp.array(offsets, jnp.int32)) % row_count
+    high_sum = reduced_over_depth(jnp.stack(panels), sign_in_order(ring_inner))
+    low_sum = reduced_over_depth(
+        low_whole, sign_in_order(jnp.arange(row_count, dtype=jnp.int32))
     )
-    parts = product.reshape(row_blocks, BS, col_blocks * BS)
-    arrived = lax.all_to_all(parts, "depth", 0, 0, tiled=True)
-    summed = jnp.sum(arrived, axis=0)
+    summed = jnp.concatenate([low_sum, high_sum], axis=0)
     own_row = lax.dynamic_index_in_dim(
         local_order, lax.axis_index("depth"), 0, keepdims=False
     )

time: 144 us -> 163 us (1.13)
  starting transfers between devices: 14.7 us -> 72.4 us
  waiting for transfers between devices: 92.8 us -> 46.3 us
  matrix products: 7.27 us -> 10.9 us
  local copies, waits for them, and re-layouts: 5.2 us -> 8.56 us
    ppermute x0 -> x15, starting transfers between devices: none -> 58.8 us  [the longest x7 41.4 us: per_device(): going_left = lax.ppermute(going_left, 'row', leftward)]
    all_gather x1, waiting for transfers between devices: 47.8 us -> 0.01 us  [per_device(): low_whole = lax.all_gather(low, 'row', axis=0, tiled=False)]
    ppermute x2, waiting for transfers between devices: 18.3 us -> 0.01 us  [swap_with(): return lax.ppermute(block, axis, [(i, i ^ flip) for i in devices])]
    ppermute x0 -> x15, waiting for transfers between devices: none -> 17.3 us  [the longest x8 17.2 us: per_device(): going_right = lax.ppermute(going_right, 'row', rightward)]
    ppermute x2, starting transfers between devices: 9.7 us -> 4.34 us  [swap_with(): return lax.ppermute(block, axis, [(i, i ^ flip) for i in devices])]
    all_to_all x1 -> x2, starting transfers between devices: 4.97 us -> 9.32 us  [reduced_over_depth(): arrived = lax.all_to_all(parts, 'depth', 0, 0, tiled=True)]
    dot_general x1 -> x2, matrix products: 7.27 us -> 10.9 us  [reduced_over_depth(): jnp.einsum('sik,skn->in', panels, signs, preferred_element_type=jnp.float32)]
    gather x1 -> x2, local copies, waits for them, and re-layouts: 2.42 us -> 4.88 us  [sign_in_order(): jnp.take(sign_four, spot * local_groups + inner_of % local_groups, axis=0...]
  transfers between devices with their start and end apart: 4 -> 20, of which waited for: 4 -> 8; matrix products, arithmetic and copies ran while one was open for 6% -> 13% of each run, Pallas kernels for 0% -> 0%
where the time goes in v7:
time: 163 us; the launch traced here: 162 us
  starting transfers between devices  72.4 us (44%)
  waiting for transfers between devices  46.3 us (28%)
  between operations  15.8 us (10%)
  matrix products  10.9 us (7%)
  local copies, waits for them, and re-layouts  8.56 us (5%)
  other arithmetic  7.81 us (5%)
    ppermute x7, starting transfers between devices, per_device(): going_left = lax.ppermute(going_left, 'row', leftward)  41.4 us
    all_to_all x2, waiting for transfers between devices, reduced_over_depth(): arrived = lax.all_to_all(parts, 'depth', 0, 0, tiled=True)  29 us
    ppermute x8, starting transfers between devices, per_device(): going_right = lax.ppermute(going_right, 'row', rightward)  17.3 us
    ppermute x8, waiting for transfers between devices, per_device(): going_right = lax.ppermute(going_right, 'row', rightward)  17.2 us
    dot_general x2, matrix products, reduced_over_depth(): jnp.einsum('sik,skn->in', panels, signs, preferred_element_type=jnp.float32)  10.9 us
    all_to_all x2, starting transfers between devices, reduced_over_depth(): arrived = lax.all_to_all(parts, 'depth', 0, 0, tiled=True)  9.32 us
    gather x2, local copies, waits for them, and re-layouts, sign_in_order(): jnp.take(sign_four, spot * local_groups + inner_of % local_groups, axis=0...  4.88 us
    ppermute x2, starting transfers between devices, swap_with(): return lax.ppermute(block, axis, [(i, i ^ flip) for i in devices])  4.34 us
  transfers between devices with their start and end apart: 20, of which 8 were waited for; matrix products, arithmetic and copies ran while one was open for 13% of the time, Pallas kernels for 0%

profile of v7, /device:TPU:4, one launch (start us, length us, event | category | flops | bytes accessed | tf_op | source)
XLA Modules:
  0.0 161.8 jit_solution(8099847351572102844)
XLA Ops:
  10.3 3.8 %collective-permute-start.2 = (bf16[512,128]{1,0:T(8,128)(2,1)S(1)}, bf16[512,128]{1,0:T(8,128)(2,1)S(1)}, u32[]{:S(2)}, u32[]{:S(2)}) collective-permute-start(bf16[512,128]{1,0:T(8,128)(2,1)S(1)} %bitcast.70), channel_id=1, source_target_pairs={{0,32},{32,64},{64,96},{96,128},{128,160},{160,192},{192,224},{224... | collective-permute-start | bytes 393224 | tf_op jit(solution)/shard_map/ppermute | solution.py:64
  14.1 9.5 %collective-permute-start.3 = (bf16[512,128]{1,0:T(8,128)(2,1)S(1)}, bf16[512,128]{1,0:T(8,128)(2,1)S(1)}, u32[]{:S(2)}, u32[]{:S(2)}) collective-permute-start(bf16[512,128]{1,0:T(8,128)(2,1)S(1)} %bitcast.71), channel_id=1, source_target_pairs={{0,480},{32,0},{64,32},{96,64},{128,96},{160,128},{192,160},{224,1... | collective-permute-start | bytes 393224 | tf_op jit(solution)/shard_map/ppermute | solution.py:68
  24.4 2.4 %collective-permute-start = (bf16[4,128,768]{2,1,0:T(8,128)(2,1)S(1)}, bf16[4,128,768]{2,1,0:T(8,128)(2,1)S(1)}, u32[]{:S(2)}, u32[]{:S(2)}) collective-permute-start(bf16[4,128,768]{2,1,0:T(8,128)(2,1)S(1)} %bitcast_multiply_fusion), channel_id=1, source_target_pairs={{0,16},{8,24},{16,0},{24,8},{1,17},{9,25},{17,1},{25,9},{2,18},{10... | collective-permute-start | bytes 2359304 | tf_op jit(solution)/shard_map/ppermute | solution.py:11
  27.0 1.9 %collective-permute-start.4 = (bf16[512,128]{1,0:T(8,128)(2,1)S(1)}, bf16[512,128]{1,0:T(8,128)(2,1)S(1)}, u32[]{:S(2)}, u32[]{:S(2)}) collective-permute-start(bf16[512,128]{1,0:T(8,128)(2,1)S(1)} %collective-permute-done.2), channel_id=1, source_target_pairs={{0,32},{32,64},{64,96},{96,128},{128,160},{160,192},{192,224},{224... | collective-permute-start | bytes 393224 | tf_op jit(solution)/shard_map/ppermute | solution.py:64
  28.9 5.1 %collective-permute-start.5 = (bf16[512,128]{1,0:T(8,128)(2,1)S(1)}, bf16[512,128]{1,0:T(8,128)(2,1)S(1)}, u32[]{:S(2)}, u32[]{:S(2)}) collective-permute-start(bf16[512,128]{1,0:T(8,128)(2,1)S(1)} %collective-permute-done.3), channel_id=1, source_target_pairs={{0,480},{32,0},{64,32},{96,64},{128,96},{160,128},{192,160},{224,1... | collective-permute-start | bytes 393224 | tf_op jit(solution)/shard_map/ppermute | solution.py:68
  37.0 5.1 %collective-permute-start.7 = (bf16[512,128]{1,0:T(8,128)(2,1)S(1)}, bf16[512,128]{1,0:T(8,128)(2,1)S(1)}, u32[]{:S(2)}, u32[]{:S(2)}) collective-permute-start(bf16[512,128]{1,0:T(8,128)(2,1)S(1)} %collective-permute-done.5), channel_id=1, source_target_pairs={{0,480},{32,0},{64,32},{96,64},{128,96},{160,128},{192,160},{224,1... | collective-permute-start | bytes 393224 | tf_op jit(solution)/shard_map/ppermute | solution.py:68
  43.1 1.9 %collective-permute-start.8 = (bf16[512,128]{1,0:T(8,128)(2,1)S(1)}, bf16[512,128]{1,0:T(8,128)(2,1)S(1)}, u32[]{:S(2)}, u32[]{:S(2)}) collective-permute-start(bf16[512,128]{1,0:T(8,128)(2,1)S(1)} %collective-permute-done.6), channel_id=1, source_target_pairs={{0,32},{32,64},{64,96},{96,128},{128,160},{160,192},{192,224},{224... | collective-permute-start | bytes 393224 | tf_op jit(solution)/shard_map/ppermute | solution.py:64
  45.1 5.4 %collective-permute-start.9 = (bf16[512,128]{1,0:T(8,128)(2,1)S(1)}, bf16[512,128]{1,0:T(8,128)(2,1)S(1)}, u32[]{:S(2)}, u32[]{:S(2)}) collective-permute-start(bf16[512,128]{1,0:T(8,128)(2,1)S(1)} %collective-permute-done.7), channel_id=1, source_target_pairs={{0,480},{32,0},{64,32},{96,64},{128,96},{160,128},{192,160},{224,1... | collective-permute-start | bytes 393224 | tf_op jit(solution)/shard_map/ppermute | solution.py:68
  50.5 2.1 %collective-permute-done.8 = bf16[512,128]{1,0:T(8,128)(2,1)S(1)} collective-permute-done((bf16[512,128]{1,0:T(8,128)(2,1)S(1)}, bf16[512,128]{1,0:T(8,128)(2,1)S(1)}, u32[]{:S(2)}, u32[]{:S(2)}) %collective-permute-start.8) | collective-permute-done | bytes 131104 | tf_op jit(solution)/shard_map/ppermute | solution.py:64
  54.5 5.6 %collective-permute-start.11 = (bf16[512,128]{1,0:T(8,128)(2,1)S(1)}, bf16[512,128]{1,0:T(8,128)(2,1)S(1)}, u32[]{:S(2)}, u32[]{:S(2)}) collective-permute-start(bf16[512,128]{1,0:T(8,128)(2,1)S(1)} %collective-permute-done.9), channel_id=1, source_target_pairs={{0,480},{32,0},{64,32},{96,64},{128,96},{160,128},{192,160},{224,1... | collective-permute-start | bytes 393224 | tf_op jit(solution)/shard_map/ppermute | solution.py:68
  63.3 5.6 %collective-permute-start.13 = (bf16[512,128]{1,0:T(8,128)(2,1)S(1)}, bf16[512,128]{1,0:T(8,128)(2,1)S(1)}, u32[]{:S(2)}, u32[]{:S(2)}) collective-permute-start(bf16[512,128]{1,0:T(8,128)(2,1)S(1)} %collective-permute-done.11), channel_id=1, source_target_pairs={{0,480},{32,0},{64,32},{96,64},{128,96},{160,128},{192,160},{224,1... | collective-permute-start | bytes 393224 | tf_op jit(solution)/shard_map/ppermute | solution.py:68
  69.0 1.9 %collective-permute-start.1 = (bf16[8,128,768]{2,1,0:T(8,128)(2,1)S(1)}, bf16[8,128,768]{2,1,0:T(8,128)(2,1)S(1)}, u32[]{:S(2)}, u32[]{:S(2)}) collective-permute-start(bf16[8,128,768]{2,1,0:T(8,128)(2,1)S(1)} %pad_maximum_fusion.1), channel_id=1, source_target_pairs={{0,8},{8,0},{16,24},{24,16},{1,9},{9,1},{17,25},{25,17},{2,10},{10... | collective-permute-start | bytes 4718600 | tf_op jit(solution)/shard_map/ppermute | solution.py:11
  71.0 2.1 %collective-permute-start.14 = (bf16[512,128]{1,0:T(8,128)(2,1)S(1)}, bf16[512,128]{1,0:T(8,128)(2,1)S(1)}, u32[]{:S(2)}, u32[]{:S(2)}) collective-permute-start(bf16[512,128]{1,0:T(8,128)(2,1)S(1)} %collective-permute-done.12), channel_id=1, source_target_pairs={{0,32},{32,64},{64,96},{96,128},{128,160},{160,192},{192,224},{224... | collective-permute-start | bytes 393224 | tf_op jit(solution)/shard_map/ppermute | solution.py:64
  73.1 5.1 %collective-permute-start.15 = (bf16[512,128]{1,0:T(8,128)(2,1)S(1)}, bf16[512,128]{1,0:T(8,128)(2,1)S(1)}, u32[]{:S(2)}, u32[]{:S(2)}) collective-permute-start(bf16[512,128]{1,0:T(8,128)(2,1)S(1)} %collective-permute-done.13), channel_id=1, source_target_pairs={{0,480},{32,0},{64,32},{96,64},{128,96},{160,128},{192,160},{224,1... | collective-permute-start | bytes 393224 | tf_op jit(solution)/shard_map/ppermute | solution.py:68
  78.3 3.7 %collective-permute-done.14 = bf16[512,128]{1,0:T(8,128)(2,1)S(1)} collective-permute-done((bf16[512,128]{1,0:T(8,128)(2,1)S(1)}, bf16[512,128]{1,0:T(8,128)(2,1)S(1)}, u32[]{:S(2)}, u32[]{:S(2)}) %collective-permute-start.14) | collective-permute-done | bytes 131104 | tf_op jit(solution)/shard_map/ppermute | solution.py:64
  84.0 8.4 %collective-permute-done.16 = bf16[512,128]{1,0:T(8,128)(2,1)S(1)} collective-permute-done((bf16[512,128]{1,0:T(8,128)(2,1)S(1)}, bf16[512,128]{1,0:T(8,128)(2,1)S(1)}, u32[]{:S(2)}, u32[]{:S(2)}) %collective-permute-start.16) | collective-permute-done | bytes 131104 | tf_op jit(solution)/shard_map/ppermute | solution.py:64
  95.2 2.4 %gather_fusion.2 = bf16[16,128,768]{2,1,0:T(8,128)(2,1)} fusion(bf16[16,128,768]{2,1,0:T(8,128)(2,1)S(1)} %pad_maximum_fusion, s32[1024]{0:T(1024)S(1)} %pad_clamp_fusion), kind=kCustom, calls=%fused_computation.2 | custom fusion | bytes 6291520 | tf_op jit(solution)/shard_map/jit(_take)/gather | solution.py:46
  97.6 5.5 %fusion.12 = f32[512,768,1]{1,0,2:T(8,128)} fusion(bf16[16,512,128]{2,1,0:T(8,128)(2,1)} %copy-done.4, bf16[16,128,768]{2,1,0:T(8,128)(2,1)} %gather_fusion.2), kind=kOutput, calls=%fused_computation.69 | convolution fusion | flops 1610612736 | bytes 6815744 | tf_op jit(solution)/shard_map/sik,skn->in/dot_general | solution.py:49
  103.1 5.7 %all-to-all-start.1 = ((f32[8,64,768]{2,1,0:T(8,128)}), f32[8,64,768]{2,1,0:T(8,128)}, u32[]{:S(2)}, u32[]{:S(2)}) async-start(f32[8,64,768]{2,1,0:T(8,128)} %bitcast.67), calls=%async_computation.1 | async-start | bytes 3145728 | tf_op jit(solution)/shard_map/all_to_all | solution.py:53
  108.8 2.5 %gather_fusion.1 = bf16[16,128,768]{2,1,0:T(8,128)(2,1)} fusion(bf16[16,128,768]{2,1,0:T(8,128)(2,1)S(1)} %pad_maximum_fusion, s32[1024]{0:T(1024)S(1)} %pad_clamp_fusion.1), kind=kCustom, calls=%fused_computation.1 | custom fusion | bytes 6291520 | tf_op jit(solution)/shard_map/jit(_take)/gather | solution.py:46
  111.3 5.5 %fusion.11 = f32[512,768,1]{1,0,2:T(8,128)} fusion(bf16[16,512,128]{2,1,0:T(8,128)(2,1)} %all-gather.2.cloned.1.call-done, bf16[16,128,768]{2,1,0:T(8,128)(2,1)} %gather_fusion.1), kind=kOutput, calls=%fused_computation.68 | convolution fusion | flops 1610612736 | bytes 6815744 | tf_op jit(solution)/shard_map/sik,skn->in/dot_general | solution.py:49
  116.8 13.3 %all-to-all-done.1 = f32[8,64,768]{2,1,0:T(8,128)} async-done(((f32[8,64,768]{2,1,0:T(8,128)}), f32[8,64,768]{2,1,0:T(8,128)}, u32[]{:S(2)}, u32[]{:S(2)}) %all-to-all-start.1) | async-done | bytes 1572896 | tf_op jit(solution)/shard_map/all_to_all | solution.py:53
  130.0 3.6 %all-to-all-start = ((f32[8,64,768]{2,1,0:T(8,128)}), f32[8,64,768]{2,1,0:T(8,128)S(1)}, u32[]{:S(2)}, u32[]{:S(2)}) async-start(f32[8,64,768]{2,1,0:T(8,128)} %bitcast.9), calls=%async_computation | async-start | bytes 3145728 | tf_op jit(solution)/shard_map/all_to_all | solution.py:53
  138.4 15.8 %all-to-all-done = f32[8,64,768]{2,1,0:T(8,128)S(1)} async-done(((f32[8,64,768]{2,1,0:T(8,128)}), f32[8,64,768]{2,1,0:T(8,128)S(1)}, u32[]{:S(2)}, u32[]{:S(2)}) %all-to-all-start) | async-done | bytes 1572896 | tf_op jit(solution)/shard_map/all_to_all | solution.py:53
  (73 shorter events, 22.2 us)
Async XLA Ops:
  6.5 20.4 %copy-start.6 = (s32[16]{0:T(128)S(1)}, s32[16]{0:T(128)}, u32[]{:S(2)}) copy-start(s32[16]{0:T(128)} %constant.113.clone) | copy-start | bytes 196
  6.5 17.8 %copy-start.3 = (bf16[4,1,128,768]{3,2,1,0:T(8,128)(2,1)S(1)}, bf16[4,1,128,768]{3,2,1,0:T(8,128)(2,1)}, u32[]{:S(2)}) copy-start(bf16[4,1,128,768]{3,2,1,0:T(8,128)(2,1)} %param.8) | copy-start | bytes 2359300
  6.5 104.7 %all-gather.2.cloned.1.call-start = ((), (), s32[]{:S(2)}) async-start(), calls=%async_computation.2 | async-start | bytes 2228224 | tf_op jit(solution)/shard_map/all_gather | solution.py:56
  10.3 16.7 %collective-permute-start.2 = (bf16[512,128]{1,0:T(8,128)(2,1)S(1)}, bf16[512,128]{1,0:T(8,128)(2,1)S(1)}, u32[]{:S(2)}, u32[]{:S(2)}) collective-permute-start(bf16[512,128]{1,0:T(8,128)(2,1)S(1)} %bitcast.70), channel_id=1, source_target_pairs={{0,32},{32,64},{64,96},{96,128},{128,160},{160,192},{192,224},{224... | collective-permute-start | bytes 393224 | tf_op jit(solution)/shard_map/ppermute | solution.py:64
  14.1 14.9 %collective-permute-start.3 = (bf16[512,128]{1,0:T(8,128)(2,1)S(1)}, bf16[512,128]{1,0:T(8,128)(2,1)S(1)}, u32[]{:S(2)}, u32[]{:S(2)}) collective-permute-start(bf16[512,128]{1,0:T(8,128)(2,1)S(1)} %bitcast.71), channel_id=1, source_target_pairs={{0,480},{32,0},{64,32},{96,64},{128,96},{160,128},{192,160},{224,1... | collective-permute-start | bytes 393224 | tf_op jit(solution)/shard_map/ppermute | solution.py:68
  24.4 44.6 %copy-start = (bf16[4,128,768]{2,1,0:T(8,128)(2,1)}, bf16[4,128,768]{2,1,0:T(8,128)(2,1)S(1)}, u32[]{:S(2)}) copy-start(bf16[4,128,768]{2,1,0:T(8,128)(2,1)S(1)} %bitcast_multiply_fusion) | copy-start | bytes 2359300
  24.4 44.4 %collective-permute-start = (bf16[4,128,768]{2,1,0:T(8,128)(2,1)S(1)}, bf16[4,128,768]{2,1,0:T(8,128)(2,1)S(1)}, u32[]{:S(2)}, u32[]{:S(2)}) collective-permute-start(bf16[4,128,768]{2,1,0:T(8,128)(2,1)S(1)} %bitcast_multiply_fusion), channel_id=1, source_target_pairs={{0,16},{8,24},{16,0},{24,8},{1,17},{9,25},{17,1},{25,9},{2,18},{10... | collective-permute-start | bytes 2359304 | tf_op jit(solution)/shard_map/ppermute | solution.py:11
  27.0 8.1 %collective-permute-start.4 = (bf16[512,128]{1,0:T(8,128)(2,1)S(1)}, bf16[512,128]{1,0:T(8,128)(2,1)S(1)}, u32[]{:S(2)}, u32[]{:S(2)}) collective-permute-start(bf16[512,128]{1,0:T(8,128)(2,1)S(1)} %collective-permute-done.2), channel_id=1, source_target_pairs={{0,32},{32,64},{64,96},{96,128},{128,160},{160,192},{192,224},{224... | collective-permute-start | bytes 393224 | tf_op jit(solution)/shard_map/ppermute | solution.py:64
  28.9 8.1 %collective-permute-start.5 = (bf16[512,128]{1,0:T(8,128)(2,1)S(1)}, bf16[512,128]{1,0:T(8,128)(2,1)S(1)}, u32[]{:S(2)}, u32[]{:S(2)}) collective-permute-start(bf16[512,128]{1,0:T(8,128)(2,1)S(1)} %collective-permute-done.3), channel_id=1, source_target_pairs={{0,480},{32,0},{64,32},{96,64},{128,96},{160,128},{192,160},{224,1... | collective-permute-start | bytes 393224 | tf_op jit(solution)/shard_map/ppermute | solution.py:68
  35.0 8.1 %collective-permute-start.6 = (bf16[512,128]{1,0:T(8,128)(2,1)S(1)}, bf16[512,128]{1,0:T(8,128)(2,1)S(1)}, u32[]{:S(2)}, u32[]{:S(2)}) collective-permute-start(bf16[512,128]{1,0:T(8,128)(2,1)S(1)} %collective-permute-done.4), channel_id=1, source_target_pairs={{0,32},{32,64},{64,96},{96,128},{128,160},{160,192},{192,224},{224... | collective-permute-start | bytes 393224 | tf_op jit(solution)/shard_map/ppermute | solution.py:64
  37.0 8.1 %collective-permute-start.7 = (bf16[512,128]{1,0:T(8,128)(2,1)S(1)}, bf16[512,128]{1,0:T(8,128)(2,1)S(1)}, u32[]{:S(2)}, u32[]{:S(2)}) collective-permute-start(bf16[512,128]{1,0:T(8,128)(2,1)S(1)} %collective-permute-done.5), channel_id=1, source_target_pairs={{0,480},{32,0},{64,32},{96,64},{128,96},{160,128},{192,160},{224,1... | collective-permute-start | bytes 393224 | tf_op jit(solution)/shard_map/ppermute | solution.py:68
  43.1 9.5 %collective-permute-start.8 = (bf16[512,128]{1,0:T(8,128)(2,1)S(1)}, bf16[512,128]{1,0:T(8,128)(2,1)S(1)}, u32[]{:S(2)}, u32[]{:S(2)}) collective-permute-start(bf16[512,128]{1,0:T(8,128)(2,1)S(1)} %collective-permute-done.6), channel_id=1, source_target_pairs={{0,32},{32,64},{64,96},{96,128},{128,160},{160,192},{192,224},{224... | collective-permute-start | bytes 393224 | tf_op jit(solution)/shard_map/ppermute | solution.py:64
  45.1 9.4 %collective-permute-start.9 = (bf16[512,128]{1,0:T(8,128)(2,1)S(1)}, bf16[512,128]{1,0:T(8,128)(2,1)S(1)}, u32[]{:S(2)}, u32[]{:S(2)}) collective-permute-start(bf16[512,128]{1,0:T(8,128)(2,1)S(1)} %collective-permute-done.7), channel_id=1, source_target_pairs={{0,480},{32,0},{64,32},{96,64},{128,96},{160,128},{192,160},{224,1... | collective-permute-start | bytes 393224 | tf_op jit(solution)/shard_map/ppermute | solution.py:68
  52.6 8.8 %collective-permute-start.10 = (bf16[512,128]{1,0:T(8,128)(2,1)S(1)}, bf16[512,128]{1,0:T(8,128)(2,1)S(1)}, u32[]{:S(2)}, u32[]{:S(2)}) collective-permute-start(bf16[512,128]{1,0:T(8,128)(2,1)S(1)} %collective-permute-done.8), channel_id=1, source_target_pairs={{0,32},{32,64},{64,96},{96,128},{128,160},{160,192},{192,224},{224... | collective-permute-start | bytes 393224 | tf_op jit(solution)/shard_map/ppermute | solution.py:64
  54.5 8.8 %collective-permute-start.11 = (bf16[512,128]{1,0:T(8,128)(2,1)S(1)}, bf16[512,128]{1,0:T(8,128)(2,1)S(1)}, u32[]{:S(2)}, u32[]{:S(2)}) collective-permute-start(bf16[512,128]{1,0:T(8,128)(2,1)S(1)} %collective-permute-done.9), channel_id=1, source_target_pairs={{0,480},{32,0},{64,32},{96,64},{128,96},{160,128},{192,160},{224,1... | collective-permute-start | bytes 393224 | tf_op jit(solution)/shard_map/ppermute | solution.py:68
  61.3 9.7 %collective-permute-start.12 = (bf16[512,128]{1,0:T(8,128)(2,1)S(1)}, bf16[512,128]{1,0:T(8,128)(2,1)S(1)}, u32[]{:S(2)}, u32[]{:S(2)}) collective-permute-start(bf16[512,128]{1,0:T(8,128)(2,1)S(1)} %collective-permute-done.10), channel_id=1, source_target_pairs={{0,32},{32,64},{64,96},{96,128},{128,160},{160,192},{192,224},{224... | collective-permute-start | bytes 393224 | tf_op jit(solution)/shard_map/ppermute | solution.py:64
  63.3 9.8 %collective-permute-start.13 = (bf16[512,128]{1,0:T(8,128)(2,1)S(1)}, bf16[512,128]{1,0:T(8,128)(2,1)S(1)}, u32[]{:S(2)}, u32[]{:S(2)}) collective-permute-start(bf16[512,128]{1,0:T(8,128)(2,1)S(1)} %collective-permute-done.11), channel_id=1, source_target_pairs={{0,480},{32,0},{64,32},{96,64},{128,96},{160,128},{192,160},{224,1... | collective-permute-start | bytes 393224 | tf_op jit(solution)/shard_map/ppermute | solution.py:68
  69.0 24.7 %collective-permute-start.1 = (bf16[8,128,768]{2,1,0:T(8,128)(2,1)S(1)}, bf16[8,128,768]{2,1,0:T(8,128)(2,1)S(1)}, u32[]{:S(2)}, u32[]{:S(2)}) collective-permute-start(bf16[8,128,768]{2,1,0:T(8,128)(2,1)S(1)} %pad_maximum_fusion.1), channel_id=1, source_target_pairs={{0,8},{8,0},{16,24},{24,16},{1,9},{9,1},{17,25},{25,17},{2,10},{10... | collective-permute-start | bytes 4718600 | tf_op jit(solution)/shard_map/ppermute | solution.py:11
  71.0 22.8 %copy-start.1 = (bf16[4,128,768]{2,1,0:T(8,128)(2,1)S(1)}, bf16[4,128,768]{2,1,0:T(8,128)(2,1)}, u32[]{:S(2)}) copy-start(bf16[4,128,768]{2,1,0:T(8,128)(2,1)} %copy-done) | copy-start | bytes 2359300
  71.0 10.9 %collective-permute-start.14 = (bf16[512,128]{1,0:T(8,128)(2,1)S(1)}, bf16[512,128]{1,0:T(8,128)(2,1)S(1)}, u32[]{:S(2)}, u32[]{:S(2)}) collective-permute-start(bf16[512,128]{1,0:T(8,128)(2,1)S(1)} %collective-permute-done.12), channel_id=1, source_target_pairs={{0,32},{32,64},{64,96},{96,128},{128,160},{160,192},{192,224},{224... | collective-permute-start | bytes 393224 | tf_op jit(solution)/shard_map/ppermute | solution.py:64
  73.1 10.8 %collective-permute-start.15 = (bf16[512,128]{1,0:T(8,128)(2,1)S(1)}, bf16[512,128]{1,0:T(8,128)(2,1)S(1)}, u32[]{:S(2)}, u32[]{:S(2)}) collective-permute-start(bf16[512,128]{1,0:T(8,128)(2,1)S(1)} %collective-permute-done.13), channel_id=1, source_target_pairs={{0,480},{32,0},{64,32},{96,64},{128,96},{160,128},{192,160},{224,1... | collective-permute-start | bytes 393224 | tf_op jit(solution)/shard_map/ppermute | solution.py:68
  82.0 10.4 %collective-permute-start.16 = (bf16[512,128]{1,0:T(8,128)(2,1)S(1)}, bf16[512,128]{1,0:T(8,128)(2,1)S(1)}, u32[]{:S(2)}, u32[]{:S(2)}) collective-permute-start(bf16[512,128]{1,0:T(8,128)(2,1)S(1)} %collective-permute-done.14), channel_id=1, source_target_pairs={{0,32},{32,64},{64,96},{96,128},{128,160},{160,192},{192,224},{224... | collective-permute-start | bytes 393224 | tf_op jit(solution)/shard_map/ppermute | solution.py:64
  103.1 27.0 %all-to-all-start.1 = ((f32[8,64,768]{2,1,0:T(8,128)}), f32[8,64,768]{2,1,0:T(8,128)}, u32[]{:S(2)}, u32[]{:S(2)}) async-start(f32[8,64,768]{2,1,0:T(8,128)} %bitcast.67), calls=%async_computation.1 | async-start | bytes 3145728 | tf_op jit(solution)/shard_map/all_to_all | solution.py:53
  130.0 24.2 %all-to-all-start = ((f32[8,64,768]{2,1,0:T(8,128)}), f32[8,64,768]{2,1,0:T(8,128)S(1)}, u32[]{:S(2)}, u32[]{:S(2)}) async-start(f32[8,64,768]{2,1,0:T(8,128)} %bitcast.9), calls=%async_computation | async-start | bytes 3145728 | tf_op jit(solution)/shard_map/all_to_all | solution.py:53
  (3 other events, 27.6 us)
Sparse Core Ops, SparseCore 0:
  27.0 73.7 all-gather.1

commit v8 on v6

--- a/solution.py
+++ b/solution.py
@@ -1,7 +1,7 @@
 import jax
 import jax.numpy as jnp
 from jax import lax
-from jax.sharding import PartitionSpec as P
+from jax.sharding import Mesh, PartitionSpec as P
 
 BS = 128
 
@@ -33,8 +33,12 @@
     near = swap_with(pair, "col", 1)
     sign_four = jnp.concatenate([pair, near], axis=0)
     me = lax.axis_index("col")
-    ks_whole = lax.all_gather(ks_panel, "row", axis=0, tiled=False)
-    inner_of = jnp.arange(lax.axis_size("row"), dtype=jnp.int32)
+    near_count = lax.axis_size("near")
+    far_count = lax.axis_size("far")
+    ks_whole = lax.all_gather(ks_panel, "far", axis=0, tiled=False)
+    ks_whole = lax.all_gather(ks_whole, "near", axis=0, tiled=True)
+    spots = jnp.arange(near_count * far_count, dtype=jnp.int32)
+    inner_of = (spots % far_count) * near_count + spots // far_count
     flipped = (inner_of // local_groups) ^ me
     spot = (flipped % 2) * 2 + flipped // 2
     sign_four = jnp.take(sign_four, spot * local_groups + inner_of % local_groups, axis=0, mode="clip")
@@ -53,15 +57,22 @@
 
 
 def solution(mesh):
+    rows, cols, depths = mesh.devices.shape
+    near_count = 2
+    split_mesh = Mesh(
+        mesh.devices.reshape(rows // near_count, near_count, cols, depths),
+        ("far", "near", "col", "depth"),
+    )
+    row = ("far", "near")
     in_specs = (
-        P("col", ("row", "depth")),
-        P("col", "depth", None, "row"),
-        P("col", ("row", "depth")),
-        P("col", "depth", None, "row"),
-        P("col", "row"),
+        P("col", (*row, "depth")),
+        P("col", "depth", None, row),
+        P("col", (*row, "depth")),
+        P("col", "depth", None, row),
+        P("col", row),
         P("col", None),
     )
-    out_specs = P(("col", "depth"), "row")
+    out_specs = P(("col", "depth"), row)
     return jax.shard_map(
-        per_device, mesh=mesh, in_specs=in_specs, out_specs=out_specs, check_vma=False
+        per_device, mesh=split_mesh, in_specs=in_specs, out_specs=out_specs, check_vma=False
     )

time: 144 us -> 203 us (1.41)
  waiting for transfers between devices: 92.8 us -> 158 us
  starting transfers between devices: 14.7 us -> 10.2 us
    all_gather x1 -> x2, waiting for transfers between devices: 47.8 us -> 101 us  [the longest x1 67.6 us: per_device(): ks_whole = lax.all_gather(ks_panel, 'far', axis=0, tiled=False)]
    all_to_all x1, waiting for transfers between devices: 26.7 us -> 34.9 us  [per_device(): arrived = lax.all_to_all(parts, 'depth', 0, 0, tiled=True)]
    ppermute x2, starting transfers between devices: 9.7 us -> 5.08 us  [swap_with(): return lax.ppermute(block, axis, [(i, i ^ flip) for i in devices])]
    ppermute x2, waiting for transfers between devices: 18.3 us -> 22.2 us  [swap_with(): return lax.ppermute(block, axis, [(i, i ^ flip) for i in devices])]
  transfers between devices with their start and end apart: 4 -> 5, of which waited for: 4 -> 5; matrix products, arithmetic and copies ran while one was open for 6% -> 3% of each run, Pallas kernels for 0% -> 0%
where the time goes in v8:
time: 203 us; the launch traced here: 202 us
  waiting for transfers between devices  158 us (78%)
  between operations  15.4 us (8%)
  starting transfers between devices  10.2 us (5%)
  matrix products  7.28 us (4%)
  other arithmetic  6.41 us (3%)
  local copies, waits for them, and re-layouts  5.22 us (3%)
    all_gather x1, waiting for transfers between devices, per_device(): ks_whole = lax.all_gather(ks_panel, 'far', axis=0, tiled=False)  67.6 us
    all_to_all x1, waiting for transfers between devices, per_device(): arrived = lax.all_to_all(parts, 'depth', 0, 0, tiled=True)  34.9 us
    all_gather x1, waiting for transfers between devices, per_device(): ks_whole = lax.all_gather(ks_whole, 'near', axis=0, tiled=True)  33.2 us
    ppermute x2, waiting for transfers between devices, swap_with(): return lax.ppermute(block, axis, [(i, i ^ flip) for i in devices])  22.2 us
    dot_general x1, matrix products, per_device(): jnp.einsum('sik,skn->in', ks_whole, sign_four, preferred_element_type=jnp...  7.28 us
    ppermute x2, starting transfers between devices, swap_with(): return lax.ppermute(block, axis, [(i, i ^ flip) for i in devices])  5.08 us
    all_to_all x1, starting transfers between devices, per_device(): arrived = lax.all_to_all(parts, 'depth', 0, 0, tiled=True)  5.03 us
  transfers between devices with their start and end apart: 5, of which 5 were waited for; matrix products, arithmetic and copies ran while one was open for 3% of the time, Pallas kernels for 0%

profile of v8, /device:TPU:4, one launch (start us, length us, event | category | flops | bytes accessed | tf_op | source)
XLA Modules:
  0.0 202.5 jit_solution(12575476235313619693)
XLA Ops:
  6.5 0.7 convert_bitcast_fusion.1
  7.3 0.7 pad_clamp_fusion.1
  7.9 1.0 multiply_bitcast_fusion
  9.0 1.3 gather_fusion
  10.3 67.6 %all-gather.3.cloned.1.call-done = bf16[8,1024,128]{2,1,0:T(8,128)(2,1)} async-done(((bf16[1,1024,128]{2,1,0:T(8,128)(2,1)}), bf16[8,1024,128]{2,1,0:T(8,128)(2,1)}) %all-gather.3.cloned.1.call-update) | async-done | bytes 2097168 | tf_op jit(solution)/shard_map/all_gather | solution.py:38
  78.0 0.1 broadcast_bitcast_fusion
  78.1 0.1 bitcast_multiply_fusion
  78.2 3.2 %collective-permute-start = (bf16[4,128,768]{2,1,0:T(8,128)(2,1)S(1)}, bf16[4,128,768]{2,1,0:T(8,128)(2,1)S(1)}, u32[]{:S(2)}, u32[]{:S(2)}) collective-permute-start(bf16[4,128,768]{2,1,0:T(8,128)(2,1)S(1)} %bitcast_multiply_fusion), channel_id=1, source_target_pairs={{0,16},{8,24},{16,0},{24,8},{1,17},{9,25},{17,1},{25,9},{2,18},{10... | collective-permute-start | bytes 2359304 | tf_op jit(solution)/shard_map/ppermute | solution.py:11
  81.4 18.7 %collective-permute-done = bf16[4,128,768]{2,1,0:T(8,128)(2,1)S(1)} collective-permute-done((bf16[4,128,768]{2,1,0:T(8,128)(2,1)S(1)}, bf16[4,128,768]{2,1,0:T(8,128)(2,1)S(1)}, u32[]{:S(2)}, u32[]{:S(2)}) %collective-permute-start) | collective-permute-done | bytes 786464 | tf_op jit(solution)/shard_map/ppermute | solution.py:11
  100.1 0.1 pad_maximum_fusion.1
  100.2 0.7 copy-done.1
  101.0 1.9 collective-permute-start.1
  102.9 3.5 %collective-permute-done.1 = bf16[8,128,768]{2,1,0:T(8,128)(2,1)} collective-permute-done((bf16[8,128,768]{2,1,0:T(8,128)(2,1)S(1)}, bf16[8,128,768]{2,1,0:T(8,128)(2,1)}, u32[]{:S(2)}, u32[]{:S(2)}) %collective-permute-start.1) | collective-permute-done | bytes 1572896 | tf_op jit(solution)/shard_map/ppermute | solution.py:11
  106.4 2.1 %pad_maximum_fusion = bf16[16,128,768]{2,1,0:T(8,128)(2,1)S(1)} fusion(bf16[8,128,768]{2,1,0:T(8,128)(2,1)} %collective-permute-done.1, bf16[4,128,768]{2,1,0:T(8,128)(2,1)} %copy-done.1, bf16[4,128,768]{2,1,0:T(8,128)(2,1)} %copy-done), kind=kLoop, calls=%fused_computation.2 | loop fusion | flops 3145728 | bytes 6291456 | tf_op jit(solution)/shard_map/concatenate | solution.py:34
  108.6 2.4 %gather_fusion.1 = bf16[16,128,768]{2,1,0:T(8,128)(2,1)} fusion(bf16[16,128,768]{2,1,0:T(8,128)(2,1)S(1)} %pad_maximum_fusion, s32[1024]{0:T(1024)S(1)} %pad_clamp_fusion), kind=kCustom, calls=%fused_computation.1 | custom fusion | bytes 6291520 | tf_op jit(solution)/shard_map/jit(_take)/gather | solution.py:44
  111.0 33.2 %all-gather.5.cloned.1.call-done = bf16[16,1024,128]{2,1,0:T(8,128)(2,1)} async-done(((bf16[8,1024,128]{2,1,0:T(8,128)(2,1)}), bf16[16,1024,128]{2,1,0:T(8,128)(2,1)}) %all-gather.5.cloned.1.call-update) | async-done | bytes 4194320 | tf_op jit(solution)/shard_map/all_gather | solution.py:39
  144.2 7.3 %fusion.6 = f32[1024,768,1]{1,0,2:T(8,128)} fusion(bf16[16,1024,128]{2,1,0:T(8,128)(2,1)} %all-gather.5.cloned.1.call-done, bf16[16,128,768]{2,1,0:T(8,128)(2,1)} %gather_fusion.1), kind=kOutput, calls=%fused_computation.37 | convolution fusion | flops 3221225472 | bytes 10485760 | tf_op jit(solution)/shard_map/sik,skn->in/dot_general | solution.py:45
  151.5 5.0 %all-to-all-start = ((f32[8,128,768]{2,1,0:T(8,128)}), f32[8,128,768]{2,1,0:T(8,128)S(1)}, u32[]{:S(2)}, u32[]{:S(2)}) async-start(f32[8,128,768]{2,1,0:T(8,128)} %bitcast.29), calls=%async_computation | async-start | bytes 6291456 | tf_op jit(solution)/shard_map/all_to_all | solution.py:49
  156.5 0.6 constant_dynamic-slice_fusion
  159.0 0.7 convert_bitcast_fusion
  159.7 0.1 broadcast_bitcast_fusion.1
  159.8 34.9 %all-to-all-done = f32[8,128,768]{2,1,0:T(8,128)S(1)} async-done(((f32[8,128,768]{2,1,0:T(8,128)}), f32[8,128,768]{2,1,0:T(8,128)S(1)}, u32[]{:S(2)}, u32[]{:S(2)}) %all-to-all-start) | async-done | bytes 3145760 | tf_op jit(solution)/shard_map/all_to_all | solution.py:49
  194.7 0.2 reduce_sum.9
  194.9 0.7 multiply_convert_fusion
  (18 shorter events, 0.1 us)
Async XLA Ops:
  6.5 71.5 %copy-start.3 = (s32[4,1,1,6]{3,2,1,0:T(1,128)S(1)}, s32[4,1,1,6]{3,2,1,0:T(1,128)}, u32[]{:S(2)}) copy-start(s32[4,1,1,6]{3,2,1,0:T(1,128)} %param.9) | copy-start | bytes 292
  6.5 71.6 %copy-start.2 = (bf16[4,1,128,768]{3,2,1,0:T(8,128)(2,1)S(1)}, bf16[4,1,128,768]{3,2,1,0:T(8,128)(2,1)}, u32[]{:S(2)}) copy-start(bf16[4,1,128,768]{3,2,1,0:T(8,128)(2,1)} %param.7) | copy-start | bytes 2359300
  6.5 71.4 %all-gather.3.cloned.1.call-start = ((), (), s32[]{:S(2)}) async-start(), calls=%async_computation.1 | async-start | bytes 2359296 | tf_op jit(solution)/shard_map/all_gather | solution.py:38
  10.3 133.9 %all-gather.5.cloned.1.call-start = ((), (), s32[]{:S(2)}) async-start(), calls=%async_computation.2 | async-start | bytes 6291456 | tf_op jit(solution)/shard_map/all_gather | solution.py:39
  78.2 21.9 %copy-start = (bf16[4,128,768]{2,1,0:T(8,128)(2,1)}, bf16[4,128,768]{2,1,0:T(8,128)(2,1)S(1)}, u32[]{:S(2)}) copy-start(bf16[4,128,768]{2,1,0:T(8,128)(2,1)S(1)} %bitcast_multiply_fusion) | copy-start | bytes 2359300
  78.2 21.9 %collective-permute-start = (bf16[4,128,768]{2,1,0:T(8,128)(2,1)S(1)}, bf16[4,128,768]{2,1,0:T(8,128)(2,1)S(1)}, u32[]{:S(2)}, u32[]{:S(2)}) collective-permute-start(bf16[4,128,768]{2,1,0:T(8,128)(2,1)S(1)} %bitcast_multiply_fusion), channel_id=1, source_target_pairs={{0,16},{8,24},{16,0},{24,8},{1,17},{9,25},{17,1},{25,9},{2,18},{10... | collective-permute-start | bytes 2359304 | tf_op jit(solution)/shard_map/ppermute | solution.py:11
  100.1 0.9 copy-start.1
  101.0 5.4 %collective-permute-start.1 = (bf16[8,128,768]{2,1,0:T(8,128)(2,1)S(1)}, bf16[8,128,768]{2,1,0:T(8,128)(2,1)}, u32[]{:S(2)}, u32[]{:S(2)}) collective-permute-start(bf16[8,128,768]{2,1,0:T(8,128)(2,1)S(1)} %pad_maximum_fusion.1), channel_id=1, source_target_pairs={{0,8},{8,0},{16,24},{24,16},{1,9},{9,1},{17,25},{25,17},{2,10},{10... | collective-permute-start | bytes 4718600 | tf_op jit(solution)/shard_map/ppermute | solution.py:11
  151.5 5.0 %copy-start.4 = (s32[1,8]{1,0:T(1,128)S(1)}, s32[1,8]{1,0:T(1,128)}, u32[]{:S(2)}) copy-start(s32[1,8]{1,0:T(1,128)} %param.11) | copy-start | bytes 100
  151.5 43.2 %all-to-all-start = ((f32[8,128,768]{2,1,0:T(8,128)}), f32[8,128,768]{2,1,0:T(8,128)S(1)}, u32[]{:S(2)}, u32[]{:S(2)}) async-start(f32[8,128,768]{2,1,0:T(8,128)} %bitcast.29), calls=%async_computation | async-start | bytes 6291456 | tf_op jit(solution)/shard_map/all_to_all | solution.py:49
Sparse Core Ops, SparseCore 0:
  10.4 67.5 all-gather.2
  80.1 64.0 all-gather.4

commit v9 on v6

--- a/solution.py
+++ b/solution.py
@@ -17,11 +17,10 @@
     sign_inner = sign_mask.shape[2]
     col_blocks = sign_mask.shape[3]
     local_order = row_order[0]
-    ks_panel = (
-        ks_matrix.reshape(row_blocks, BS, inner_blocks, BS)
-        * ks_mask.astype(jnp.bfloat16)[:, None, :, None]
-    )
-    ks_panel = jnp.take(ks_panel, local_order, axis=0, mode="clip")
+    ks_blocks = ks_matrix.reshape(row_blocks, BS, inner_blocks, BS)
+    ks_blocks = jnp.take(ks_blocks, local_order, axis=0, mode="clip")
+    row_mask = jnp.take(ks_mask, local_order, axis=0, mode="clip")
+    ks_panel = ks_blocks * row_mask.astype(jnp.bfloat16)[:, None, :, None]
     ks_panel = ks_panel.reshape(row_blocks * BS, inner_blocks * BS)
     sign_kept = sign_matrix.reshape(local_groups, sign_inner, BS, col_blocks, BS)
     sign_kept = sign_kept * sign_mask.astype(jnp.bfloat16).reshape(
@@ -38,12 +37,19 @@
     flipped = (inner_of // local_groups) ^ me
     spot = (flipped % 2) * 2 + flipped // 2
     sign_four = jnp.take(sign_four, spot * local_groups + inner_of % local_groups, axis=0, mode="clip")
-    product = jnp.einsum(
-        "sik,skn->in", ks_whole, sign_four, preferred_element_type=jnp.float32
-    )
-    parts = product.reshape(row_blocks, BS, col_blocks * BS)
-    arrived = lax.all_to_all(parts, "depth", 0, 0, tiled=True)
-    summed = jnp.sum(arrived, axis=0)
+    halves = []
+    half_cols = col_blocks * BS // 2
+    for half in range(2):
+        product = jnp.einsum(
+            "sik,skn->in",
+            ks_whole,
+            sign_four[:, :, half * half_cols:(half + 1) * half_cols],
+            preferred_element_type=jnp.float32,
+        )
+        parts = product.reshape(row_blocks, BS, half_cols)
+        arrived = lax.all_to_all(parts, "depth", 0, 0, tiled=True)
+        halves.append(jnp.sum(arrived, axis=0))
+    summed = jnp.concatenate(halves, axis=1)
     own_row = lax.dynamic_index_in_dim(
         local_order, lax.axis_index("depth"), 0, keepdims=False
     )

time: 144 us -> 151 us (1.049)
  the two profiles are of different devices: /device:TPU:4 before, /device:TPU:32 now
where the time goes in v9:
time: 151 us; the launch traced here: 150 us
  waiting for transfers between devices  89.2 us (59%)
  starting transfers between devices  18.4 us (12%)
  between operations  15.4 us (10%)
  matrix products  12.4 us (8%)
  other arithmetic  8.98 us (6%)
  local copies, waits for them, and re-layouts  5.91 us (4%)
    all_gather x1, waiting for transfers between devices, per_device(): ks_whole = lax.all_gather(ks_panel, 'row', axis=0, tiled=False)  47.3 us
    ppermute x2, waiting for transfers between devices, swap_with(): return lax.ppermute(block, axis, [(i, i ^ flip) for i in devices])  21.2 us
    all_to_all x2, waiting for transfers between devices, per_device(): arrived = lax.all_to_all(parts, 'depth', 0, 0, tiled=True)  20.7 us
    dot_general x2, matrix products, per_device(): jnp.einsum('sik,skn->in', ks_whole, sign_four[:, :, half * half_cols:(hal...  12.4 us
    all_to_all x2, starting transfers between devices, per_device(): arrived = lax.all_to_all(parts, 'depth', 0, 0, tiled=True)  11.6 us
    ppermute x2, starting transfers between devices, swap_with(): return lax.ppermute(block, axis, [(i, i ^ flip) for i in devices])  6.84 us
  transfers between devices with their start and end apart: 5, of which 5 were waited for; matrix products, arithmetic and copies ran while one was open for 10% of the time, Pallas kernels for 0%

profile of v9, /device:TPU:32, one launch (start us, length us, event | category | flops | bytes accessed | tf_op | source)
XLA Modules:
  0.0 150.3 jit_solution(7288199668519292189)
XLA Ops:
  6.5 0.7 pad_clamp_fusion.1
  7.2 1.3 gather_fusion.1
  8.6 0.6 gather_fusion
  9.2 0.9 bitcast_multiply_fusion.1
  10.2 0.7 convert_element_type.30
  10.9 1.2 bitcast_multiply_fusion
  12.1 4.9 %collective-permute-start = (bf16[4,128,768]{2,1,0:T(8,128)(2,1)S(1)}, bf16[4,128,768]{2,1,0:T(8,128)(2,1)S(1)}, u32[]{:S(2)}, u32[]{:S(2)}) collective-permute-start(bf16[4,128,768]{2,1,0:T(8,128)(2,1)S(1)} %bitcast_multiply_fusion), channel_id=1, source_target_pairs={{0,16},{8,24},{16,0},{24,8},{1,17},{9,25},{17,1},{25,9},{2,18},{10... | collective-permute-start | bytes 2359304 | tf_op jit(solution)/shard_map/ppermute | solution.py:11
  17.1 17.7 %collective-permute-done = bf16[4,128,768]{2,1,0:T(8,128)(2,1)S(1)} collective-permute-done((bf16[4,128,768]{2,1,0:T(8,128)(2,1)S(1)}, bf16[4,128,768]{2,1,0:T(8,128)(2,1)S(1)}, u32[]{:S(2)}, u32[]{:S(2)}) %collective-permute-start) | collective-permute-done | bytes 786464 | tf_op jit(solution)/shard_map/ppermute | solution.py:11
  35.0 0.8 copy-done.2
  35.7 1.9 %collective-permute-start.1 = (bf16[8,128,768]{2,1,0:T(8,128)(2,1)S(1)}, bf16[8,128,768]{2,1,0:T(8,128)(2,1)}, u32[]{:S(2)}, u32[]{:S(2)}) collective-permute-start(bf16[8,128,768]{2,1,0:T(8,128)(2,1)S(1)} %pad_maximum_fusion.1), channel_id=1, source_target_pairs={{0,8},{8,0},{16,24},{24,16},{1,9},{9,1},{17,25},{25,17},{2,10},{10... | collective-permute-start | bytes 4718600 | tf_op jit(solution)/shard_map/ppermute | solution.py:11
  37.7 3.5 %collective-permute-done.1 = bf16[8,128,768]{2,1,0:T(8,128)(2,1)} collective-permute-done((bf16[8,128,768]{2,1,0:T(8,128)(2,1)S(1)}, bf16[8,128,768]{2,1,0:T(8,128)(2,1)}, u32[]{:S(2)}, u32[]{:S(2)}) %collective-permute-start.1) | collective-permute-done | bytes 1572896 | tf_op jit(solution)/shard_map/ppermute | solution.py:11
  41.1 2.2 %pad_maximum_fusion = bf16[16,128,768]{2,1,0:T(8,128)(2,1)S(1)} fusion(bf16[8,128,768]{2,1,0:T(8,128)(2,1)} %collective-permute-done.1, bf16[4,128,768]{2,1,0:T(8,128)(2,1)} %copy-done.2, bf16[4,128,768]{2,1,0:T(8,128)(2,1)} %copy-done.1), kind=kLoop, calls=%fused_computation.3 | loop fusion | flops 3145728 | bytes 6291456 | tf_op jit(solution)/shard_map/concatenate | solution.py:33
  43.3 2.4 %gather_fusion.2 = bf16[16,128,768]{2,1,0:T(8,128)(2,1)} fusion(bf16[16,128,768]{2,1,0:T(8,128)(2,1)S(1)} %pad_maximum_fusion, s32[1024]{0:T(1024)S(1)} %pad_clamp_fusion), kind=kCustom, calls=%fused_computation.2 | custom fusion | bytes 6291520 | tf_op jit(solution)/shard_map/jit(_take)/gather | solution.py:39
  45.7 47.3 %all-gather.2.cloned.1.call-done = bf16[16,1024,128]{2,1,0:T(8,128)(2,1)} async-done(((bf16[1,1024,128]{2,1,0:T(8,128)(2,1)}), bf16[16,1024,128]{2,1,0:T(8,128)(2,1)}) %all-gather.2.cloned.1.call-update) | async-done | bytes 4194320 | tf_op jit(solution)/shard_map/all_gather | solution.py:35
  93.1 6.1 %fusion.2 = f32[1024,384,1]{1,0,2:T(8,128)} fusion(bf16[16,1024,128]{2,1,0:T(8,128)(2,1)} %all-gather.2.cloned.1.call-done, bf16[16,128,768]{2,1,0:T(8,128)(2,1)} %gather_fusion.2), kind=kOutput, calls=%fused_computation.6 | convolution fusion | flops 1610612736 | bytes 7340032 | tf_op jit(solution)/shard_map/sik,skn->in/dot_general | solution.py:43
  99.2 5.2 %all-to-all-start = ((f32[8,128,384]{2,1,0:T(8,128)}), f32[8,128,384]{2,1,0:T(8,128)S(1)}, u32[]{:S(2)}, u32[]{:S(2)}) async-start(f32[8,128,384]{2,1,0:T(8,128)} %bitcast.8), calls=%async_computation | async-start | bytes 3145728 | tf_op jit(solution)/shard_map/all_to_all | solution.py:50
  104.4 6.2 %fusion = f32[1024,384,1]{1,0,2:T(8,128)} fusion(bf16[16,1024,128]{2,1,0:T(8,128)(2,1)} %all-gather.2.cloned.1.call-done, bf16[16,128,768]{2,1,0:T(8,128)(2,1)} %gather_fusion.2), kind=kOutput, calls=%fused_computation.4 | convolution fusion | flops 1610612736 | bytes 7340032 | tf_op jit(solution)/shard_map/sik,skn->in/dot_general | solution.py:43
  110.6 10.4 %all-to-all-done = f32[8,128,384]{2,1,0:T(8,128)S(1)} async-done(((f32[8,128,384]{2,1,0:T(8,128)}), f32[8,128,384]{2,1,0:T(8,128)S(1)}, u32[]{:S(2)}, u32[]{:S(2)}) %all-to-all-start) | async-done | bytes 1572896 | tf_op jit(solution)/shard_map/all_to_all | solution.py:50
  121.0 6.4 %all-to-all-start.1 = ((f32[8,128,384]{2,1,0:T(8,128)}), f32[8,128,384]{2,1,0:T(8,128)S(1)}, u32[]{:S(2)}, u32[]{:S(2)}) async-start(f32[8,128,384]{2,1,0:T(8,128)} %bitcast.35), calls=%async_computation.1 | async-start | bytes 3145728 | tf_op jit(solution)/shard_map/all_to_all | solution.py:50
  127.4 0.6 constant_dynamic-slice_fusion
  130.0 0.7 convert_bitcast_fusion
  130.7 0.8 reduce_sum.18
  131.5 10.3 %all-to-all-done.1 = f32[8,128,384]{2,1,0:T(8,128)S(1)} async-done(((f32[8,128,384]{2,1,0:T(8,128)}), f32[8,128,384]{2,1,0:T(8,128)S(1)}, u32[]{:S(2)}, u32[]{:S(2)}) %all-to-all-start.1) | async-done | bytes 1572896 | tf_op jit(solution)/shard_map/all_to_all | solution.py:50
  141.9 1.6 %fusion.4 = bf16[128,768]{1,0:T(8,128)(2,1)} fusion(f32[128,384]{1,0:T(8,128)S(1)} %reduce_sum.19, f32[128,384]{1,0:T(8,128)} %reduce_sum.18, f32[768]{0:T(1024)S(1)} %broadcast_bitcast_fusion.1), kind=kLoop, calls=%fused_computation.11 | loop fusion | flops 294912 | bytes 592896 | tf_op jit(solution)/shard_map/convert_element_type | solution.py:58
  (19 shorter events, 0.5 us)
Async XLA Ops:
  6.5 2.1 %copy-start = (bf16[1024,128]{1,0:T(8,128)(2,1)S(1)}, bf16[1024,128]{1,0:T(8,128)(2,1)}, u32[]{:S(2)}) copy-start(bf16[1024,128]{1,0:T(8,128)(2,1)} %param.6) | copy-start | bytes 786436
  6.5 86.5 %all-gather.2.cloned.1.call-start = ((), (), s32[]{:S(2)}) async-start(), calls=%async_computation.2 | async-start | bytes 4456448 | tf_op jit(solution)/shard_map/all_gather | solution.py:35
  12.1 22.7 %copy-start.1 = (bf16[4,128,768]{2,1,0:T(8,128)(2,1)}, bf16[4,128,768]{2,1,0:T(8,128)(2,1)S(1)}, u32[]{:S(2)}) copy-start(bf16[4,128,768]{2,1,0:T(8,128)(2,1)S(1)} %bitcast_multiply_fusion) | copy-start | bytes 2359300
  12.1 22.7 %collective-permute-start = (bf16[4,128,768]{2,1,0:T(8,128)(2,1)S(1)}, bf16[4,128,768]{2,1,0:T(8,128)(2,1)S(1)}, u32[]{:S(2)}, u32[]{:S(2)}) collective-permute-start(bf16[4,128,768]{2,1,0:T(8,128)(2,1)S(1)} %bitcast_multiply_fusion), channel_id=1, source_target_pairs={{0,16},{8,24},{16,0},{24,8},{1,17},{9,25},{17,1},{25,9},{2,18},{10... | collective-permute-start | bytes 2359304 | tf_op jit(solution)/shard_map/ppermute | solution.py:11
  34.8 0.9 copy-start.2
  35.7 5.4 %collective-permute-start.1 = (bf16[8,128,768]{2,1,0:T(8,128)(2,1)S(1)}, bf16[8,128,768]{2,1,0:T(8,128)(2,1)}, u32[]{:S(2)}, u32[]{:S(2)}) collective-permute-start(bf16[8,128,768]{2,1,0:T(8,128)(2,1)S(1)} %pad_maximum_fusion.1), channel_id=1, source_target_pairs={{0,8},{8,0},{16,24},{24,16},{1,9},{9,1},{17,25},{25,17},{2,10},{10... | collective-permute-start | bytes 4718600 | tf_op jit(solution)/shard_map/ppermute | solution.py:11
  99.2 21.8 %all-to-all-start = ((f32[8,128,384]{2,1,0:T(8,128)}), f32[8,128,384]{2,1,0:T(8,128)S(1)}, u32[]{:S(2)}, u32[]{:S(2)}) async-start(f32[8,128,384]{2,1,0:T(8,128)} %bitcast.8), calls=%async_computation | async-start | bytes 3145728 | tf_op jit(solution)/shard_map/all_to_all | solution.py:50
  110.6 16.8 %copy-start.3 = (s32[1,8]{1,0:T(1,128)S(1)}, s32[1,8]{1,0:T(1,128)}, u32[]{:S(2)}) copy-start(s32[1,8]{1,0:T(1,128)} %param.11) | copy-start | bytes 100
  121.0 20.7 %all-to-all-start.1 = ((f32[8,128,384]{2,1,0:T(8,128)}), f32[8,128,384]{2,1,0:T(8,128)S(1)}, u32[]{:S(2)}, u32[]{:S(2)}) async-start(f32[8,128,384]{2,1,0:T(8,128)} %bitcast.35), calls=%async_computation.1 | async-start | bytes 3145728 | tf_op jit(solution)/shard_map/all_to_all | solution.py:50
Sparse Core Ops, SparseCore 0:
  10.3 82.7 all-gather.1

commit v10 on v6

--- a/solution.py
+++ b/solution.py
@@ -33,13 +33,15 @@
     near = swap_with(pair, "col", 1)
     sign_four = jnp.concatenate([pair, near], axis=0)
     me = lax.axis_index("col")
-    ks_whole = lax.all_gather(ks_panel, "row", axis=0, tiled=False)
+    ks_whole = lax.all_gather(ks_panel, "row", axis=1, tiled=True)
     inner_of = jnp.arange(lax.axis_size("row"), dtype=jnp.int32)
     flipped = (inner_of // local_groups) ^ me
     spot = (flipped % 2) * 2 + flipped // 2
     sign_four = jnp.take(sign_four, spot * local_groups + inner_of % local_groups, axis=0, mode="clip")
-    product = jnp.einsum(
-        "sik,skn->in", ks_whole, sign_four, preferred_element_type=jnp.float32
+    product = jnp.dot(
+        ks_whole,
+        sign_four.reshape(-1, col_blocks * BS),
+        preferred_element_type=jnp.float32,
     )
     parts = product.reshape(row_blocks, BS, col_blocks * BS)
     arrived = lax.all_to_all(parts, "depth", 0, 0, tiled=True)

time: 144 us -> 161 us (1.12)
  the two profiles are of different devices: /device:TPU:4 before, /device:TPU:32 now
where the time goes in v10:
time: 161 us; the launch traced here: 160 us
  waiting for transfers between devices  110 us (68%)
  between operations  15.4 us (10%)
  starting transfers between devices  12.9 us (8%)
  matrix products  8.28 us (5%)
  other arithmetic  8.14 us (5%)
  local copies, waits for them, and re-layouts  5.2 us (3%)
    all_gather x1, waiting for transfers between devices, per_device(): ks_whole = lax.all_gather(ks_panel, 'row', axis=1, tiled=True)  64.1 us
    all_to_all x1, waiting for transfers between devices, per_device(): arrived = lax.all_to_all(parts, 'depth', 0, 0, tiled=True)  24.9 us
    ppermute x2, waiting for transfers between devices, swap_with(): return lax.ppermute(block, axis, [(i, i ^ flip) for i in devices])  21.2 us
    dot_general x1, matrix products, per_device(): jnp.dot(ks_whole, sign_four.reshape(-1, col_blocks * BS), preferred_eleme...  8.28 us
    ppermute x2, starting transfers between devices, swap_with(): return lax.ppermute(block, axis, [(i, i ^ flip) for i in devices])  6.84 us
    all_to_all x1, starting transfers between devices, per_device(): arrived = lax.all_to_all(parts, 'depth', 0, 0, tiled=True)  6.07 us
  transfers between devices with their start and end apart: 4, of which 4 were waited for; matrix products, arithmetic and copies ran while one was open for 5% of the time, Pallas kernels for 0%

profile of v10, /device:TPU:32, one launch (start us, length us, event | category | flops | bytes accessed | tf_op | source)
XLA Modules:
  0.0 160.2 jit_solution(598620229438126589)
XLA Ops:
  6.5 0.7 convert_bitcast_fusion.1
  7.2 0.7 pad_clamp_fusion.1
  7.9 1.0 multiply_bitcast_fusion
  8.9 1.3 gather_fusion
  10.2 0.7 convert_element_type.20
  10.9 0.1 broadcast_bitcast_fusion
  11.0 1.2 bitcast_multiply_fusion
  12.2 4.9 %collective-permute-start = (bf16[4,128,768]{2,1,0:T(8,128)(2,1)S(1)}, bf16[4,128,768]{2,1,0:T(8,128)(2,1)S(1)}, u32[]{:S(2)}, u32[]{:S(2)}) collective-permute-start(bf16[4,128,768]{2,1,0:T(8,128)(2,1)S(1)} %bitcast_multiply_fusion), channel_id=1, source_target_pairs={{0,16},{8,24},{16,0},{24,8},{1,17},{9,25},{17,1},{25,9},{2,18},{10... | collective-permute-start | bytes 2359304 | tf_op jit(solution)/shard_map/ppermute | solution.py:11
  17.1 17.7 %collective-permute-done = bf16[4,128,768]{2,1,0:T(8,128)(2,1)S(1)} collective-permute-done((bf16[4,128,768]{2,1,0:T(8,128)(2,1)S(1)}, bf16[4,128,768]{2,1,0:T(8,128)(2,1)S(1)}, u32[]{:S(2)}, u32[]{:S(2)}) %collective-permute-start) | collective-permute-done | bytes 786464 | tf_op jit(solution)/shard_map/ppermute | solution.py:11
  34.9 0.1 pad_maximum_fusion.1
  35.0 0.8 copy-done.1
  35.8 1.9 %collective-permute-start.1 = (bf16[8,128,768]{2,1,0:T(8,128)(2,1)S(1)}, bf16[8,128,768]{2,1,0:T(8,128)(2,1)}, u32[]{:S(2)}, u32[]{:S(2)}) collective-permute-start(bf16[8,128,768]{2,1,0:T(8,128)(2,1)S(1)} %pad_maximum_fusion.1), channel_id=1, source_target_pairs={{0,8},{8,0},{16,24},{24,16},{1,9},{9,1},{17,25},{25,17},{2,10},{10... | collective-permute-start | bytes 4718600 | tf_op jit(solution)/shard_map/ppermute | solution.py:11
  37.7 3.5 %collective-permute-done.1 = bf16[8,128,768]{2,1,0:T(8,128)(2,1)} collective-permute-done((bf16[8,128,768]{2,1,0:T(8,128)(2,1)S(1)}, bf16[8,128,768]{2,1,0:T(8,128)(2,1)}, u32[]{:S(2)}, u32[]{:S(2)}) %collective-permute-start.1) | collective-permute-done | bytes 1572896 | tf_op jit(solution)/shard_map/ppermute | solution.py:11
  41.2 2.1 %pad_maximum_fusion = bf16[16,128,768]{2,1,0:T(8,128)(2,1)S(1)} fusion(bf16[8,128,768]{2,1,0:T(8,128)(2,1)} %collective-permute-done.1, bf16[4,128,768]{2,1,0:T(8,128)(2,1)} %copy-done.1, bf16[4,128,768]{2,1,0:T(8,128)(2,1)} %copy-done), kind=kLoop, calls=%fused_computation.2 | loop fusion | flops 3145728 | bytes 6291456 | tf_op jit(solution)/shard_map/concatenate | solution.py:34
  43.3 2.4 %gather_fusion.1 = bf16[16,128,768]{2,1,0:T(8,128)(2,1)} fusion(bf16[16,128,768]{2,1,0:T(8,128)(2,1)S(1)} %pad_maximum_fusion, s32[1024]{0:T(1024)S(1)} %pad_clamp_fusion), kind=kCustom, calls=%fused_computation.1 | custom fusion | bytes 6291520 | tf_op jit(solution)/shard_map/jit(_take)/gather | solution.py:40
  45.8 64.1 %all-gather.2.cloned.1.call-done = bf16[1024,2048]{1,0:T(8,128)(2,1)} async-done(((bf16[1024,128]{1,0:T(8,128)(2,1)}), bf16[1024,2048]{1,0:T(8,128)(2,1)}) %all-gather.2.cloned.1.call-update) | async-done | bytes 4194320 | tf_op jit(solution)/shard_map/all_gather | solution.py:36
  109.9 8.3 %fusion.5 = f32[8,128,768]{2,1,0:T(8,128)} fusion(bf16[8,128,2048]{2,1,0:T(8,128)(2,1)} %bitcast.36, bf16[2048,768,1]{1,0,2:T(8,128)(2,1)} %bitcast.30), kind=kOutput, calls=%fused_computation.31 | convolution fusion | flops 3221225472 | bytes 10485760 | tf_op jit(solution)/shard_map/dot_general | solution.py:41
  118.2 6.1 %all-to-all-start = ((f32[8,128,768]{2,1,0:T(8,128)}), f32[8,128,768]{2,1,0:T(8,128)S(1)}, u32[]{:S(2)}, u32[]{:S(2)}) async-start(f32[8,128,768]{2,1,0:T(8,128)} %fusion.5), calls=%async_computation | async-start | bytes 6291456 | tf_op jit(solution)/shard_map/all_to_all | solution.py:47
  124.2 0.6 constant_dynamic-slice_fusion
  126.8 0.7 convert_bitcast_fusion
  127.5 0.1 broadcast_bitcast_fusion.1
  127.5 24.9 %all-to-all-done = f32[8,128,768]{2,1,0:T(8,128)S(1)} async-done(((f32[8,128,768]{2,1,0:T(8,128)}), f32[8,128,768]{2,1,0:T(8,128)S(1)}, u32[]{:S(2)}, u32[]{:S(2)}) %all-to-all-start) | async-done | bytes 3145760 | tf_op jit(solution)/shard_map/all_to_all | solution.py:47
  152.4 0.2 reduce_sum.9
  152.6 0.7 multiply_convert_fusion
  (11 shorter events, 0.1 us)
Async XLA Ops:
  6.5 103.3 %all-gather.2.cloned.1.call-start = ((), (), s32[]{:S(2)}) async-start(), calls=%async_computation.1 | async-start | bytes 4456448 | tf_op jit(solution)/shard_map/all_gather | solution.py:36
  12.2 22.7 %copy-start = (bf16[4,128,768]{2,1,0:T(8,128)(2,1)}, bf16[4,128,768]{2,1,0:T(8,128)(2,1)S(1)}, u32[]{:S(2)}) copy-start(bf16[4,128,768]{2,1,0:T(8,128)(2,1)S(1)} %bitcast_multiply_fusion) | copy-start | bytes 2359300
  12.2 22.7 %collective-permute-start = (bf16[4,128,768]{2,1,0:T(8,128)(2,1)S(1)}, bf16[4,128,768]{2,1,0:T(8,128)(2,1)S(1)}, u32[]{:S(2)}, u32[]{:S(2)}) collective-permute-start(bf16[4,128,768]{2,1,0:T(8,128)(2,1)S(1)} %bitcast_multiply_fusion), channel_id=1, source_target_pairs={{0,16},{8,24},{16,0},{24,8},{1,17},{9,25},{17,1},{25,9},{2,18},{10... | collective-permute-start | bytes 2359304 | tf_op jit(solution)/shard_map/ppermute | solution.py:11
  34.9 0.9 copy-start.1
  35.8 5.4 %collective-permute-start.1 = (bf16[8,128,768]{2,1,0:T(8,128)(2,1)S(1)}, bf16[8,128,768]{2,1,0:T(8,128)(2,1)}, u32[]{:S(2)}, u32[]{:S(2)}) collective-permute-start(bf16[8,128,768]{2,1,0:T(8,128)(2,1)S(1)} %pad_maximum_fusion.1), channel_id=1, source_target_pairs={{0,8},{8,0},{16,24},{24,16},{1,9},{9,1},{17,25},{25,17},{2,10},{10... | collective-permute-start | bytes 4718600 | tf_op jit(solution)/shard_map/ppermute | solution.py:11
  118.1 6.1 %copy-start.2 = (s32[1,8]{1,0:T(1,128)S(1)}, s32[1,8]{1,0:T(1,128)}, u32[]{:S(2)}) copy-start(s32[1,8]{1,0:T(1,128)} %param.11) | copy-start | bytes 100
  118.2 34.3 %all-to-all-start = ((f32[8,128,768]{2,1,0:T(8,128)}), f32[8,128,768]{2,1,0:T(8,128)S(1)}, u32[]{:S(2)}, u32[]{:S(2)}) async-start(f32[8,128,768]{2,1,0:T(8,128)} %fusion.5), calls=%async_computation | async-start | bytes 6291456 | tf_op jit(solution)/shard_map/all_to_all | solution.py:47
Sparse Core Ops, SparseCore 0:
  10.3 99.5 all-gather.1

commit v11 on v6

v11 whole, which is shorter than its diff:
```python
import jax
import jax.numpy as jnp
from jax import lax
from jax.sharding import Mesh, PartitionSpec as P

BS = 128


def swap_with(block, axis, flip):
    devices = range(lax.axis_size(axis))
    return lax.ppermute(block, axis, [(i, i ^ flip) for i in devices])


def per_device(ks_matrix, sign_matrix, ks_mask, sign_mask, product_mask, row_order):
    row_blocks, inner_blocks = ks_mask.shape
    local_groups = sign_mask.shape[0]
    sign_inner = sign_mask.shape[2]
    col_blocks = sign_mask.shape[3]
    ring_count = lax.axis_size("y")
    pair_count = lax.axis_size("xlo")
    ring_me = lax.axis_index("y")
    pair_me = lax.axis_index("xlo")
    local_order = row_order[0]
    ks_panel = (
        ks_matrix.reshape(row_blocks, BS, inner_blocks, BS)
        * ks_mask.astype(jnp.bfloat16)[:, None, :, None]
    )
    ks_panel = jnp.take(ks_panel, local_order, axis=0, mode="clip")
    ks_split = ks_panel.reshape(ring_count, pair_count, BS, inner_blocks * BS)
    mine = lax.dynamic_index_in_dim(ks_split, pair_me, 1, keepdims=False)
    theirs = lax.dynamic_index_in_dim(ks_split, 1 - pair_me, 1, keepdims=False)
    lent = swap_with(theirs, "xlo", 1)
    payload = jnp.stack([mine, lent])
    payload = payload.reshape(pair_count, ring_count * BS, inner_blocks * BS)
    sign_kept = sign_matrix.reshape(local_groups, sign_inner, BS, col_blocks, BS)
    sign_kept = sign_kept * sign_mask.astype(jnp.bfloat16).reshape(
        local_groups, sign_inner, 1, col_blocks, 1
    )
    sign_kept = sign_kept.reshape(local_groups, sign_inner * BS, col_blocks * BS)
    sign_kept = jnp.stack([sign_kept, swap_with(sign_kept, "xlo", 1)])
    far = swap_with(sign_kept, "col", 2)
    pair = jnp.concatenate([sign_kept, far], axis=1)
    near = swap_with(pair, "col", 1)
    sign_four = jnp.concatenate([pair, near], axis=1)
    me = lax.axis_index("col")
    ks_whole = lax.all_gather(payload, "row", axis=0, tiled=False)
    inner_of = jnp.arange(lax.axis_size("row"), dtype=jnp.int32)
    flipped = (inner_of // local_groups) ^ me
    spot = (flipped % 2) * 2 + flipped // 2
    sign_four = jnp.take(sign_four, spot * local_groups + inner_of % local_groups, axis=1, mode="clip")
    product = jnp.einsum(
        "sjik,jskn->in", ks_whole, sign_four, preferred_element_type=jnp.float32
    )
    parts = product.reshape(ring_count, BS, col_blocks * BS)
    arrived = lax.all_to_all(parts, "y", 0, 0, tiled=True)
    summed = jnp.sum(arrived, axis=0)
    own_row = lax.dynamic_index_in_dim(
        local_order, ring_me * pair_count + pair_me, 0, keepdims=False
    )
    own_mask = lax.dynamic_index_in_dim(product_mask, own_row, 0, keepdims=False)
    kept = summed.reshape(BS, col_blocks, BS) * own_mask.astype(jnp.float32)[None, :, None]
    return kept.reshape(BS, col_blocks * BS).astype(jnp.bfloat16)


def solution(mesh):
    rows, cols, depths = mesh.devices.shape
    pair_count = 2
    split_mesh = Mesh(
        mesh.devices.reshape(rows, cols, depths // pair_count, pair_count),
        ("row", "col", "y", "xlo"),
    )
    depth = ("y", "xlo")
    in_specs = (
        P("col", ("row", *depth)),
        P("col", depth, None, "row"),
        P("col", ("row", *depth)),
        P("col", depth, None, "row"),
        P("col", "row"),
        P("col", None),
    )
    out_specs = P(("col", *depth), "row")
    return jax.shard_map(
        per_device, mesh=split_mesh, in_specs=in_specs, out_specs=out_specs, check_vma=False
    )
```

time: 144 us -> 140 us (0.972)
  the two profiles are of different devices: /device:TPU:4 before, /device:TPU:388 now
where the time goes in v11:
time: 140 us
  waiting for transfers between devices  80.2 us (57%)
  between operations  15.4 us (11%)
  starting transfers between devices  15 us (11%)
  other arithmetic  14 us (10%)
  local copies, waits for them, and re-layouts  7.77 us (6%)
  matrix products  7.28 us (5%)
    ppermute x4, waiting for transfers between devices, swap_with(): return lax.ppermute(block, axis, [(i, i ^ flip) for i in devices])  62.5 us
    all_to_all x1, waiting for transfers between devices, per_device(): arrived = lax.all_to_all(parts, 'y', 0, 0, tiled=True)  17.7 us
    ppermute x4, starting transfers between devices, swap_with(): return lax.ppermute(block, axis, [(i, i ^ flip) for i in devices])  10.5 us
    dot_general x1, matrix products, per_device(): jnp.einsum('sjik,jskn->in', ks_whole, sign_four, preferred_element_type=j...  7.28 us
    gather x1, local copies, waits for them, and re-layouts, per_device(): jnp.take(sign_four, spot * local_groups + inner_of % local_groups, axis=1...  6.4 us
    concatenate x1, other arithmetic, per_device(): sign_four = jnp.concatenate([pair, near], axis=1)  5.29 us
    all_to_all x1, starting transfers between devices, per_device(): arrived = lax.all_to_all(parts, 'y', 0, 0, tiled=True)  4.46 us
  transfers between devices with their start and end apart: 6, of which 5 were waited for; matrix products, arithmetic and copies ran while one was open for 12% of the time, Pallas kernels for 0%

profile of v11, /device:TPU:388, one launch (start us, length us, event | category | flops | bytes accessed | tf_op | source)
XLA Modules:
  0.0 139.7 jit_solution(9537030266357898070)
XLA Ops:
  6.5 0.7 convert_bitcast_fusion
  7.3 0.7 pad_clamp_fusion.1
  7.9 1.0 multiply_bitcast_fusion
  9.0 0.6 gather_fusion
  9.6 3.1 %collective-permute-start = (bf16[4,128,128]{2,1,0:T(8,128)(2,1)S(1)}, bf16[4,128,128]{2,1,0:T(8,128)(2,1)S(1)}, u32[]{:S(2)}, u32[]{:S(2)}) collective-permute-start(bf16[4,128,128]{2,1,0:T(8,128)(2,1)S(1)} %get-tuple-element.6), channel_id=1, source_target_pairs={{0,1},{1,0},{2,3},{3,2},{4,5},{5,4},{6,7},{7,6},{8,9},{9,8},{10,11... | collective-permute-start | bytes 393224 | tf_op jit(solution)/shard_map/ppermute | solution.py:11
  12.7 4.0 %collective-permute-done = bf16[4,128,128]{2,1,0:T(8,128)(2,1)S(1)} collective-permute-done((bf16[4,128,128]{2,1,0:T(8,128)(2,1)S(1)}, bf16[4,128,128]{2,1,0:T(8,128)(2,1)S(1)}, u32[]{:S(2)}, u32[]{:S(2)}) %collective-permute-start) | collective-permute-done | bytes 131104 | tf_op jit(solution)/shard_map/ppermute | solution.py:11
  16.7 0.7 pad_maximum_fusion.3
  17.5 0.7 convert_element_type.20
  18.3 1.2 bitcast_multiply_fusion
  19.5 3.1 %collective-permute-start.1 = (bf16[4,128,768]{2,1,0:T(8,128)(2,1)S(1)}, bf16[4,128,768]{2,1,0:T(8,128)(2,1)S(1)}, u32[]{:S(2)}, u32[]{:S(2)}) collective-permute-start(bf16[4,128,768]{2,1,0:T(8,128)(2,1)S(1)} %bitcast_multiply_fusion), channel_id=1, source_target_pairs={{0,1},{1,0},{2,3},{3,2},{4,5},{5,4},{6,7},{7,6},{8,9},{9,8},{10,11... | collective-permute-start | bytes 2359304 | tf_op jit(solution)/shard_map/ppermute | solution.py:11
  22.7 17.1 %collective-permute-done.1 = bf16[4,128,768]{2,1,0:T(8,128)(2,1)S(1)} collective-permute-done((bf16[4,128,768]{2,1,0:T(8,128)(2,1)S(1)}, bf16[4,128,768]{2,1,0:T(8,128)(2,1)S(1)}, u32[]{:S(2)}, u32[]{:S(2)}) %collective-permute-start.1) | collective-permute-done | bytes 786464 | tf_op jit(solution)/shard_map/ppermute | solution.py:11
  39.9 2.4 %collective-permute-start.2 = (bf16[2,4,128,768]{3,2,1,0:T(8,128)(2,1)S(1)}, bf16[2,4,128,768]{3,2,1,0:T(8,128)(2,1)S(1)}, u32[]{:S(2)}, u32[]{:S(2)}) collective-permute-start(bf16[2,4,128,768]{3,2,1,0:T(8,128)(2,1)S(1)} %pad_maximum_fusion.2), channel_id=1, source_target_pairs={{0,16},{8,24},{16,0},{24,8},{1,17},{9,25},{17,1},{25,9},{2,18},{10... | collective-permute-start | bytes 4718600 | tf_op jit(solution)/shard_map/ppermute | solution.py:11
  42.3 35.4 %collective-permute-done.2 = bf16[2,4,128,768]{3,2,1,0:T(8,128)(2,1)S(1)} collective-permute-done((bf16[2,4,128,768]{3,2,1,0:T(8,128)(2,1)S(1)}, bf16[2,4,128,768]{3,2,1,0:T(8,128)(2,1)S(1)}, u32[]{:S(2)}, u32[]{:S(2)}) %collective-permute-start.2) | collective-permute-done | bytes 1572896 | tf_op jit(solution)/shard_map/ppermute | solution.py:11
  77.8 2.0 %pad_maximum_fusion.1 = bf16[2,8,128,768]{3,2,1,0:T(8,128)(2,1)} fusion(bf16[2,4,128,768]{3,2,1,0:T(8,128)(2,1)S(1)} %collective-permute-done.2, bf16[1,4,128,768]{3,2,1,0:T(8,128)(2,1)S(1)} %bitcast.42, bf16[1,4,128,768]{3,2,1,0:T(8,128)(2,1)S(1)} %bitcast_multiply_fusion.1), kind=kLoop, calls=%fused_computation.5 | loop fusion | flops 3145728 | bytes 6291456 | tf_op jit(solution)/shard_map/concatenate | solution.py:42
  79.8 1.9 %collective-permute-start.3 = (bf16[2,8,128,768]{3,2,1,0:T(8,128)(2,1)}, bf16[2,8,128,768]{3,2,1,0:T(8,128)(2,1)}, u32[]{:S(2)}, u32[]{:S(2)}) collective-permute-start(bf16[2,8,128,768]{3,2,1,0:T(8,128)(2,1)} %pad_maximum_fusion.1), channel_id=1, source_target_pairs={{0,8},{8,0},{16,24},{24,16},{1,9},{9,1},{17,25},{25,17},{2,10},{10... | collective-permute-start | bytes 9437192 | tf_op jit(solution)/shard_map/ppermute | solution.py:11
  81.7 5.9 %collective-permute-done.3 = bf16[2,8,128,768]{3,2,1,0:T(8,128)(2,1)} collective-permute-done((bf16[2,8,128,768]{3,2,1,0:T(8,128)(2,1)}, bf16[2,8,128,768]{3,2,1,0:T(8,128)(2,1)}, u32[]{:S(2)}, u32[]{:S(2)}) %collective-permute-start.3) | collective-permute-done | bytes 3145760 | tf_op jit(solution)/shard_map/ppermute | solution.py:11
  87.6 5.3 %pad_maximum_fusion = bf16[2,16,128,768]{3,2,1,0:T(8,128)(2,1)} fusion(bf16[2,8,128,768]{3,2,1,0:T(8,128)(2,1)} %collective-permute-done.3, bf16[2,4,128,768]{3,2,1,0:T(8,128)(2,1)S(1)} %collective-permute-done.2, bf16[1,4,128,768]{3,2,1,0:T(8,128)(2,1)S(1)} %bitcast.43, bf16[1,4,128,768]{3,2,1,0:T(8,128)(2,1)S(1)} %bitcast_multiply_fusion.1), kind=kLoop, calls=%fused_computation.2 | loop fusion | flops 9437184 | bytes 12582912 | tf_op jit(solution)/shard_map/concatenate | solution.py:44
  92.9 6.4 %gather_fusion.1 = bf16[16,2,128,768]{3,2,1,0:T(8,128)(2,1)} fusion(bf16[2,16,128,768]{3,2,1,0:T(8,128)(2,1)} %pad_maximum_fusion, s32[1024]{0:T(1024)S(1)} %pad_clamp_fusion), kind=kCustom, calls=%fused_computation.1 | custom fusion | bytes 12582976 | tf_op jit(solution)/shard_map/jit(_take)/gather | solution.py:50
  99.3 7.3 %fusion = f32[512,768,1,1]{1,0,3,2:T(8,128)} fusion(bf16[16,2,512,128]{3,2,0,1:T(8,128)(2,1)} %all-gather.2.cloned.1.call-done, bf16[16,2,128,768]{3,2,1,0:T(8,128)(2,1)} %gather_fusion.1), kind=kOutput, calls=%fused_computation.3 | convolution fusion | flops 3221225472 | bytes 12058624 | tf_op jit(solution)/shard_map/sjik,jskn->in/dot_general | solution.py:51
  106.6 4.5 %all-to-all-start = ((f32[4,128,768]{2,1,0:T(8,128)}), f32[4,128,768]{2,1,0:T(8,128)S(1)}, u32[]{:S(2)}, u32[]{:S(2)}) async-start(f32[4,128,768]{2,1,0:T(8,128)} %bitcast.15), calls=%async_computation | async-start | bytes 3145728 | tf_op jit(solution)/shard_map/all_to_all | solution.py:55
  111.1 0.6 constant_dynamic-slice_fusion.1
  113.6 0.7 fusion.5
  114.4 17.7 %all-to-all-done = f32[4,128,768]{2,1,0:T(8,128)S(1)} async-done(((f32[4,128,768]{2,1,0:T(8,128)}), f32[4,128,768]{2,1,0:T(8,128)S(1)}, u32[]{:S(2)}, u32[]{:S(2)}) %all-to-all-start) | async-done | bytes 1572896 | tf_op jit(solution)/shard_map/all_to_all | solution.py:55
  132.2 0.7 multiply_convert_fusion
  (17 shorter events, 0.6 us)
Async XLA Ops:
  6.5 16.0 %copy-start = (bf16[4,1,128,768]{3,2,1,0:T(8,128)(2,1)S(1)}, bf16[4,1,128,768]{3,2,1,0:T(8,128)(2,1)}, u32[]{:S(2)}) copy-start(bf16[4,1,128,768]{3,2,1,0:T(8,128)(2,1)} %param.7) | copy-start | bytes 2359300
  6.5 92.8 %all-gather.2.cloned.1.call-start = ((), (), s32[]{:S(2)}) async-start(), calls=%async_computation.1 | async-start | bytes 4456448 | tf_op jit(solution)/shard_map/all_gather | solution.py:46
  9.6 7.1 %collective-permute-start = (bf16[4,128,128]{2,1,0:T(8,128)(2,1)S(1)}, bf16[4,128,128]{2,1,0:T(8,128)(2,1)S(1)}, u32[]{:S(2)}, u32[]{:S(2)}) collective-permute-start(bf16[4,128,128]{2,1,0:T(8,128)(2,1)S(1)} %get-tuple-element.6), channel_id=1, source_target_pairs={{0,1},{1,0},{2,3},{3,2},{4,5},{5,4},{6,7},{7,6},{8,9},{9,8},{10,11... | collective-permute-start | bytes 393224 | tf_op jit(solution)/shard_map/ppermute | solution.py:11
  19.5 20.3 %collective-permute-start.1 = (bf16[4,128,768]{2,1,0:T(8,128)(2,1)S(1)}, bf16[4,128,768]{2,1,0:T(8,128)(2,1)S(1)}, u32[]{:S(2)}, u32[]{:S(2)}) collective-permute-start(bf16[4,128,768]{2,1,0:T(8,128)(2,1)S(1)} %bitcast_multiply_fusion), channel_id=1, source_target_pairs={{0,1},{1,0},{2,3},{3,2},{4,5},{5,4},{6,7},{7,6},{8,9},{9,8},{10,11... | collective-permute-start | bytes 2359304 | tf_op jit(solution)/shard_map/ppermute | solution.py:11
  39.9 37.8 %collective-permute-start.2 = (bf16[2,4,128,768]{3,2,1,0:T(8,128)(2,1)S(1)}, bf16[2,4,128,768]{3,2,1,0:T(8,128)(2,1)S(1)}, u32[]{:S(2)}, u32[]{:S(2)}) collective-permute-start(bf16[2,4,128,768]{3,2,1,0:T(8,128)(2,1)S(1)} %pad_maximum_fusion.2), channel_id=1, source_target_pairs={{0,16},{8,24},{16,0},{24,8},{1,17},{9,25},{17,1},{25,9},{2,18},{10... | collective-permute-start | bytes 4718600 | tf_op jit(solution)/shard_map/ppermute | solution.py:11
  79.8 7.9 %collective-permute-start.3 = (bf16[2,8,128,768]{3,2,1,0:T(8,128)(2,1)}, bf16[2,8,128,768]{3,2,1,0:T(8,128)(2,1)}, u32[]{:S(2)}, u32[]{:S(2)}) collective-permute-start(bf16[2,8,128,768]{3,2,1,0:T(8,128)(2,1)} %pad_maximum_fusion.1), channel_id=1, source_target_pairs={{0,8},{8,0},{16,24},{24,16},{1,9},{9,1},{17,25},{25,17},{2,10},{10... | collective-permute-start | bytes 9437192 | tf_op jit(solution)/shard_map/ppermute | solution.py:11
  99.3 11.7 %copy-start.1 = (s32[1,8]{1,0:T(1,128)S(1)}, s32[1,8]{1,0:T(1,128)}, u32[]{:S(2)}) copy-start(s32[1,8]{1,0:T(1,128)} %param.11) | copy-start | bytes 100
  106.6 25.5 %all-to-all-start = ((f32[4,128,768]{2,1,0:T(8,128)}), f32[4,128,768]{2,1,0:T(8,128)S(1)}, u32[]{:S(2)}, u32[]{:S(2)}) async-start(f32[4,128,768]{2,1,0:T(8,128)} %bitcast.15), calls=%async_computation | async-start | bytes 3145728 | tf_op jit(solution)/shard_map/all_to_all | solution.py:55
Sparse Core Ops, SparseCore 0:
  17.6 75.5 all-gather.1

commit v12 on v11

--- a/solution.py
+++ b/solution.py
@@ -21,15 +21,18 @@
     ring_me = lax.axis_index("y")
     pair_me = lax.axis_index("xlo")
     local_order = row_order[0]
-    ks_panel = (
-        ks_matrix.reshape(row_blocks, BS, inner_blocks, BS)
-        * ks_mask.astype(jnp.bfloat16)[:, None, :, None]
-    )
-    ks_panel = jnp.take(ks_panel, local_order, axis=0, mode="clip")
-    ks_split = ks_panel.reshape(ring_count, pair_count, BS, inner_blocks * BS)
-    mine = lax.dynamic_index_in_dim(ks_split, pair_me, 1, keepdims=False)
-    theirs = lax.dynamic_index_in_dim(ks_split, 1 - pair_me, 1, keepdims=False)
-    lent = swap_with(theirs, "xlo", 1)
+    ks_blocks = ks_matrix.reshape(row_blocks, BS, inner_blocks, BS)
+    by_pair = local_order.reshape(ring_count, pair_count)
+
+    def arranged_rows(pair):
+        picked = lax.dynamic_index_in_dim(by_pair, pair, 1, keepdims=False)
+        rows = jnp.take(ks_blocks, picked, axis=0, mode="clip")
+        row_mask = jnp.take(ks_mask, picked, axis=0, mode="clip")
+        rows = rows * row_mask.astype(jnp.bfloat16)[:, None, :, None]
+        return rows.reshape(ring_count, BS, inner_blocks * BS)
+
+    lent = swap_with(arranged_rows(1 - pair_me), "xlo", 1)
+    mine = arranged_rows(pair_me)
     payload = jnp.stack([mine, lent])
     payload = payload.reshape(pair_count, ring_count * BS, inner_blocks * BS)
     sign_kept = sign_matrix.reshape(local_groups, sign_inner, BS, col_blocks, BS)

time: 140 us -> 141 us (level)
  the two profiles are of different devices: /device:TPU:388 before, /device:TPU:416 now
where the time goes in v12:
time: 141 us
  waiting for transfers between devices  75 us (53%)
  starting transfers between devices  18.1 us (13%)
  between operations  15.5 us (11%)
  other arithmetic  13.2 us (9%)
  local copies, waits for them, and re-layouts  11.8 us (8%)
  matrix products  7.28 us (5%)
    ppermute x4, waiting for transfers between devices, swap_with(): return lax.ppermute(block, axis, [(i, i ^ flip) for i in devices])  57.3 us
    all_to_all x1, waiting for transfers between devices, per_device(): arrived = lax.all_to_all(parts, 'y', 0, 0, tiled=True)  17.7 us
    ppermute x4, starting transfers between devices, swap_with(): return lax.ppermute(block, axis, [(i, i ^ flip) for i in devices])  13.6 us
    dot_general x1, matrix products, per_device(): jnp.einsum('sjik,jskn->in', ks_whole, sign_four, preferred_element_type=j...  7.28 us
    gather x1, local copies, waits for them, and re-layouts, per_device(): jnp.take(sign_four, spot * local_groups + inner_of % local_groups, axis=1...  6.38 us
    concatenate x1, other arithmetic, per_device(): sign_four = jnp.concatenate([pair, near], axis=1)  5.31 us
    all_to_all x1, starting transfers between devices, per_device(): arrived = lax.all_to_all(parts, 'y', 0, 0, tiled=True)  4.46 us
  transfers between devices with their start and end apart: 6, of which 5 were waited for; matrix products, arithmetic and copies ran while one was open for 14% of the time, Pallas kernels for 0%

profile of v12, /device:TPU:416, one launch (start us, length us, event | category | flops | bytes accessed | tf_op | source)
XLA Modules:
  0.0 140.8 jit_solution(15209977657373420935)
XLA Ops:
  7.1 1.3 reduce.7
  8.7 0.6 gather_fusion.2
  9.3 1.3 gather_fusion.3
  10.7 3.4 %collective-permute-start = (bf16[4,128,128]{2,1,0:T(8,128)(2,1)S(1)}, bf16[4,128,128]{2,1,0:T(8,128)(2,1)S(1)}, u32[]{:S(2)}, u32[]{:S(2)}) collective-permute-start(bf16[4,128,128]{2,1,0:T(8,128)(2,1)S(1)} %broadcast_multiply_fusion), channel_id=1, source_target_pairs={{0,1},{1,0},{2,3},{3,2},{4,5},{5,4},{6,7},{7,6},{8,9},{9,8},{10,11... | collective-permute-start | bytes 393224 | tf_op jit(solution)/shard_map/ppermute | solution.py:11
  14.7 1.3 gather_fusion.1
  16.2 1.6 %collective-permute-done = bf16[4,128,128]{2,1,0:T(8,128)(2,1)S(1)} collective-permute-done((bf16[4,128,128]{2,1,0:T(8,128)(2,1)S(1)}, bf16[4,128,128]{2,1,0:T(8,128)(2,1)S(1)}, u32[]{:S(2)}, u32[]{:S(2)}) %collective-permute-start) | collective-permute-done | bytes 131104 | tf_op jit(solution)/shard_map/ppermute | solution.py:11
  17.8 0.7 pad_maximum_fusion.3
  18.5 0.7 convert_element_type.44
  19.3 1.2 bitcast_multiply_fusion
  20.5 3.4 %collective-permute-start.1 = (bf16[4,128,768]{2,1,0:T(8,128)(2,1)S(1)}, bf16[4,128,768]{2,1,0:T(8,128)(2,1)S(1)}, u32[]{:S(2)}, u32[]{:S(2)}) collective-permute-start(bf16[4,128,768]{2,1,0:T(8,128)(2,1)S(1)} %bitcast_multiply_fusion), channel_id=1, source_target_pairs={{0,1},{1,0},{2,3},{3,2},{4,5},{5,4},{6,7},{7,6},{8,9},{9,8},{10,11... | collective-permute-start | bytes 2359304 | tf_op jit(solution)/shard_map/ppermute | solution.py:11
  24.0 16.8 %collective-permute-done.1 = bf16[4,128,768]{2,1,0:T(8,128)(2,1)S(1)} collective-permute-done((bf16[4,128,768]{2,1,0:T(8,128)(2,1)S(1)}, bf16[4,128,768]{2,1,0:T(8,128)(2,1)S(1)}, u32[]{:S(2)}, u32[]{:S(2)}) %collective-permute-start.1) | collective-permute-done | bytes 786464 | tf_op jit(solution)/shard_map/ppermute | solution.py:11
  41.0 4.9 %collective-permute-start.2 = (bf16[2,4,128,768]{3,2,1,0:T(8,128)(2,1)S(1)}, bf16[2,4,128,768]{3,2,1,0:T(8,128)(2,1)S(1)}, u32[]{:S(2)}, u32[]{:S(2)}) collective-permute-start(bf16[2,4,128,768]{3,2,1,0:T(8,128)(2,1)S(1)} %pad_maximum_fusion.2), channel_id=1, source_target_pairs={{0,16},{8,24},{16,0},{24,8},{1,17},{9,25},{17,1},{25,9},{2,18},{10... | collective-permute-start | bytes 4718600 | tf_op jit(solution)/shard_map/ppermute | solution.py:11
  45.9 32.9 %collective-permute-done.2 = bf16[2,4,128,768]{3,2,1,0:T(8,128)(2,1)S(1)} collective-permute-done((bf16[2,4,128,768]{3,2,1,0:T(8,128)(2,1)S(1)}, bf16[2,4,128,768]{3,2,1,0:T(8,128)(2,1)S(1)}, u32[]{:S(2)}, u32[]{:S(2)}) %collective-permute-start.2) | collective-permute-done | bytes 1572896 | tf_op jit(solution)/shard_map/ppermute | solution.py:11
  78.8 2.0 %pad_maximum_fusion.1 = bf16[2,8,128,768]{3,2,1,0:T(8,128)(2,1)} fusion(bf16[2,4,128,768]{3,2,1,0:T(8,128)(2,1)S(1)} %collective-permute-done.2, bf16[1,4,128,768]{3,2,1,0:T(8,128)(2,1)S(1)} %bitcast.41, bf16[1,4,128,768]{3,2,1,0:T(8,128)(2,1)S(1)} %bitcast_multiply_fusion.1), kind=kLoop, calls=%fused_computation.8 | loop fusion | flops 3145728 | bytes 6291456 | tf_op jit(solution)/shard_map/concatenate | solution.py:45
  80.8 1.9 %collective-permute-start.3 = (bf16[2,8,128,768]{3,2,1,0:T(8,128)(2,1)}, bf16[2,8,128,768]{3,2,1,0:T(8,128)(2,1)}, u32[]{:S(2)}, u32[]{:S(2)}) collective-permute-start(bf16[2,8,128,768]{3,2,1,0:T(8,128)(2,1)} %pad_maximum_fusion.1), channel_id=1, source_target_pairs={{0,8},{8,0},{16,24},{24,16},{1,9},{9,1},{17,25},{25,17},{2,10},{10... | collective-permute-start | bytes 9437192 | tf_op jit(solution)/shard_map/ppermute | solution.py:11
  82.8 5.9 %collective-permute-done.3 = bf16[2,8,128,768]{3,2,1,0:T(8,128)(2,1)} collective-permute-done((bf16[2,8,128,768]{3,2,1,0:T(8,128)(2,1)}, bf16[2,8,128,768]{3,2,1,0:T(8,128)(2,1)}, u32[]{:S(2)}, u32[]{:S(2)}) %collective-permute-start.3) | collective-permute-done | bytes 3145760 | tf_op jit(solution)/shard_map/ppermute | solution.py:11
  88.7 5.3 %pad_maximum_fusion = bf16[2,16,128,768]{3,2,1,0:T(8,128)(2,1)} fusion(bf16[2,8,128,768]{3,2,1,0:T(8,128)(2,1)} %collective-permute-done.3, bf16[2,4,128,768]{3,2,1,0:T(8,128)(2,1)S(1)} %collective-permute-done.2, bf16[1,4,128,768]{3,2,1,0:T(8,128)(2,1)S(1)} %bitcast.42, bf16[1,4,128,768]{3,2,1,0:T(8,128)(2,1)S(1)} %bitcast_multiply_fusion.1), kind=kLoop, calls=%fused_computation.5 | loop fusion | flops 9437184 | bytes 12582912 | tf_op jit(solution)/shard_map/concatenate | solution.py:47
  94.0 6.4 %gather_fusion.4 = bf16[16,2,128,768]{3,2,1,0:T(8,128)(2,1)} fusion(bf16[2,16,128,768]{3,2,1,0:T(8,128)(2,1)} %pad_maximum_fusion, s32[1024]{0:T(1024)S(1)} %pad_clamp_fusion), kind=kCustom, calls=%fused_computation.4 | custom fusion | bytes 12582976 | tf_op jit(solution)/shard_map/jit(_take)/gather | solution.py:53
  100.4 7.3 %fusion = f32[512,768,1,1]{1,0,3,2:T(8,128)} fusion(bf16[16,2,512,128]{3,2,0,1:T(8,128)(2,1)} %all-gather.2.cloned.1.call-done, bf16[16,2,128,768]{3,2,1,0:T(8,128)(2,1)} %gather_fusion.4), kind=kOutput, calls=%fused_computation.6 | convolution fusion | flops 3221225472 | bytes 12058624 | tf_op jit(solution)/shard_map/sjik,jskn->in/dot_general | solution.py:54
  107.7 4.5 %all-to-all-start = ((f32[4,128,768]{2,1,0:T(8,128)}), f32[4,128,768]{2,1,0:T(8,128)S(1)}, u32[]{:S(2)}, u32[]{:S(2)}) async-start(f32[4,128,768]{2,1,0:T(8,128)} %bitcast.12), calls=%async_computation | async-start | bytes 3145728 | tf_op jit(solution)/shard_map/all_to_all | solution.py:58
  112.1 0.6 constant_dynamic-slice_fusion.1
  114.6 0.7 fusion.5
  115.4 17.7 %all-to-all-done = f32[4,128,768]{2,1,0:T(8,128)S(1)} async-done(((f32[4,128,768]{2,1,0:T(8,128)}), f32[4,128,768]{2,1,0:T(8,128)S(1)}, u32[]{:S(2)}, u32[]{:S(2)}) %all-to-all-start) | async-done | bytes 1572896 | tf_op jit(solution)/shard_map/all_to_all | solution.py:58
  133.2 0.7 multiply_convert_fusion
  (28 shorter events, 2.2 us)
Async XLA Ops:
  6.5 2.2 %copy-start = (bf16[1024,128]{1,0:T(8,128)(2,1)S(1)}, bf16[1024,128]{1,0:T(8,128)(2,1)}, u32[]{:S(2)}) copy-start(bf16[1024,128]{1,0:T(8,128)(2,1)} %param.6) | copy-start | bytes 786436
  6.5 17.4 %copy-start.1 = (bf16[4,1,128,768]{3,2,1,0:T(8,128)(2,1)S(1)}, bf16[4,1,128,768]{3,2,1,0:T(8,128)(2,1)}, u32[]{:S(2)}) copy-start(bf16[4,1,128,768]{3,2,1,0:T(8,128)(2,1)} %param.7) | copy-start | bytes 2359300
  6.5 93.8 %all-gather.2.cloned.1.call-start = ((), (), s32[]{:S(2)}) async-start(), calls=%async_computation.1 | async-start | bytes 4456448 | tf_op jit(solution)/shard_map/all_gather | solution.py:49
  10.7 7.1 %collective-permute-start = (bf16[4,128,128]{2,1,0:T(8,128)(2,1)S(1)}, bf16[4,128,128]{2,1,0:T(8,128)(2,1)S(1)}, u32[]{:S(2)}, u32[]{:S(2)}) collective-permute-start(bf16[4,128,128]{2,1,0:T(8,128)(2,1)S(1)} %broadcast_multiply_fusion), channel_id=1, source_target_pairs={{0,1},{1,0},{2,3},{3,2},{4,5},{5,4},{6,7},{7,6},{8,9},{9,8},{10,11... | collective-permute-start | bytes 393224 | tf_op jit(solution)/shard_map/ppermute | solution.py:11
  20.5 20.3 %collective-permute-start.1 = (bf16[4,128,768]{2,1,0:T(8,128)(2,1)S(1)}, bf16[4,128,768]{2,1,0:T(8,128)(2,1)S(1)}, u32[]{:S(2)}, u32[]{:S(2)}) collective-permute-start(bf16[4,128,768]{2,1,0:T(8,128)(2,1)S(1)} %bitcast_multiply_fusion), channel_id=1, source_target_pairs={{0,1},{1,0},{2,3},{3,2},{4,5},{5,4},{6,7},{7,6},{8,9},{9,8},{10,11... | collective-permute-start | bytes 2359304 | tf_op jit(solution)/shard_map/ppermute | solution.py:11
  41.0 37.8 %collective-permute-start.2 = (bf16[2,4,128,768]{3,2,1,0:T(8,128)(2,1)S(1)}, bf16[2,4,128,768]{3,2,1,0:T(8,128)(2,1)S(1)}, u32[]{:S(2)}, u32[]{:S(2)}) collective-permute-start(bf16[2,4,128,768]{3,2,1,0:T(8,128)(2,1)S(1)} %pad_maximum_fusion.2), channel_id=1, source_target_pairs={{0,16},{8,24},{16,0},{24,8},{1,17},{9,25},{17,1},{25,9},{2,18},{10... | collective-permute-start | bytes 4718600 | tf_op jit(solution)/shard_map/ppermute | solution.py:11
  80.8 7.9 %collective-permute-start.3 = (bf16[2,8,128,768]{3,2,1,0:T(8,128)(2,1)}, bf16[2,8,128,768]{3,2,1,0:T(8,128)(2,1)}, u32[]{:S(2)}, u32[]{:S(2)}) collective-permute-start(bf16[2,8,128,768]{3,2,1,0:T(8,128)(2,1)} %pad_maximum_fusion.1), channel_id=1, source_target_pairs={{0,8},{8,0},{16,24},{24,16},{1,9},{9,1},{17,25},{25,17},{2,10},{10... | collective-permute-start | bytes 9437192 | tf_op jit(solution)/shard_map/ppermute | solution.py:11
  100.4 11.7 %copy-start.2 = (s32[1,8]{1,0:T(1,128)S(1)}, s32[1,8]{1,0:T(1,128)}, u32[]{:S(2)}) copy-start(s32[1,8]{1,0:T(1,128)} %param.11) | copy-start | bytes 100
  107.7 25.5 %all-to-all-start = ((f32[4,128,768]{2,1,0:T(8,128)}), f32[4,128,768]{2,1,0:T(8,128)S(1)}, u32[]{:S(2)}, u32[]{:S(2)}) async-start(f32[4,128,768]{2,1,0:T(8,128)} %bitcast.12), calls=%async_computation | async-start | bytes 3145728 | tf_op jit(solution)/shard_map/all_to_all | solution.py:58
Sparse Core Ops, SparseCore 0:
  18.7 75.4 all-gather.1

commit v13 on v11

--- a/solution.py
+++ b/solution.py
@@ -38,16 +38,22 @@
     )
     sign_kept = sign_kept.reshape(local_groups, sign_inner * BS, col_blocks * BS)
     sign_kept = jnp.stack([sign_kept, swap_with(sign_kept, "xlo", 1)])
+    me = lax.axis_index("col")
+    chip_bit = me // 2
+    core_bit = me % 2
     far = swap_with(sign_kept, "col", 2)
-    pair = jnp.concatenate([sign_kept, far], axis=1)
+    pair = jnp.where(
+        chip_bit == 0,
+        jnp.concatenate([sign_kept, far], axis=1),
+        jnp.concatenate([far, sign_kept], axis=1),
+    )
     near = swap_with(pair, "col", 1)
-    sign_four = jnp.concatenate([pair, near], axis=1)
-    me = lax.axis_index("col")
+    core0 = jnp.where(core_bit == 0, pair, near)
+    core1 = jnp.where(core_bit == 0, near, pair)
+    shape = (pair_count, 2, local_groups, sign_inner * BS, col_blocks * BS)
+    sign_four = jnp.stack([core0.reshape(shape), core1.reshape(shape)], axis=2)
+    sign_four = sign_four.reshape(pair_count, -1, sign_inner * BS, col_blocks * BS)
     ks_whole = lax.all_gather(payload, "row", axis=0, tiled=False)
-    inner_of = jnp.arange(lax.axis_size("row"), dtype=jnp.int32)
-    flipped = (inner_of // local_groups) ^ me
-    spot = (flipped % 2) * 2 + flipped // 2
-    sign_four = jnp.take(sign_four, spot * local_groups + inner_of % local_groups, axis=1, mode="clip")
     product = jnp.einsum(
         "sjik,jskn->in", ks_whole, sign_four, preferred_element_type=jnp.float32
     )

time: 140 us -> 135 us (0.964)
  the two profiles are of different devices: /device:TPU:388 before, /device:TPU:196 now
where the time goes in v13:
time: 135 us
  waiting for transfers between devices  80.6 us (60%)
  between operations  15.5 us (11%)
  other arithmetic  15.4 us (11%)
  starting transfers between devices  14.9 us (11%)
  matrix products  7.27 us (5%)
  local copies, waits for them, and re-layouts  1.37 us (1%)
    ppermute x4, waiting for transfers between devices, swap_with(): return lax.ppermute(block, axis, [(i, i ^ flip) for i in devices])  62.7 us
    all_to_all x1, waiting for transfers between devices, per_device(): arrived = lax.all_to_all(parts, 'y', 0, 0, tiled=True)  16.8 us
    ppermute x4, starting transfers between devices, swap_with(): return lax.ppermute(block, axis, [(i, i ^ flip) for i in devices])  10.5 us
    dot_general x1, matrix products, per_device(): jnp.einsum('sjik,jskn->in', ks_whole, sign_four, preferred_element_type=j...  7.27 us
    all_to_all x1, starting transfers between devices, per_device(): arrived = lax.all_to_all(parts, 'y', 0, 0, tiled=True)  4.41 us
    another operation x1, other arithmetic, per_device(): sign_four = jnp.stack([core0.reshape(shape), core1.reshape(shape)], axis=2)  3.23 us
  transfers between devices with their start and end apart: 6, of which 6 were waited for; matrix products, arithmetic and copies ran while one was open for 9% of the time, Pallas kernels for 0%

profile of v13, /device:TPU:196, one launch (start us, length us, event | category | flops | bytes accessed | tf_op | source)
XLA Modules:
  0.0 135.0 jit_solution(13261833858046111061)
XLA Ops:
  6.5 0.7 convert_bitcast_fusion
  7.3 0.7 pad_clamp_fusion
  7.9 1.0 multiply_bitcast_fusion
  9.6 3.1 %collective-permute-start = (bf16[4,128,128]{2,1,0:T(8,128)(2,1)S(1)}, bf16[4,128,128]{2,1,0:T(8,128)(2,1)S(1)}, u32[]{:S(2)}, u32[]{:S(2)}) collective-permute-start(bf16[4,128,128]{2,1,0:T(8,128)(2,1)S(1)} %get-tuple-element.8), channel_id=1, source_target_pairs={{0,1},{1,0},{2,3},{3,2},{4,5},{5,4},{6,7},{7,6},{8,9},{9,8},{10,11... | collective-permute-start | bytes 393224 | tf_op jit(solution)/shard_map/ppermute | solution.py:11
  12.7 4.0 %collective-permute-done = bf16[4,128,128]{2,1,0:T(8,128)(2,1)S(1)} collective-permute-done((bf16[4,128,128]{2,1,0:T(8,128)(2,1)S(1)}, bf16[4,128,128]{2,1,0:T(8,128)(2,1)S(1)}, u32[]{:S(2)}, u32[]{:S(2)}) %collective-permute-start) | collective-permute-done | bytes 131104 | tf_op jit(solution)/shard_map/ppermute | solution.py:11
  16.7 0.7 pad_maximum_fusion.2
  17.5 0.7 convert_element_type.20
  18.3 1.2 bitcast_multiply_fusion
  19.5 3.1 %collective-permute-start.1 = (bf16[4,128,768]{2,1,0:T(8,128)(2,1)S(1)}, bf16[4,128,768]{2,1,0:T(8,128)(2,1)S(1)}, u32[]{:S(2)}, u32[]{:S(2)}) collective-permute-start(bf16[4,128,768]{2,1,0:T(8,128)(2,1)S(1)} %bitcast_multiply_fusion), channel_id=1, source_target_pairs={{0,1},{1,0},{2,3},{3,2},{4,5},{5,4},{6,7},{7,6},{8,9},{9,8},{10,11... | collective-permute-start | bytes 2359304 | tf_op jit(solution)/shard_map/ppermute | solution.py:11
  22.7 17.1 %collective-permute-done.1 = bf16[4,128,768]{2,1,0:T(8,128)(2,1)S(1)} collective-permute-done((bf16[4,128,768]{2,1,0:T(8,128)(2,1)S(1)}, bf16[4,128,768]{2,1,0:T(8,128)(2,1)S(1)}, u32[]{:S(2)}, u32[]{:S(2)}) %collective-permute-start.1) | collective-permute-done | bytes 786464 | tf_op jit(solution)/shard_map/ppermute | solution.py:11
  39.8 1.3 pad_maximum_fusion.1
  41.1 2.4 %collective-permute-start.2 = (bf16[2,4,128,768]{3,2,1,0:T(8,128)(2,1)}, bf16[2,4,128,768]{3,2,1,0:T(8,128)(2,1)S(1)}, u32[]{:S(2)}, u32[]{:S(2)}) collective-permute-start(bf16[2,4,128,768]{3,2,1,0:T(8,128)(2,1)} %pad_maximum_fusion.1), channel_id=1, source_target_pairs={{0,16},{8,24},{16,0},{24,8},{1,17},{9,25},{17,1},{25,9},{2,18},{10... | collective-permute-start | bytes 4718600 | tf_op jit(solution)/shard_map/ppermute | solution.py:11
  43.5 35.6 %collective-permute-done.2 = bf16[2,4,128,768]{3,2,1,0:T(8,128)(2,1)S(1)} collective-permute-done((bf16[2,4,128,768]{3,2,1,0:T(8,128)(2,1)}, bf16[2,4,128,768]{3,2,1,0:T(8,128)(2,1)S(1)}, u32[]{:S(2)}, u32[]{:S(2)}) %collective-permute-start.2) | collective-permute-done | bytes 1572896 | tf_op jit(solution)/shard_map/ppermute | solution.py:11
  79.1 1.9 %maximum_select_fusion = bf16[2,8,128,768]{3,2,1,0:T(8,128)(2,1)} fusion(bf16[2,4,128,768]{3,2,1,0:T(8,128)(2,1)S(1)} %collective-permute-done.2, bf16[1,4,128,768]{3,2,1,0:T(8,128)(2,1)S(1)} %bitcast.49, bf16[1,4,128,768]{3,2,1,0:T(8,128)(2,1)S(1)} %bitcast_multiply_fusion.1, pred[]{:T(512)S(6)} %eq.10), kind=kLoop, calls=%fused_computation.4 | loop fusion | flops 7864320 | bytes 6291457 | tf_op jit(solution)/shard_map/jit(_where)/select_n | solution.py:45
  81.1 1.9 %collective-permute-start.3 = (bf16[2,8,128,768]{3,2,1,0:T(8,128)(2,1)}, bf16[2,8,128,768]{3,2,1,0:T(8,128)(2,1)}, u32[]{:S(2)}, u32[]{:S(2)}) collective-permute-start(bf16[2,8,128,768]{3,2,1,0:T(8,128)(2,1)} %maximum_select_fusion), channel_id=1, source_target_pairs={{0,8},{8,0},{16,24},{24,16},{1,9},{9,1},{17,25},{25,17},{2,10},{10... | collective-permute-start | bytes 9437192 | tf_op jit(solution)/shard_map/ppermute | solution.py:11
  83.0 6.0 %collective-permute-done.3 = bf16[2,8,128,768]{3,2,1,0:T(8,128)(2,1)} collective-permute-done((bf16[2,8,128,768]{3,2,1,0:T(8,128)(2,1)}, bf16[2,8,128,768]{3,2,1,0:T(8,128)(2,1)}, u32[]{:S(2)}, u32[]{:S(2)}) %collective-permute-start.3) | collective-permute-done | bytes 3145760 | tf_op jit(solution)/shard_map/ppermute | solution.py:11
  88.9 2.3 %broadcast_select_fusion.1 = (bf16[2,8,128,768]{3,2,1,0:T(8,128)(2,1)S(1)}, bf16[2,8,128,768]{3,2,1,0:T(8,128)(2,1)S(1)}) fusion(bf16[2,8,128,768]{3,2,1,0:T(8,128)(2,1)} %collective-permute-done.3, pred[]{:T(512)S(6)} %eq.9, bf16[1,4,128,768]{3,2,1,0:T(8,128)(2,1)S(1)} %bitcast.50, bf16[1,4,128,768]{3,2,1,0:T(8,128)(2,1)S(1)} %bitcast_multiply_fusion.1, ...), kind=kLoop, calls=%fused_computation.6 | loop fusion | flops 11010048 | bytes 12582914 | tf_op jit(solution)/shard_map/jit(_where)/select_n | solution.py:51
  91.3 3.2 %pad_maximum_fusion = bf16[2,2,2,4,128,768]{5,4,3,2,1,0:T(8,128)(2,1)} fusion(bf16[2,2,1,4,128,768]{5,4,3,2,1,0:T(8,128)(2,1)S(1)} %bitcast.47, bf16[2,2,1,4,128,768]{5,4,3,2,1,0:T(8,128)(2,1)S(1)} %bitcast.46), kind=kLoop, calls=%fused_computation.1 | loop fusion | flops 3145728 | bytes 12582912 | tf_op jit(solution)/shard_map/stack | solution.py:54
  94.5 1.1 all-gather.2.cloned.1.call-done
  95.5 7.3 %fusion.2 = f32[4,128,768]{2,1,0:T(8,128)} fusion(bf16[2,16,128,768,1]{3,2,1,0,4:T(8,128)(2,1)} %bitcast.51, bf16[4,128,2,128,16]{3,1,0,2,4:T(8,128)(2,1)} %bitcast.60), kind=kOutput, calls=%fused_computation.8 | convolution fusion | flops 3221225472 | bytes 12058624 | tf_op jit(solution)/shard_map/sjik,jskn->in/dot_general | solution.py:57
  102.8 4.4 %all-to-all-start = ((f32[4,128,768]{2,1,0:T(8,128)}), f32[4,128,768]{2,1,0:T(8,128)S(1)}, u32[]{:S(2)}, u32[]{:S(2)}) async-start(f32[4,128,768]{2,1,0:T(8,128)} %fusion.2), calls=%async_computation | async-start | bytes 3145728 | tf_op jit(solution)/shard_map/all_to_all | solution.py:61
  109.8 0.7 fusion.6
  110.5 16.8 %all-to-all-done = f32[4,128,768]{2,1,0:T(8,128)S(1)} async-done(((f32[4,128,768]{2,1,0:T(8,128)}), f32[4,128,768]{2,1,0:T(8,128)S(1)}, u32[]{:S(2)}, u32[]{:S(2)}) %all-to-all-start) | async-done | bytes 1572896 | tf_op jit(solution)/shard_map/all_to_all | solution.py:61
  127.4 0.7 multiply_convert_fusion
  (15 shorter events, 1.6 us)
Async XLA Ops:
  6.5 16.1 %copy-start = (bf16[4,1,128,768]{3,2,1,0:T(8,128)(2,1)S(1)}, bf16[4,1,128,768]{3,2,1,0:T(8,128)(2,1)}, u32[]{:S(2)}) copy-start(bf16[4,1,128,768]{3,2,1,0:T(8,128)(2,1)} %param.7) | copy-start | bytes 2359300
  6.5 89.0 %all-gather.2.cloned.1.call-start = ((), (), s32[]{:S(2)}) async-start(), calls=%async_computation.1 | async-start | bytes 4456448 | tf_op jit(solution)/shard_map/all_gather | solution.py:56
  9.6 7.1 %collective-permute-start = (bf16[4,128,128]{2,1,0:T(8,128)(2,1)S(1)}, bf16[4,128,128]{2,1,0:T(8,128)(2,1)S(1)}, u32[]{:S(2)}, u32[]{:S(2)}) collective-permute-start(bf16[4,128,128]{2,1,0:T(8,128)(2,1)S(1)} %get-tuple-element.8), channel_id=1, source_target_pairs={{0,1},{1,0},{2,3},{3,2},{4,5},{5,4},{6,7},{7,6},{8,9},{9,8},{10,11... | collective-permute-start | bytes 393224 | tf_op jit(solution)/shard_map/ppermute | solution.py:11
  19.5 20.3 %collective-permute-start.1 = (bf16[4,128,768]{2,1,0:T(8,128)(2,1)S(1)}, bf16[4,128,768]{2,1,0:T(8,128)(2,1)S(1)}, u32[]{:S(2)}, u32[]{:S(2)}) collective-permute-start(bf16[4,128,768]{2,1,0:T(8,128)(2,1)S(1)} %bitcast_multiply_fusion), channel_id=1, source_target_pairs={{0,1},{1,0},{2,3},{3,2},{4,5},{5,4},{6,7},{7,6},{8,9},{9,8},{10,11... | collective-permute-start | bytes 2359304 | tf_op jit(solution)/shard_map/ppermute | solution.py:11
  41.1 38.0 %collective-permute-start.2 = (bf16[2,4,128,768]{3,2,1,0:T(8,128)(2,1)}, bf16[2,4,128,768]{3,2,1,0:T(8,128)(2,1)S(1)}, u32[]{:S(2)}, u32[]{:S(2)}) collective-permute-start(bf16[2,4,128,768]{3,2,1,0:T(8,128)(2,1)} %pad_maximum_fusion.1), channel_id=1, source_target_pairs={{0,16},{8,24},{16,0},{24,8},{1,17},{9,25},{17,1},{25,9},{2,18},{10... | collective-permute-start | bytes 4718600 | tf_op jit(solution)/shard_map/ppermute | solution.py:11
  81.1 7.9 %collective-permute-start.3 = (bf16[2,8,128,768]{3,2,1,0:T(8,128)(2,1)}, bf16[2,8,128,768]{3,2,1,0:T(8,128)(2,1)}, u32[]{:S(2)}, u32[]{:S(2)}) collective-permute-start(bf16[2,8,128,768]{3,2,1,0:T(8,128)(2,1)} %maximum_select_fusion), channel_id=1, source_target_pairs={{0,8},{8,0},{16,24},{24,16},{1,9},{9,1},{17,25},{25,17},{2,10},{10... | collective-permute-start | bytes 9437192 | tf_op jit(solution)/shard_map/ppermute | solution.py:11
  102.8 4.4 %copy-start.1 = (s32[1,8]{1,0:T(1,128)S(1)}, s32[1,8]{1,0:T(1,128)}, u32[]{:S(2)}) copy-start(s32[1,8]{1,0:T(1,128)} %param.11) | copy-start | bytes 100
  102.8 24.5 %all-to-all-start = ((f32[4,128,768]{2,1,0:T(8,128)}), f32[4,128,768]{2,1,0:T(8,128)S(1)}, u32[]{:S(2)}, u32[]{:S(2)}) async-start(f32[4,128,768]{2,1,0:T(8,128)} %fusion.2), calls=%async_computation | async-start | bytes 3145728 | tf_op jit(solution)/shard_map/all_to_all | solution.py:61
Sparse Core Ops, SparseCore 0:
  17.6 77.8 all-gather.1

commit v14 on v13

--- a/solution.py
+++ b/solution.py
@@ -37,16 +37,19 @@
         local_groups, sign_inner, 1, col_blocks, 1
     )
     sign_kept = sign_kept.reshape(local_groups, sign_inner * BS, col_blocks * BS)
-    sign_kept = jnp.stack([sign_kept, swap_with(sign_kept, "xlo", 1)])
     me = lax.axis_index("col")
     chip_bit = me // 2
     core_bit = me % 2
-    far = swap_with(sign_kept, "col", 2)
-    pair = jnp.where(
-        chip_bit == 0,
-        jnp.concatenate([sign_kept, far], axis=1),
-        jnp.concatenate([far, sign_kept], axis=1),
+    partner = swap_with(sign_kept, "xlo", 1)
+    diag = swap_with(sign_kept, ("col", "xlo"), 5)
+    far = swap_with(diag, "xlo", 1)
+    mine_first = jnp.stack(
+        [jnp.concatenate([sign_kept, far]), jnp.concatenate([partner, diag])]
     )
+    far_first = jnp.stack(
+        [jnp.concatenate([far, sign_kept]), jnp.concatenate([diag, partner])]
+    )
+    pair = jnp.where(chip_bit == 0, mine_first, far_first)
     near = swap_with(pair, "col", 1)
     core0 = jnp.where(core_bit == 0, pair, near)
     core1 = jnp.where(core_bit == 0, near, pair)

time: 135 us -> 134 us (level)
  the two profiles are of different devices: /device:TPU:196 before, /device:TPU:4 now
where the time goes in v14:
time: 134 us
  waiting for transfers between devices  65.9 us (49%)
  starting transfers between devices  24.3 us (18%)
  other arithmetic  18.9 us (14%)
  between operations  15.5 us (12%)
  matrix products  7.26 us (5%)
  local copies, waits for them, and re-layouts  1.89 us (1%)
    ppermute x5, waiting for transfers between devices, swap_with(): return lax.ppermute(block, axis, [(i, i ^ flip) for i in devices])  32 us
    all_gather x1, waiting for transfers between devices, per_device(): ks_whole = lax.all_gather(payload, 'row', axis=0, tiled=False)  23.5 us
    ppermute x5, starting transfers between devices, swap_with(): return lax.ppermute(block, axis, [(i, i ^ flip) for i in devices])  19.9 us
    all_to_all x1, waiting for transfers between devices, per_device(): arrived = lax.all_to_all(parts, 'y', 0, 0, tiled=True)  10.4 us
    dot_general x1, matrix products, per_device(): jnp.einsum('sjik,jskn->in', ks_whole, sign_four, preferred_element_type=j...  7.26 us
    all_to_all x1, starting transfers between devices, per_device(): arrived = lax.all_to_all(parts, 'y', 0, 0, tiled=True)  4.42 us
    another operation x2, other arithmetic, per_device(): jnp.stack([jnp.concatenate([far, sign_kept]), jnp.concatenate([diag, part...  3.86 us
    another operation x1, other arithmetic, per_device(): sign_four = jnp.stack([core0.reshape(shape), core1.reshape(shape)], axis=2)  3.23 us
  transfers between devices with their start and end apart: 7, of which 6 were waited for; matrix products, arithmetic and copies ran while one was open for 12% of the time, Pallas kernels for 0%

profile of v14, /device:TPU:4, one launch (start us, length us, event | category | flops | bytes accessed | tf_op | source)
XLA Modules:
  0.0 133.7 jit_solution(7979344591304833960)
XLA Ops:
  7.9 1.0 multiply_bitcast_fusion
  9.5 3.1 %collective-permute-start = (bf16[4,128,128]{2,1,0:T(8,128)(2,1)S(1)}, bf16[4,128,128]{2,1,0:T(8,128)(2,1)S(1)}, u32[]{:S(2)}, u32[]{:S(2)}) collective-permute-start(bf16[4,128,128]{2,1,0:T(8,128)(2,1)S(1)} %get-tuple-element.12), channel_id=1, source_target_pairs={{0,1},{1,0},{2,3},{3,2},{4,5},{5,4},{6,7},{7,6},{8,9},{9,8},{10,11... | collective-permute-start | bytes 393224 | tf_op jit(solution)/shard_map/ppermute | solution.py:11
  12.7 4.0 %collective-permute-done = bf16[4,128,128]{2,1,0:T(8,128)(2,1)S(1)} collective-permute-done((bf16[4,128,128]{2,1,0:T(8,128)(2,1)S(1)}, bf16[4,128,128]{2,1,0:T(8,128)(2,1)S(1)}, u32[]{:S(2)}, u32[]{:S(2)}) %collective-permute-start) | collective-permute-done | bytes 131104 | tf_op jit(solution)/shard_map/ppermute | solution.py:11
  16.7 0.7 pad_maximum_fusion.1
  17.4 0.7 convert_element_type.20
  18.2 1.2 bitcast_multiply_fusion
  19.4 6.1 %collective-permute-start.1 = (bf16[4,128,768]{2,1,0:T(8,128)(2,1)S(1)}, bf16[4,128,768]{2,1,0:T(8,128)(2,1)}, u32[]{:S(2)}, u32[]{:S(2)}) collective-permute-start(bf16[4,128,768]{2,1,0:T(8,128)(2,1)S(1)} %bitcast_multiply_fusion), channel_id=1, source_target_pairs={{0,17},{1,16},{8,25},{9,24},{16,1},{17,0},{24,9},{25,8},{2,19},{3,... | collective-permute-start | bytes 2359304 | tf_op jit(solution)/shard_map/ppermute | solution.py:11
  25.5 4.5 %collective-permute-start.3 = (bf16[4,128,768]{2,1,0:T(8,128)(2,1)S(1)}, bf16[4,128,768]{2,1,0:T(8,128)(2,1)}, u32[]{:S(2)}, u32[]{:S(2)}) collective-permute-start(bf16[4,128,768]{2,1,0:T(8,128)(2,1)S(1)} %bitcast_multiply_fusion), channel_id=1, source_target_pairs={{0,1},{1,0},{2,3},{3,2},{4,5},{5,4},{6,7},{7,6},{8,9},{9,8},{10,11... | collective-permute-start | bytes 2359304 | tf_op jit(solution)/shard_map/ppermute | solution.py:11
  30.0 9.8 %collective-permute-done.1 = bf16[4,128,768]{2,1,0:T(8,128)(2,1)} collective-permute-done((bf16[4,128,768]{2,1,0:T(8,128)(2,1)S(1)}, bf16[4,128,768]{2,1,0:T(8,128)(2,1)}, u32[]{:S(2)}, u32[]{:S(2)}) %collective-permute-start.1) | collective-permute-done | bytes 786464 | tf_op jit(solution)/shard_map/ppermute | solution.py:11
  39.8 4.3 %collective-permute-start.2 = (bf16[4,128,768]{2,1,0:T(8,128)(2,1)}, bf16[4,128,768]{2,1,0:T(8,128)(2,1)}, u32[]{:S(2)}, u32[]{:S(2)}) collective-permute-start(bf16[4,128,768]{2,1,0:T(8,128)(2,1)} %collective-permute-done.1), channel_id=1, source_target_pairs={{0,1},{1,0},{2,3},{3,2},{4,5},{5,4},{6,7},{7,6},{8,9},{9,8},{10,11... | collective-permute-start | bytes 2359304 | tf_op jit(solution)/shard_map/ppermute | solution.py:11
  44.2 2.2 %maximum_bitcast_fusion.3 = (bf16[1,8,128,768]{3,2,1,0:T(8,128)(2,1)S(1)}, bf16[1,8,128,768]{3,2,1,0:T(8,128)(2,1)S(1)}) fusion(bf16[4,128,768]{2,1,0:T(8,128)(2,1)} %collective-permute-done.3, bf16[4,128,768]{2,1,0:T(8,128)(2,1)} %collective-permute-done.1), kind=kLoop, calls=%fused_computation.10 | loop fusion | flops 1572864 | bytes 4718592 | tf_op jit(solution)/shard_map/stack | solution.py:49
  46.4 12.2 %collective-permute-done.2 = bf16[4,128,768]{2,1,0:T(8,128)(2,1)} collective-permute-done((bf16[4,128,768]{2,1,0:T(8,128)(2,1)}, bf16[4,128,768]{2,1,0:T(8,128)(2,1)}, u32[]{:S(2)}, u32[]{:S(2)}) %collective-permute-start.2) | collective-permute-done | bytes 786464 | tf_op jit(solution)/shard_map/ppermute | solution.py:11
  58.6 1.6 %maximum_bitcast_fusion.2 = (bf16[1,8,128,768]{3,2,1,0:T(8,128)(2,1)S(1)}, bf16[1,8,128,768]{3,2,1,0:T(8,128)(2,1)S(1)}) fusion(bf16[4,128,768]{2,1,0:T(8,128)(2,1)S(1)} %copy-done.3, bf16[4,128,768]{2,1,0:T(8,128)(2,1)} %collective-permute-done.2), kind=kLoop, calls=%fused_computation.9 | loop fusion | flops 1572864 | bytes 4718592 | tf_op jit(solution)/shard_map/stack | solution.py:49
  60.2 2.2 %maximum_select_fusion = bf16[2,8,128,768]{3,2,1,0:T(8,128)(2,1)} fusion(bf16[1,8,128,768]{3,2,1,0:T(8,128)(2,1)S(1)} %get-tuple-element.10, bf16[1,8,128,768]{3,2,1,0:T(8,128)(2,1)S(1)} %get-tuple-element.8, bf16[1,8,128,768]{3,2,1,0:T(8,128)(2,1)S(1)} %get-tuple-element.9, bf16[1,8,128,768]{3,2,1,0:T(8,128)(2,1)S(1)} %get-tuple-element.7, pred[]{:T(512)S(6)} %eq.10), kind=kLoop, calls=%fused_computation.4 | loop fusion | flops 4718592 | bytes 9437185 | tf_op jit(solution)/shard_map/jit(_where)/select_n | solution.py:52
  62.9 1.9 %collective-permute-start.4 = (bf16[2,8,128,768]{3,2,1,0:T(8,128)(2,1)}, bf16[2,8,128,768]{3,2,1,0:T(8,128)(2,1)}, u32[]{:S(2)}, u32[]{:S(2)}) collective-permute-start(bf16[2,8,128,768]{3,2,1,0:T(8,128)(2,1)} %maximum_select_fusion), channel_id=1, source_target_pairs={{0,8},{8,0},{16,24},{24,16},{1,9},{9,1},{17,25},{25,17},{2,10},{10... | collective-permute-start | bytes 9437192 | tf_op jit(solution)/shard_map/ppermute | solution.py:11
  64.8 6.0 %collective-permute-done.4 = bf16[2,8,128,768]{3,2,1,0:T(8,128)(2,1)} collective-permute-done((bf16[2,8,128,768]{3,2,1,0:T(8,128)(2,1)}, bf16[2,8,128,768]{3,2,1,0:T(8,128)(2,1)}, u32[]{:S(2)}, u32[]{:S(2)}) %collective-permute-start.4) | collective-permute-done | bytes 3145760 | tf_op jit(solution)/shard_map/ppermute | solution.py:11
  70.8 3.1 %broadcast_select_fusion.1 = (bf16[2,8,128,768]{3,2,1,0:T(8,128)(2,1)S(1)}, bf16[2,8,128,768]{3,2,1,0:T(8,128)(2,1)S(1)}) fusion(bf16[2,8,128,768]{3,2,1,0:T(8,128)(2,1)} %collective-permute-done.4, pred[]{:T(512)S(6)} %eq.9, bf16[1,8,128,768]{3,2,1,0:T(8,128)(2,1)S(1)} %get-tuple-element.9, bf16[1,8,128,768]{3,2,1,0:T(8,128)(2,1)} %copy-done, ...), kind=kLoop, calls=%fused_computation.6 | loop fusion | flops 7864320 | bytes 15728642 | tf_op jit(solution)/shard_map/jit(_where)/select_n | solution.py:54
  73.9 3.2 %pad_maximum_fusion = bf16[2,2,2,4,128,768]{5,4,3,2,1,0:T(8,128)(2,1)} fusion(bf16[2,2,1,4,128,768]{5,4,3,2,1,0:T(8,128)(2,1)S(1)} %bitcast.52, bf16[2,2,1,4,128,768]{5,4,3,2,1,0:T(8,128)(2,1)S(1)} %bitcast.51), kind=kLoop, calls=%fused_computation.1 | loop fusion | flops 3145728 | bytes 12582912 | tf_op jit(solution)/shard_map/stack | solution.py:57
  77.2 23.5 %all-gather.2.cloned.1.call-done = bf16[16,2,512,128]{3,2,1,0:T(8,128)(2,1)} async-done(((bf16[1,2,512,128]{3,2,1,0:T(8,128)(2,1)}), bf16[16,2,512,128]{3,2,1,0:T(8,128)(2,1)}) %all-gather.2.cloned.1.call-update) | async-done | bytes 4194320 | tf_op jit(solution)/shard_map/all_gather | solution.py:59
  100.7 7.3 %fusion.2 = f32[4,128,768]{2,1,0:T(8,128)} fusion(bf16[2,16,128,768,1]{3,2,1,0,4:T(8,128)(2,1)} %bitcast.53, bf16[4,128,2,128,16]{3,1,0,2,4:T(8,128)(2,1)} %bitcast.61), kind=kOutput, calls=%fused_computation.11 | convolution fusion | flops 3221225472 | bytes 12058624 | tf_op jit(solution)/shard_map/sjik,jskn->in/dot_general | solution.py:60
  107.9 4.4 %all-to-all-start = ((f32[4,128,768]{2,1,0:T(8,128)}), f32[4,128,768]{2,1,0:T(8,128)S(1)}, u32[]{:S(2)}, u32[]{:S(2)}) async-start(f32[4,128,768]{2,1,0:T(8,128)} %fusion.2), calls=%async_computation | async-start | bytes 3145728 | tf_op jit(solution)/shard_map/all_to_all | solution.py:64
  114.9 0.7 fusion.6
  115.7 10.4 %all-to-all-done = f32[4,128,768]{2,1,0:T(8,128)S(1)} async-done(((f32[4,128,768]{2,1,0:T(8,128)}), f32[4,128,768]{2,1,0:T(8,128)S(1)}, u32[]{:S(2)}, u32[]{:S(2)}) %all-to-all-start) | async-done | bytes 1572896 | tf_op jit(solution)/shard_map/all_to_all | solution.py:64
  126.2 0.7 multiply_convert_fusion
  (23 shorter events, 3.3 us)
Async XLA Ops:
  6.5 94.1 %all-gather.2.cloned.1.call-start = ((), (), s32[]{:S(2)}) async-start(), calls=%async_computation.1 | async-start | bytes 4456448 | tf_op jit(solution)/shard_map/all_gather | solution.py:59
  9.5 7.1 %collective-permute-start = (bf16[4,128,128]{2,1,0:T(8,128)(2,1)S(1)}, bf16[4,128,128]{2,1,0:T(8,128)(2,1)S(1)}, u32[]{:S(2)}, u32[]{:S(2)}) collective-permute-start(bf16[4,128,128]{2,1,0:T(8,128)(2,1)S(1)} %get-tuple-element.12), channel_id=1, source_target_pairs={{0,1},{1,0},{2,3},{3,2},{4,5},{5,4},{6,7},{7,6},{8,9},{9,8},{10,11... | collective-permute-start | bytes 393224 | tf_op jit(solution)/shard_map/ppermute | solution.py:11
  19.4 24.8 %copy-start.2 = (bf16[4,128,768]{2,1,0:T(8,128)(2,1)}, bf16[4,128,768]{2,1,0:T(8,128)(2,1)S(1)}, u32[]{:S(2)}) copy-start(bf16[4,128,768]{2,1,0:T(8,128)(2,1)S(1)} %bitcast_multiply_fusion) | copy-start | bytes 2359300
  19.4 20.4 %collective-permute-start.1 = (bf16[4,128,768]{2,1,0:T(8,128)(2,1)S(1)}, bf16[4,128,768]{2,1,0:T(8,128)(2,1)}, u32[]{:S(2)}, u32[]{:S(2)}) collective-permute-start(bf16[4,128,768]{2,1,0:T(8,128)(2,1)S(1)} %bitcast_multiply_fusion), channel_id=1, source_target_pairs={{0,17},{1,16},{8,25},{9,24},{16,1},{17,0},{24,9},{25,8},{2,19},{3,... | collective-permute-start | bytes 2359304 | tf_op jit(solution)/shard_map/ppermute | solution.py:11
  25.5 18.7 %collective-permute-start.3 = (bf16[4,128,768]{2,1,0:T(8,128)(2,1)S(1)}, bf16[4,128,768]{2,1,0:T(8,128)(2,1)}, u32[]{:S(2)}, u32[]{:S(2)}) collective-permute-start(bf16[4,128,768]{2,1,0:T(8,128)(2,1)S(1)} %bitcast_multiply_fusion), channel_id=1, source_target_pairs={{0,1},{1,0},{2,3},{3,2},{4,5},{5,4},{6,7},{7,6},{8,9},{9,8},{10,11... | collective-permute-start | bytes 2359304 | tf_op jit(solution)/shard_map/ppermute | solution.py:11
  39.8 18.8 %collective-permute-start.2 = (bf16[4,128,768]{2,1,0:T(8,128)(2,1)}, bf16[4,128,768]{2,1,0:T(8,128)(2,1)}, u32[]{:S(2)}, u32[]{:S(2)}) collective-permute-start(bf16[4,128,768]{2,1,0:T(8,128)(2,1)} %collective-permute-done.1), channel_id=1, source_target_pairs={{0,1},{1,0},{2,3},{3,2},{4,5},{5,4},{6,7},{7,6},{8,9},{9,8},{10,11... | collective-permute-start | bytes 2359304 | tf_op jit(solution)/shard_map/ppermute | solution.py:11
  44.1 14.4 %copy-start.3 = (bf16[4,128,768]{2,1,0:T(8,128)(2,1)S(1)}, bf16[4,128,768]{2,1,0:T(8,128)(2,1)}, u32[]{:S(2)}) copy-start(bf16[4,128,768]{2,1,0:T(8,128)(2,1)} %copy-done.2) | copy-start | bytes 2359300
  60.2 2.2 %copy-start = (bf16[1,8,128,768]{3,2,1,0:T(8,128)(2,1)}, bf16[1,8,128,768]{3,2,1,0:T(8,128)(2,1)S(1)}, u32[]{:S(2)}) copy-start(bf16[1,8,128,768]{3,2,1,0:T(8,128)(2,1)S(1)} %get-tuple-element.7) | copy-start | bytes 4718596
  60.2 2.7 %copy-start.1 = (bf16[1,8,128,768]{3,2,1,0:T(8,128)(2,1)}, bf16[1,8,128,768]{3,2,1,0:T(8,128)(2,1)S(1)}, u32[]{:S(2)}) copy-start(bf16[1,8,128,768]{3,2,1,0:T(8,128)(2,1)S(1)} %get-tuple-element.8) | copy-start | bytes 4718596
  62.9 7.9 %collective-permute-start.4 = (bf16[2,8,128,768]{3,2,1,0:T(8,128)(2,1)}, bf16[2,8,128,768]{3,2,1,0:T(8,128)(2,1)}, u32[]{:S(2)}, u32[]{:S(2)}) collective-permute-start(bf16[2,8,128,768]{3,2,1,0:T(8,128)(2,1)} %maximum_select_fusion), channel_id=1, source_target_pairs={{0,8},{8,0},{16,24},{24,16},{1,9},{9,1},{17,25},{25,17},{2,10},{10... | collective-permute-start | bytes 9437192 | tf_op jit(solution)/shard_map/ppermute | solution.py:11
  107.9 4.4 %copy-start.4 = (s32[1,8]{1,0:T(1,128)S(1)}, s32[1,8]{1,0:T(1,128)}, u32[]{:S(2)}) copy-start(s32[1,8]{1,0:T(1,128)} %param.11) | copy-start | bytes 100
  107.9 18.1 %all-to-all-start = ((f32[4,128,768]{2,1,0:T(8,128)}), f32[4,128,768]{2,1,0:T(8,128)S(1)}, u32[]{:S(2)}, u32[]{:S(2)}) async-start(f32[4,128,768]{2,1,0:T(8,128)} %fusion.2), calls=%async_computation | async-start | bytes 3145728 | tf_op jit(solution)/shard_map/all_to_all | solution.py:64
Sparse Core Ops, SparseCore 0:
  17.5 83.1 all-gather.1

commit v15 on v14

--- a/solution.py
+++ b/solution.py
@@ -56,9 +56,10 @@
     shape = (pair_count, 2, local_groups, sign_inner * BS, col_blocks * BS)
     sign_four = jnp.stack([core0.reshape(shape), core1.reshape(shape)], axis=2)
     sign_four = sign_four.reshape(pair_count, -1, sign_inner * BS, col_blocks * BS)
+    sign_four = jnp.swapaxes(sign_four, 0, 1)
     ks_whole = lax.all_gather(payload, "row", axis=0, tiled=False)
     product = jnp.einsum(
-        "sjik,jskn->in", ks_whole, sign_four, preferred_element_type=jnp.float32
+        "sjik,sjkn->in", ks_whole, sign_four, preferred_element_type=jnp.float32
     )
     parts = product.reshape(ring_count, BS, col_blocks * BS)
     arrived = lax.all_to_all(parts, "y", 0, 0, tiled=True)

time: 134 us -> 134 us (level)
  the two profiles are of different devices: /device:TPU:4 before, /device:TPU:2 now
where the time goes in v15:
time: 134 us
  waiting for transfers between devices  66.6 us (50%)
  starting transfers between devices  23.6 us (18%)
  other arithmetic  18.9 us (14%)
  between operations  15.5 us (12%)
  matrix products  7.25 us (5%)
  local copies, waits for them, and re-layouts  1.9 us (1%)
    ppermute x5, waiting for transfers between devices, swap_with(): return lax.ppermute(block, axis, [(i, i ^ flip) for i in devices])  33.9 us
    all_gather x1, waiting for transfers between devices, per_device(): ks_whole = lax.all_gather(payload, 'row', axis=0, tiled=False)  22.2 us
    ppermute x5, starting transfers between devices, swap_with(): return lax.ppermute(block, axis, [(i, i ^ flip) for i in devices])  19.3 us
    all_to_all x1, waiting for transfers between devices, per_device(): arrived = lax.all_to_all(parts, 'y', 0, 0, tiled=True)  10.4 us
    dot_general x1, matrix products, per_device(): jnp.einsum('sjik,sjkn->in', ks_whole, sign_four, preferred_element_type=j...  7.25 us
    all_to_all x1, starting transfers between devices, per_device(): arrived = lax.all_to_all(parts, 'y', 0, 0, tiled=True)  4.31 us
    another operation x2, other arithmetic, per_device(): jnp.stack([jnp.concatenate([far, sign_kept]), jnp.concatenate([diag, part...  3.83 us
    another operation x1, other arithmetic, per_device(): sign_four = jnp.stack([core0.reshape(shape), core1.reshape(shape)], axis=2)  3.23 us
  transfers between devices with their start and end apart: 7, of which 7 were waited for; matrix products, arithmetic and copies ran while one was open for 12% of the time, Pallas kernels for 0%

profile of v15, /device:TPU:2, one launch (start us, length us, event | category | flops | bytes accessed | tf_op | source)
XLA Modules:
  0.0 133.7 jit_solution(8934292411515562784)
XLA Ops:
  7.9 1.0 multiply_bitcast_fusion
  9.5 7.8 %collective-permute-start = (bf16[4,128,128]{2,1,0:T(8,128)(2,1)S(1)}, bf16[4,128,128]{2,1,0:T(8,128)(2,1)S(1)}, u32[]{:S(2)}, u32[]{:S(2)}) collective-permute-start(bf16[4,128,128]{2,1,0:T(8,128)(2,1)S(1)} %get-tuple-element.12), channel_id=1, source_target_pairs={{0,1},{1,0},{2,3},{3,2},{4,5},{5,4},{6,7},{7,6},{8,9},{9,8},{10,11... | collective-permute-start | bytes 393224 | tf_op jit(solution)/shard_map/ppermute | solution.py:11
  17.4 2.9 %collective-permute-done = bf16[4,128,128]{2,1,0:T(8,128)(2,1)S(1)} collective-permute-done((bf16[4,128,128]{2,1,0:T(8,128)(2,1)S(1)}, bf16[4,128,128]{2,1,0:T(8,128)(2,1)S(1)}, u32[]{:S(2)}, u32[]{:S(2)}) %collective-permute-start) | collective-permute-done | bytes 131104 | tf_op jit(solution)/shard_map/ppermute | solution.py:11
  20.3 0.7 pad_maximum_fusion.1
  21.8 1.2 bitcast_multiply_fusion
  23.0 1.9 %collective-permute-start.1 = (bf16[4,128,768]{2,1,0:T(8,128)(2,1)S(1)}, bf16[4,128,768]{2,1,0:T(8,128)(2,1)}, u32[]{:S(2)}, u32[]{:S(2)}) collective-permute-start(bf16[4,128,768]{2,1,0:T(8,128)(2,1)S(1)} %bitcast_multiply_fusion), channel_id=1, source_target_pairs={{0,17},{1,16},{8,25},{9,24},{16,1},{17,0},{24,9},{25,8},{2,19},{3,... | collective-permute-start | bytes 2359304 | tf_op jit(solution)/shard_map/ppermute | solution.py:11
  24.9 3.9 %collective-permute-start.3 = (bf16[4,128,768]{2,1,0:T(8,128)(2,1)S(1)}, bf16[4,128,768]{2,1,0:T(8,128)(2,1)}, u32[]{:S(2)}, u32[]{:S(2)}) collective-permute-start(bf16[4,128,768]{2,1,0:T(8,128)(2,1)S(1)} %bitcast_multiply_fusion), channel_id=1, source_target_pairs={{0,1},{1,0},{2,3},{3,2},{4,5},{5,4},{6,7},{7,6},{8,9},{9,8},{10,11... | collective-permute-start | bytes 2359304 | tf_op jit(solution)/shard_map/ppermute | solution.py:11
  28.9 10.7 %collective-permute-done.1 = bf16[4,128,768]{2,1,0:T(8,128)(2,1)} collective-permute-done((bf16[4,128,768]{2,1,0:T(8,128)(2,1)S(1)}, bf16[4,128,768]{2,1,0:T(8,128)(2,1)}, u32[]{:S(2)}, u32[]{:S(2)}) %collective-permute-start.1) | collective-permute-done | bytes 786464 | tf_op jit(solution)/shard_map/ppermute | solution.py:11
  39.6 3.7 %collective-permute-start.2 = (bf16[4,128,768]{2,1,0:T(8,128)(2,1)}, bf16[4,128,768]{2,1,0:T(8,128)(2,1)}, u32[]{:S(2)}, u32[]{:S(2)}) collective-permute-start(bf16[4,128,768]{2,1,0:T(8,128)(2,1)} %collective-permute-done.1), channel_id=1, source_target_pairs={{0,1},{1,0},{2,3},{3,2},{4,5},{5,4},{6,7},{7,6},{8,9},{9,8},{10,11... | collective-permute-start | bytes 2359304 | tf_op jit(solution)/shard_map/ppermute | solution.py:11
  43.3 3.2 %collective-permute-done.3 = bf16[4,128,768]{2,1,0:T(8,128)(2,1)} collective-permute-done((bf16[4,128,768]{2,1,0:T(8,128)(2,1)S(1)}, bf16[4,128,768]{2,1,0:T(8,128)(2,1)}, u32[]{:S(2)}, u32[]{:S(2)}) %collective-permute-start.3) | collective-permute-done | bytes 786464 | tf_op jit(solution)/shard_map/ppermute | solution.py:11
  46.5 2.2 %maximum_bitcast_fusion.3 = (bf16[1,8,128,768]{3,2,1,0:T(8,128)(2,1)S(1)}, bf16[1,8,128,768]{3,2,1,0:T(8,128)(2,1)S(1)}) fusion(bf16[4,128,768]{2,1,0:T(8,128)(2,1)} %collective-permute-done.3, bf16[4,128,768]{2,1,0:T(8,128)(2,1)} %collective-permute-done.1), kind=kLoop, calls=%fused_computation.8 | loop fusion | flops 1572864 | bytes 4718592 | tf_op jit(solution)/shard_map/stack | solution.py:49
  48.7 11.1 %collective-permute-done.2 = bf16[4,128,768]{2,1,0:T(8,128)(2,1)} collective-permute-done((bf16[4,128,768]{2,1,0:T(8,128)(2,1)}, bf16[4,128,768]{2,1,0:T(8,128)(2,1)}, u32[]{:S(2)}, u32[]{:S(2)}) %collective-permute-start.2) | collective-permute-done | bytes 786464 | tf_op jit(solution)/shard_map/ppermute | solution.py:11
  59.8 1.6 %maximum_bitcast_fusion.2 = (bf16[1,8,128,768]{3,2,1,0:T(8,128)(2,1)S(1)}, bf16[1,8,128,768]{3,2,1,0:T(8,128)(2,1)S(1)}) fusion(bf16[4,128,768]{2,1,0:T(8,128)(2,1)S(1)} %copy-done.3, bf16[4,128,768]{2,1,0:T(8,128)(2,1)} %collective-permute-done.2), kind=kLoop, calls=%fused_computation.7 | loop fusion | flops 1572864 | bytes 4718592 | tf_op jit(solution)/shard_map/stack | solution.py:49
  61.5 2.2 %maximum_select_fusion = bf16[2,8,128,768]{3,2,1,0:T(8,128)(2,1)} fusion(bf16[1,8,128,768]{3,2,1,0:T(8,128)(2,1)S(1)} %get-tuple-element.10, bf16[1,8,128,768]{3,2,1,0:T(8,128)(2,1)S(1)} %get-tuple-element.8, bf16[1,8,128,768]{3,2,1,0:T(8,128)(2,1)S(1)} %get-tuple-element.9, bf16[1,8,128,768]{3,2,1,0:T(8,128)(2,1)S(1)} %get-tuple-element.7, pred[]{:T(512)S(6)} %eq.10), kind=kLoop, calls=%fused_computation.2 | loop fusion | flops 4718592 | bytes 9437185 | tf_op jit(solution)/shard_map/jit(_where)/select_n | solution.py:52
  64.2 1.9 %collective-permute-start.4 = (bf16[2,8,128,768]{3,2,1,0:T(8,128)(2,1)}, bf16[2,8,128,768]{3,2,1,0:T(8,128)(2,1)}, u32[]{:S(2)}, u32[]{:S(2)}) collective-permute-start(bf16[2,8,128,768]{3,2,1,0:T(8,128)(2,1)} %maximum_select_fusion), channel_id=1, source_target_pairs={{0,8},{8,0},{16,24},{24,16},{1,9},{9,1},{17,25},{25,17},{2,10},{10... | collective-permute-start | bytes 9437192 | tf_op jit(solution)/shard_map/ppermute | solution.py:11
  66.1 6.0 %collective-permute-done.4 = bf16[2,8,128,768]{3,2,1,0:T(8,128)(2,1)} collective-permute-done((bf16[2,8,128,768]{3,2,1,0:T(8,128)(2,1)}, bf16[2,8,128,768]{3,2,1,0:T(8,128)(2,1)}, u32[]{:S(2)}, u32[]{:S(2)}) %collective-permute-start.4) | collective-permute-done | bytes 3145760 | tf_op jit(solution)/shard_map/ppermute | solution.py:11
  72.1 3.2 %broadcast_select_fusion.1 = (bf16[2,8,128,768]{3,2,1,0:T(8,128)(2,1)S(1)}, bf16[2,8,128,768]{3,2,1,0:T(8,128)(2,1)S(1)}) fusion(bf16[2,8,128,768]{3,2,1,0:T(8,128)(2,1)} %collective-permute-done.4, pred[]{:T(512)S(6)} %eq.9, bf16[1,8,128,768]{3,2,1,0:T(8,128)(2,1)S(1)} %get-tuple-element.9, bf16[1,8,128,768]{3,2,1,0:T(8,128)(2,1)} %copy-done, ...), kind=kLoop, calls=%fused_computation.4 | loop fusion | flops 7864320 | bytes 15728642 | tf_op jit(solution)/shard_map/jit(_where)/select_n | solution.py:54
  75.3 3.2 %pad_maximum_fusion = bf16[2,2,2,4,128,768]{5,4,3,2,1,0:T(8,128)(2,1)} fusion(bf16[2,2,1,4,128,768]{5,4,3,2,1,0:T(8,128)(2,1)S(1)} %bitcast.51, bf16[2,2,1,4,128,768]{5,4,3,2,1,0:T(8,128)(2,1)S(1)} %bitcast.50), kind=kLoop, calls=%fused_computation.1 | loop fusion | flops 3145728 | bytes 12582912 | tf_op jit(solution)/shard_map/stack | solution.py:57
  78.5 22.2 %all-gather.2.cloned.1.call-done = bf16[16,2,512,128]{3,2,0,1:T(8,128)(2,1)} async-done(((bf16[1,2,512,128]{3,2,0,1:T(8,128)(2,1)}), bf16[16,2,512,128]{3,2,0,1:T(8,128)(2,1)}) %all-gather.2.cloned.1.call-update) | async-done | bytes 4194320 | tf_op jit(solution)/shard_map/all_gather | solution.py:60
  100.7 7.3 %fusion.2 = f32[512,768,1,1]{1,0,3,2:T(8,128)} fusion(bf16[16,2,512,128]{3,2,0,1:T(8,128)(2,1)} %all-gather.2.cloned.1.call-done, bf16[16,2,128,768]{3,2,0,1:T(8,128)(2,1)} %bitcast.52), kind=kOutput, calls=%fused_computation.25 | convolution fusion | flops 3221225472 | bytes 12058624 | tf_op jit(solution)/shard_map/sjik,sjkn->in/dot_general | solution.py:61
  108.0 4.3 %all-to-all-start = ((f32[4,128,768]{2,1,0:T(8,128)}), f32[4,128,768]{2,1,0:T(8,128)S(1)}, u32[]{:S(2)}, u32[]{:S(2)}) async-start(f32[4,128,768]{2,1,0:T(8,128)} %bitcast.21), calls=%async_computation | async-start | bytes 3145728 | tf_op jit(solution)/shard_map/all_to_all | solution.py:65
  114.8 0.7 fusion.1
  115.6 10.4 %all-to-all-done = f32[4,128,768]{2,1,0:T(8,128)S(1)} async-done(((f32[4,128,768]{2,1,0:T(8,128)}), f32[4,128,768]{2,1,0:T(8,128)S(1)}, u32[]{:S(2)}, u32[]{:S(2)}) %all-to-all-start) | async-done | bytes 1572896 | tf_op jit(solution)/shard_map/all_to_all | solution.py:65
  126.1 0.7 multiply_convert_fusion
  (23 shorter events, 4.0 us)
Async XLA Ops:
  6.5 94.2 %all-gather.2.cloned.1.call-start = ((), (), s32[]{:S(2)}) async-start(), calls=%async_computation.1 | async-start | bytes 4456448 | tf_op jit(solution)/shard_map/all_gather | solution.py:60
  9.5 10.8 %collective-permute-start = (bf16[4,128,128]{2,1,0:T(8,128)(2,1)S(1)}, bf16[4,128,128]{2,1,0:T(8,128)(2,1)S(1)}, u32[]{:S(2)}, u32[]{:S(2)}) collective-permute-start(bf16[4,128,128]{2,1,0:T(8,128)(2,1)S(1)} %get-tuple-element.12), channel_id=1, source_target_pairs={{0,1},{1,0},{2,3},{3,2},{4,5},{5,4},{6,7},{7,6},{8,9},{9,8},{10,11... | collective-permute-start | bytes 393224 | tf_op jit(solution)/shard_map/ppermute | solution.py:11
  23.0 20.3 %copy-start.2 = (bf16[4,128,768]{2,1,0:T(8,128)(2,1)}, bf16[4,128,768]{2,1,0:T(8,128)(2,1)S(1)}, u32[]{:S(2)}) copy-start(bf16[4,128,768]{2,1,0:T(8,128)(2,1)S(1)} %bitcast_multiply_fusion) | copy-start | bytes 2359300
  23.0 16.5 %collective-permute-start.1 = (bf16[4,128,768]{2,1,0:T(8,128)(2,1)S(1)}, bf16[4,128,768]{2,1,0:T(8,128)(2,1)}, u32[]{:S(2)}, u32[]{:S(2)}) collective-permute-start(bf16[4,128,768]{2,1,0:T(8,128)(2,1)S(1)} %bitcast_multiply_fusion), channel_id=1, source_target_pairs={{0,17},{1,16},{8,25},{9,24},{16,1},{17,0},{24,9},{25,8},{2,19},{3,... | collective-permute-start | bytes 2359304 | tf_op jit(solution)/shard_map/ppermute | solution.py:11
  24.9 21.6 %collective-permute-start.3 = (bf16[4,128,768]{2,1,0:T(8,128)(2,1)S(1)}, bf16[4,128,768]{2,1,0:T(8,128)(2,1)}, u32[]{:S(2)}, u32[]{:S(2)}) collective-permute-start(bf16[4,128,768]{2,1,0:T(8,128)(2,1)S(1)} %bitcast_multiply_fusion), channel_id=1, source_target_pairs={{0,1},{1,0},{2,3},{3,2},{4,5},{5,4},{6,7},{7,6},{8,9},{9,8},{10,11... | collective-permute-start | bytes 2359304 | tf_op jit(solution)/shard_map/ppermute | solution.py:11
  39.6 20.3 %collective-permute-start.2 = (bf16[4,128,768]{2,1,0:T(8,128)(2,1)}, bf16[4,128,768]{2,1,0:T(8,128)(2,1)}, u32[]{:S(2)}, u32[]{:S(2)}) collective-permute-start(bf16[4,128,768]{2,1,0:T(8,128)(2,1)} %collective-permute-done.1), channel_id=1, source_target_pairs={{0,1},{1,0},{2,3},{3,2},{4,5},{5,4},{6,7},{7,6},{8,9},{9,8},{10,11... | collective-permute-start | bytes 2359304 | tf_op jit(solution)/shard_map/ppermute | solution.py:11
  46.5 13.3 %copy-start.3 = (bf16[4,128,768]{2,1,0:T(8,128)(2,1)S(1)}, bf16[4,128,768]{2,1,0:T(8,128)(2,1)}, u32[]{:S(2)}) copy-start(bf16[4,128,768]{2,1,0:T(8,128)(2,1)} %copy-done.2) | copy-start | bytes 2359300
  61.5 2.2 %copy-start = (bf16[1,8,128,768]{3,2,1,0:T(8,128)(2,1)}, bf16[1,8,128,768]{3,2,1,0:T(8,128)(2,1)S(1)}, u32[]{:S(2)}) copy-start(bf16[1,8,128,768]{3,2,1,0:T(8,128)(2,1)S(1)} %get-tuple-element.7) | copy-start | bytes 4718596
  61.5 2.7 %copy-start.1 = (bf16[1,8,128,768]{3,2,1,0:T(8,128)(2,1)}, bf16[1,8,128,768]{3,2,1,0:T(8,128)(2,1)S(1)}, u32[]{:S(2)}) copy-start(bf16[1,8,128,768]{3,2,1,0:T(8,128)(2,1)S(1)} %get-tuple-element.8) | copy-start | bytes 4718596
  64.2 7.9 %collective-permute-start.4 = (bf16[2,8,128,768]{3,2,1,0:T(8,128)(2,1)}, bf16[2,8,128,768]{3,2,1,0:T(8,128)(2,1)}, u32[]{:S(2)}, u32[]{:S(2)}) collective-permute-start(bf16[2,8,128,768]{3,2,1,0:T(8,128)(2,1)} %maximum_select_fusion), channel_id=1, source_target_pairs={{0,8},{8,0},{16,24},{24,16},{1,9},{9,1},{17,25},{25,17},{2,10},{10... | collective-permute-start | bytes 9437192 | tf_op jit(solution)/shard_map/ppermute | solution.py:11
  108.0 4.3 %copy-start.4 = (s32[1,8]{1,0:T(1,128)S(1)}, s32[1,8]{1,0:T(1,128)}, u32[]{:S(2)}) copy-start(s32[1,8]{1,0:T(1,128)} %param.11) | copy-start | bytes 100
  108.0 18.0 %all-to-all-start = ((f32[4,128,768]{2,1,0:T(8,128)}), f32[4,128,768]{2,1,0:T(8,128)S(1)}, u32[]{:S(2)}, u32[]{:S(2)}) async-start(f32[4,128,768]{2,1,0:T(8,128)} %bitcast.21), calls=%async_computation | async-start | bytes 3145728 | tf_op jit(solution)/shard_map/all_to_all | solution.py:65
Sparse Core Ops, SparseCore 0:
  21.1 79.5 all-gather.1
